TPU v7x, 768 devices: a whole 4x8x12 slice. The times are simulated.
768 devices in a mesh: dp: 192 (over y, z, core), tensor: 4 (over x).
Axes of the slice: x: 4, y: 8, z: 12, core: 2. Of those that a mesh axis runs over, the one named last changes fastest.
Arguments:
- inputs: bfloat16 [24576, 4096], P('dp'), may hold values from -6 to 6
- d_hidden: bfloat16 [24576, 14336], P('dp', 'tensor'), may hold values from -6 to 6
- tile_store: bfloat16 [4, 192, 4096], P('tensor', 'dp'), may hold values from -0.4375 to 0.4375
- tile_row: int32 [224, 3], P('tensor'), may hold values from 0 to 63, as said below
- tile_slot: int32 [224, 3], P('tensor'), may hold values from 0 to 191, as said below
Outputs:
- grad_inputs: bfloat16 [24576, 4096], P('dp', 'tensor')
- grad_tiles: float32 [4, 192, 4096], P('tensor', 'dp')
Inputs may be any that keep to these rules, and one draw needn't show every extreme that they name: `tile_row`: the 3 tile rows of one tile column are all different. `tile_slot`: tile column c uses the store of index c // (14336 // (64 * 4)) of tensor; the slots of one store are all different; slot s belongs to the owner s // 1 of dp; in every store some owner has all its 1 slots used.
All inputs are finite; a program needn't handle non-finite values.
Results may differ from a plain program's by a relative error of at most 0.012.
Values may be sent and summed in bfloat16 or wider, within the bound.
No kernel may reach another device: no remote copies, remote signals or barrier semaphores. Data moves between devices by JAX's collectives and lax.ppermute only.
A program may use at most 64 MiB of HBM per device.

v0:
```python
import jax
import jax.numpy as jnp
from jax import lax
from jax.sharding import PartitionSpec as P

TILE = 64


def silu_slope(value):
    sigma = jax.nn.sigmoid(value)
    return sigma * (1.0 + value * (1.0 - sigma))


def local(inputs, d_hidden, tile_store, tile_row, tile_slot):
    tok_rows = inputs.shape[0]
    model_width = inputs.shape[1]
    row_count = model_width // TILE
    per_slice = tile_row.shape[0]
    keep_count = tile_row.shape[1]
    gathered = lax.all_gather(tile_store, "dp", axis=1, tiled=True)[0]
    slot_count = gathered.shape[0]
    kept_tiles = gathered[tile_slot].reshape(per_slice, keep_count, TILE, TILE)
    input_blocks = inputs.reshape(tok_rows, row_count, TILE)
    picked = input_blocks[:, tile_row]
    pre_act = jnp.einsum("tcki,ckij->tcj", picked, kept_tiles, preferred_element_type=jnp.float32)
    upstream = d_hidden.reshape(tok_rows, per_slice, TILE).astype(jnp.float32)
    pre_grad = (upstream * silu_slope(pre_act)).astype(jnp.bfloat16)
    row_ids = jnp.arange(row_count, dtype=jnp.int32)
    back_all = jnp.einsum(
        "tcj,ckij->tcki", pre_grad, kept_tiles, preferred_element_type=jnp.float32
    )
    row_select = (tile_row[:, :, None] == row_ids[None, None, :]).astype(jnp.float32)
    partial_value = jnp.einsum(
        "tcki,ckr->tri", back_all, row_select, precision=lax.Precision.HIGHEST
    )
    grad_inputs = lax.psum_scatter(
        partial_value.reshape(tok_rows, model_width).astype(jnp.bfloat16),
        "tensor",
        scatter_dimension=1,
        tiled=True,
    )
    flat_slot = tile_slot.reshape(-1)
    grad_term = jnp.einsum("tcki,tcj->ckij", picked, pre_grad, preferred_element_type=jnp.float32)
    slot_store = jnp.zeros((slot_count, TILE * TILE), jnp.float32)
    slot_store = slot_store.at[flat_slot].set(
        grad_term.reshape(per_slice * keep_count, TILE * TILE)
    )
    owned_grads = lax.psum_scatter(slot_store, "dp", scatter_dimension=0, tiled=True)
    return (grad_inputs, owned_grads[None])


def solution(mesh):
    placed = (
        P("dp", None),
        P("dp", "tensor"),
        P("tensor", "dp", None),
        P("tensor", None),
        P("tensor", None),
    )
    return jax.shard_map(
        local,
        mesh=mesh,
        in_specs=placed,
        out_specs=(P("dp", "tensor"), P("tensor", "dp", None)),
        check_vma=False,
    )
```

profile of v0, /device:TPU:6, one launch (start us, length us, event | category | flops | bytes accessed | tf_op | source)
XLA Modules:
  0.0 526.1 jit_solution(12139165458920886908)
XLA Ops:
  7.2 0.0 copy-start.3
  7.2 0.0 all-gather.2.cloned.1.call-start
  7.2 0.7 all-gather.2.cloned.1.call-update
  7.9 0.0 all-reduce.3.cloned.1.call-start
  8.0 0.8 copy.36
  8.7 0.7 compare_select_fusion.2
  9.4 0.1 copy.29
  9.5 0.1 reshape.57
  9.6 1.6 copy.31
  11.3 0.7 compare_select_fusion.1
  11.9 0.1 copy.32
  12.0 0.1 reshape.65
  12.2 0.0 copy-done.3
  12.2 1.5 copy.30
  13.7 0.1 reshape.52
  13.9 2.6 gather_fusion.1
  16.5 125.5 %all-gather.2.cloned.1.call-done = bf16[1,192,4096]{2,0,1:T(2,128)(2,1)} async-done(((bf16[1,1,4096]{2,0,1:T(2,128)(2,1)}), bf16[1,192,4096]{2,0,1:T(2,128)(2,1)}) %all-gather.2.cloned.1.call-update) | async-done | bytes 1572880 | tf_op jit(solution)/shard_map/all_gather | solution.py:20
  142.0 3.6 copy.50
  145.6 2.5 gather_fusion
  148.1 0.0 copy-start
  148.1 5.2 reshape.50
  153.3 0.0 copy-done
  153.3 3.7 fusion.16
  157.0 0.0 copy-start.2
  157.0 1.0 copy-done.2
  158.0 3.3 fusion.20
  161.2 5.5 %reshape.75 = f32[168,4096]{1,0:T(8,128)} reshape(f32[56,3,64,64]{3,2,1,0:T(8,128)} %fusion.20) | data formatting | bytes 5505024 | tf_op jit(solution)/shard_map/reshape | solution.py:46
  166.7 0.0 copy-start.1
  166.7 5.3 %scatter_custom_fusion = f32[192,4096]{1,0:T(8,128)} fusion(s32[168]{0:T(256)S(1)} %bitcast.69, f32[168,4096]{1,0:T(8,128)} %reshape.75, f32[]{:T(128)} %constant.2.clone.1), kind=kCustom, calls=%fused_computation.17 | custom fusion | bytes 3146240 | tf_op jit(solution)/shard_map/scatter | solution.py:45
  172.0 0.0 all-reduce.3.cloned.1.call-update
  172.0 0.0 copy-start.4
  172.1 0.2 reduce-scatter.2.cloned.1.call-start
  172.3 0.0 copy-done.1
  172.3 2.0 convolution_bitcast_fusion
  174.3 0.0 copy-done.4
  174.3 5.7 %fusion.13 = bf16[128,64,64]{0,1,2:T(8,128)(2,1)S(1)} fusion(f32[128,56,3,64]{0,3,2,1:T(8,128)S(1)} %convolution_bitcast_fusion, s32[56,3]{0,1:T(4,128)S(1)} %copy-done.4), kind=kOutput, calls=%fused_computation.19 | convolution fusion | flops 1057499648 | bytes 6554272 | tf_op jit(solution)/shard_map/tcki,ckr->tri/dot_general | solution.py:33
  180.0 1.7 copy.35
  181.7 0.0 reduce-scatter.2.cloned.1.call-update
  181.7 1.3 dynamic-slice
  183.0 302.6 %all-reduce.3.cloned.1.call-done = f32[192,4096]{1,0:T(8,128)} async-done(((f32[192,4096]{1,0:T(8,128)}), f32[192,4096]{1,0:T(8,128)}) %all-reduce.3.cloned.1.call-update) | async-done | bytes 3145744
  485.6 2.2 dynamic-slice_bitcast_fusion
  487.7 30.1 %reduce-scatter.2.cloned.1.call-done = bf16[128,1024]{0,1:T(8,128)(2,1)} async-done(((bf16[128,4096]{0,1:T(8,128)(2,1)}), bf16[128,1024]{0,1:T(8,128)(2,1)}) %reduce-scatter.2.cloned.1.call-update) | async-done | bytes 262160 | tf_op jit(solution)/shard_map/reduce_scatter | solution.py:36
  517.8 1.8 copy.37
  (3 shorter events, 0.0 us)
Async XLA Ops:
  7.2 5.0 copy-start.3
  7.2 134.8 %all-gather.2.cloned.1.call-start = ((), (), s32[]{:S(2)}) async-start(), calls=%async_computation.1 | async-start | bytes 3162112 | tf_op jit(solution)/shard_map/all_gather | solution.py:20
  7.9 477.7 %all-reduce.3.cloned.1.call-start = ((), (), s32[]{:S(2)}) async-start(), calls=%async_computation.3 | async-start | bytes 6291456
  148.1 5.2 copy-start
  157.0 1.0 copy-start.2
  166.7 5.6 %copy-start.1 = (bf16[56,3,64,64]{3,2,1,0:T(8,128)(2,1)S(1)}, bf16[56,3,64,64]{3,2,1,0:T(8,128)(2,1)}, u32[]{:S(2)}) copy-start(bf16[56,3,64,64]{3,2,1,0:T(8,128)(2,1)} %reshape.50) | copy-start | bytes 4128772
  172.0 2.3 copy-start.4
  172.1 345.8 %reduce-scatter.2.cloned.1.call-start = ((), (), s32[]{:S(2)}) async-start(), calls=%async_computation.2 | async-start | bytes 1310720 | tf_op jit(solution)/shard_map/reduce_scatter | solution.py:36
Sparse Core Ops, SparseCore 0:
  11.7 130.1 all-gather.1
  172.2 313.3 all-reduce.2
  488.7 29.0 reduce-scatter.1
where the time goes:
time: 528 us; the launch traced here: 526 us
  waiting for transfers between devices  459 us (87%)
  local copies, waits for them, and re-layouts  37.1 us (7%)
  matrix products  14.7 us (3%)
  between operations  13.9 us (3%)
    unnamed x4, waiting for transfers between devices  303 us
    all_gather x1, waiting for transfers between devices, local(): gathered = lax.all_gather(tile_store, 'dp', axis=1, tiled=True)[0]  125 us
    reduce_scatter x1, waiting for transfers between devices, local(): lax.psum_scatter(partial_value.reshape(tok_rows, model_width).astype(jnp....  30.1 us
  transfers between devices with their start and end apart: 3, of which 3 were waited for; matrix products, arithmetic and copies ran while one was open for 4% of the time, Pallas kernels for 0%

commit v1 on v0

v1 whole, which is shorter than its diff:
```python
import jax
import jax.numpy as jnp
from jax import lax
from jax.sharding import Mesh
from jax.sharding import PartitionSpec as P

TILE = 64
DP_AXES = ("y", "z", "c")


def silu_slope(value):
    sigma = jax.nn.sigmoid(value)
    return sigma * (1.0 + value * (1.0 - sigma))


def pair_over_core(block, axis):
    core = lax.axis_index("c")
    other = lax.ppermute(block, "c", [(0, 1), (1, 0)])
    first = jnp.where(core == 0, block, other)
    second = jnp.where(core == 0, other, block)
    return jnp.concatenate([first, second], axis=axis)


def gather_by_a2a(block, name, count):
    copies = jnp.broadcast_to(block[None], (count,) + block.shape)
    got = lax.all_to_all(copies, name, 0, 0, tiled=True)
    return got.reshape((count * block.shape[0],) + block.shape[1:])


def reduce_by_a2a(value, name, count):
    parts = value.reshape((count, value.shape[0] // count) + value.shape[1:])
    got = lax.all_to_all(parts, name, 0, 0, tiled=True)
    return got.sum(axis=0)


def make_local(ny, nz, nc, nx):
    def local(inputs, d_hidden, tile_store, tile_row, tile_slot):
        tok_rows = inputs.shape[0]
        model_width = inputs.shape[1]
        row_count = model_width // TILE
        per_slice = tile_row.shape[0]
        keep_count = tile_row.shape[1]
        flat = tile_store.shape[-1]
        own = tile_store.reshape(1, flat)
        chip = pair_over_core(own, 0)
        row_z = gather_by_a2a(chip, "z", nz)
        gathered = gather_by_a2a(row_z, "y", ny)
        slot_count = gathered.shape[0]
        kept_tiles = gathered[tile_slot].reshape(per_slice, keep_count, TILE, TILE)
        input_blocks = inputs.reshape(tok_rows, row_count, TILE)
        picked = input_blocks[:, tile_row]
        pre_act = jnp.einsum("tcki,ckij->tcj", picked, kept_tiles, preferred_element_type=jnp.float32)
        upstream = d_hidden.reshape(tok_rows, per_slice, TILE).astype(jnp.float32)
        pre_grad = (upstream * silu_slope(pre_act)).astype(jnp.bfloat16)
        row_ids = jnp.arange(row_count, dtype=jnp.int32)
        back_all = jnp.einsum(
            "tcj,ckij->tcki", pre_grad, kept_tiles, preferred_element_type=jnp.float32
        )
        row_select = (tile_row[:, :, None] == row_ids[None, None, :]).astype(jnp.float32)
        partial_value = jnp.einsum(
            "tcki,ckr->tri", back_all, row_select, precision=lax.Precision.HIGHEST
        )
        partial_value = partial_value.reshape(tok_rows, model_width).astype(jnp.bfloat16)
        width = model_width // nx
        chunks = partial_value.reshape(tok_rows, nx, width)
        me = lax.axis_index("x")
        acc = lax.dynamic_index_in_dim(chunks, me, axis=1, keepdims=False).astype(jnp.float32)
        for shift in range(1, nx):
            send = lax.dynamic_index_in_dim(chunks, (me + shift) % nx, axis=1, keepdims=False)
            got = lax.ppermute(send, "x", [(j, (j + shift) % nx) for j in range(nx)])
            acc = acc + got.astype(jnp.float32)
        grad_inputs = acc.astype(jnp.bfloat16)
        flat_slot = tile_slot.reshape(-1)
        grad_term = jnp.einsum("tcki,tcj->ckij", picked, pre_grad, preferred_element_type=jnp.float32)
        slot_store = jnp.zeros((slot_count, TILE * TILE), jnp.float32)
        slot_store = slot_store.at[flat_slot].set(
            grad_term.reshape(per_slice * keep_count, TILE * TILE)
        )
        grid = slot_store.reshape(ny, nz, nc, flat)
        core = lax.axis_index("c")
        mine = lax.dynamic_index_in_dim(grid, core, axis=2, keepdims=False)
        theirs = lax.dynamic_index_in_dim(grid, 1 - core, axis=2, keepdims=False)
        chip_sum = mine + lax.ppermute(theirs, "c", [(0, 1), (1, 0)])
        by_z = jnp.swapaxes(chip_sum, 0, 1).reshape(nz * ny, flat)
        row_sum = reduce_by_a2a(by_z, "z", nz)
        owned = reduce_by_a2a(row_sum, "y", ny)
        return (grad_inputs, owned.reshape(1, 1, flat))

    return local


def split_dp(mesh):
    devices = mesh.devices
    column = list(devices[:, 0])
    cores = len({d.core_on_chip for d in column})
    zs = len({d.coords[2] for d in column})
    ys = len(column) // (cores * zs)
    assert ys * zs * cores == len(column) and cores == 2
    return ys, zs, cores


def solution(mesh):
    ny, nz, nc = split_dp(mesh)
    nx = mesh.devices.shape[1]
    grid = Mesh(mesh.devices.reshape(ny, nz, nc, nx), DP_AXES + ("x",))
    placed = (
        P(DP_AXES, None),
        P(DP_AXES, "x"),
        P("x", DP_AXES, None),
        P("x", None),
        P("x", None),
    )
    return jax.shard_map(
        make_local(ny, nz, nc, nx),
        mesh=grid,
        in_specs=placed,
        out_specs=(P(DP_AXES, "x"), P("x", DP_AXES, None)),
        check_vma=False,
    )
```

time: 528 us -> 205 us (0.39)
  waiting for transfers between devices: 459 us -> 85.8 us
  blocking collectives: 0 us -> 29.2 us
  starting transfers between devices: 0.3 us -> 29 us
  between operations: 13.9 us -> 0.93 us
    unnamed x4 -> x0, waiting for transfers between devices: 303 us -> none
    all_gather x1 -> x0, waiting for transfers between devices: 125 us -> none  [local(): gathered = lax.all_gather(tile_store, 'dp', axis=1, tiled=True)[0]]
    all_to_all x0 -> x3, waiting for transfers between devices: none -> 81.1 us  [the longest x2 49.2 us: reduce_by_a2a(): got = lax.all_to_all(parts, name, 0, 0, tiled=True)]
    reduce_scatter x1 -> x0, waiting for transfers between devices: 30.1 us -> none  [local(): lax.psum_scatter(partial_value.reshape(tok_rows, model_width).astype(jnp....]
    all_to_all x0 -> x1, blocking collectives: none -> 29.2 us  [gather_by_a2a(): got = lax.all_to_all(copies, name, 0, 0, tiled=True)]
    all_to_all x0 -> x3, starting transfers between devices: none -> 15.4 us  [the longest x2 8.27 us: reduce_by_a2a(): got = lax.all_to_all(parts, name, 0, 0, tiled=True)]
    ppermute x0 -> x5, starting transfers between devices: none -> 13.6 us  [the longest x3 9.76 us: local(): got = lax.ppermute(send, 'x', [(j, (j + shift) % nx) for j in range(nx)])]
    dynamic_slice x0 -> x2, local copies, waits for them, and re-layouts: none -> 7.26 us  [the longest x1 6.16 us: local(): mine = lax.dynamic_index_in_dim(grid, core, axis=2, keepdims=False)]
  transfers between devices with their start and end apart: 3 -> 8, of which waited for: 3 -> 5; matrix products, arithmetic and copies ran while one was open for 4% -> 9% of each run, Pallas kernels for 0% -> 0%
where the time goes in v1:
time: 205 us; the launch traced here: 204 us
  waiting for transfers between devices  85.8 us (42%)
  local copies, waits for them, and re-layouts  39.2 us (19%)
  blocking collectives  29.2 us (14%)
  starting transfers between devices  29 us (14%)
  matrix products  14.7 us (7%)
  other arithmetic  5.57 us (3%)
    all_to_all x2, waiting for transfers between devices, reduce_by_a2a(): got = lax.all_to_all(parts, name, 0, 0, tiled=True)  49.2 us
    all_to_all x1, waiting for transfers between devices, gather_by_a2a(): got = lax.all_to_all(copies, name, 0, 0, tiled=True)  31.9 us
    all_to_all x1, blocking collectives, gather_by_a2a(): got = lax.all_to_all(copies, name, 0, 0, tiled=True)  29.2 us
    ppermute x3, starting transfers between devices, local(): got = lax.ppermute(send, 'x', [(j, (j + shift) % nx) for j in range(nx)])  9.76 us
    all_to_all x2, starting transfers between devices, reduce_by_a2a(): got = lax.all_to_all(parts, name, 0, 0, tiled=True)  8.27 us
    all_to_all x1, starting transfers between devices, gather_by_a2a(): got = lax.all_to_all(copies, name, 0, 0, tiled=True)  7.1 us
    dynamic_slice x1, local copies, waits for them, and re-layouts, local(): mine = lax.dynamic_index_in_dim(grid, core, axis=2, keepdims=False)  6.16 us
    dot_general x1, matrix products, local(): jnp.einsum('tcki,ckr->tri', back_all, row_select, precision=lax.Precision...  5.67 us
  transfers between devices with their start and end apart: 8, of which 5 were waited for; matrix products, arithmetic and copies ran while one was open for 9% of the time, Pallas kernels for 0%

profile of v1, /device:TPU:6, one launch (start us, length us, event | category | flops | bytes accessed | tf_op | source)
XLA Modules:
  0.0 204.4 jit_solution(15628619240315039379)
XLA Ops:
  0.6 1.9 collective-permute-start
  2.6 1.4 collective-permute-done
  3.9 0.8 broadcast_select_fusion.1
  4.7 0.1 broadcast_in_dim.12
  4.9 29.2 %all_to_all.20 = bf16[12,2,4096]{2,1,0:T(2,128)(2,1)S(1)} all-to-all(bf16[12,2,4096]{2,1,0:T(2,128)(2,1)S(1)} %broadcast_in_dim.12), channel_id=1, replica_groups=mesh['y'=8,'z'=12,'c'=2,'x'=4] {'z'}, dimensions={0} | all-to-all | bytes 393216 | tf_op jit(solution)/shard_map/all_to_all | solution.py:26
  34.1 0.0 copy-start.5
  34.1 0.0 copy-start.4
  34.1 0.0 copy-start.3
  34.1 0.1 broadcast_in_dim.26
  34.2 1.3 broadcast_in_dim.27
  35.5 7.1 %all-to-all-start.1 = ((bf16[8,24,4096]{2,1,0:T(8,128)(2,1)}), bf16[8,24,4096]{2,1,0:T(8,128)(2,1)S(1)}, u32[]{:S(2)}, u32[]{:S(2)}) async-start(bf16[8,24,4096]{2,1,0:T(8,128)(2,1)} %broadcast_in_dim.27), calls=%async_computation.1 | async-start | bytes 3145728 | tf_op jit(solution)/shard_map/all_to_all | solution.py:26
  42.6 0.0 copy-done.5
  42.6 0.1 copy.36
  42.7 0.0 copy-done.4
  42.7 0.1 copy.29
  42.8 0.1 reshape.86
  43.0 0.0 copy-done.3
  43.0 1.6 copy.30
  44.5 1.6 copy.31
  46.1 0.1 copy.32
  46.2 0.1 reshape.94
  46.4 0.1 reshape.77
  46.5 2.6 %gather_fusion.1 = bf16[168,128,64]{1,2,0:T(8,128)(2,1)} fusion(bf16[128,64,64]{0,2,1:T(8,128)(2,1)S(1)} %bitcast.79, s32[1024]{0:T(1024)S(1)} %pad_clamp_fusion), kind=kCustom, calls=%fused_computation.1 | custom fusion | bytes 5505696 | tf_op jit(solution)/shard_map/gather | solution.py:51
  49.1 31.9 %all-to-all-done.1 = bf16[8,24,4096]{2,1,0:T(8,128)(2,1)S(1)} async-done(((bf16[8,24,4096]{2,1,0:T(8,128)(2,1)}), bf16[8,24,4096]{2,1,0:T(8,128)(2,1)S(1)}, u32[]{:S(2)}, u32[]{:S(2)}) %all-to-all-start.1) | async-done | bytes 1572896 | tf_op jit(solution)/shard_map/all_to_all | solution.py:26
  81.0 2.6 %gather_fusion = bf16[168,4096]{1,0:T(8,128)(2,1)} fusion(bf16[192,4096]{1,0:T(8,128)(2,1)S(1)} %bitcast.78, s32[1024]{0:T(1024)S(1)} %pad_clamp_fusion.1), kind=kCustom, calls=%fused_computation | custom fusion | bytes 2753184 | tf_op jit(solution)/shard_map/gather | solution.py:49
  83.6 0.0 copy-start
  83.6 5.2 %reshape.75 = bf16[56,3,64,64]{3,2,1,0:T(8,128)(2,1)} reshape(bf16[168,4096]{1,0:T(8,128)(2,1)} %gather_fusion) | data formatting | bytes 2752512 | tf_op jit(solution)/shard_map/reshape | solution.py:49
  88.8 0.0 copy-done
  88.8 3.7 %fusion.17 = bf16[128,56,64,1]{0,2,3,1:T(8,128)(2,1)S(1)} fusion(f32[128,56,64]{0,2,1:T(8,128)} %bitcast.84, bf16[56,3,64,64]{3,2,1,0:T(8,128)(2,1)} %reshape.75, bf16[128,56,3,64]{0,3,2,1:T(8,128)(2,1)S(1)} %bitcast.80), kind=kOutput, calls=%fused_computation.22 | convolution fusion | flops 180289536 | bytes 6881280 | tf_op jit(solution)/shard_map/tcki,ckij->tcj/dot_general | solution.py:52
  92.6 0.0 copy-start.2
  92.6 0.9 copy-done.2
  93.5 3.3 %fusion.24 = f32[56,3,64,64]{3,2,1,0:T(8,128)} fusion(bf16[128,56,3,64]{0,3,2,1:T(8,128)(2,1)S(1)} %bitcast.81, bf16[128,56,64,1]{0,2,3,1:T(8,128)(2,1)S(1)} %fusion.17), kind=kOutput, calls=%fused_computation.43 | convolution fusion | flops 176160768 | bytes 6422528 | tf_op jit(solution)/shard_map/tcki,tcj->ckij/dot_general | solution.py:74
  96.7 5.5 %reshape.104 = f32[168,4096]{1,0:T(8,128)} reshape(f32[56,3,64,64]{3,2,1,0:T(8,128)} %fusion.24) | data formatting | bytes 5505024 | tf_op jit(solution)/shard_map/reshape | solution.py:77
  102.2 4.3 %scatter_custom_fusion = f32[192,4096]{1,0:T(8,128)S(1)} fusion(s32[168]{0:T(256)S(1)} %bitcast.88, f32[168,4096]{1,0:T(8,128)} %reshape.104, f32[]{:T(128)} %constant.64.clone.1), kind=kCustom, calls=%fused_computation.19 | custom fusion | bytes 3146240 | tf_op jit(solution)/shard_map/scatter | solution.py:76
  106.5 3.2 %reshape.79 = f32[8,12,2,4096]{3,2,1,0:T(2,128)} reshape(f32[192,4096]{1,0:T(8,128)S(1)} %scatter_custom_fusion) | data formatting | bytes 6291456 | tf_op jit(solution)/shard_map/reshape | solution.py:79
  109.7 6.2 %constant_dynamic-slice_fusion.1 = (f32[8,12,1,4096]{3,2,1,0:T(1,128)S(1)}, f32[8,12,1,4096]{3,2,1,0:T(1,128)S(1)}) fusion(f32[8,12,2,4096]{3,2,1,0:T(2,128)} %reshape.79, s32[]{:T(128)S(6)} %select_n.76, s32[]{:T(128)S(6)} %select_n.77), kind=kLoop, calls=%fused_computation.42 | loop fusion | bytes 6291464 | tf_op jit(solution)/shard_map/jit(dynamic_index_in_dim)/dynamic_slice | solution.py:81
  115.9 1.1 copy.52
  117.0 1.9 collective-permute-start.4
  118.9 3.4 %collective-permute-done.4 = f32[8,12,4096]{2,0,1:T(8,128)S(1)} collective-permute-done((f32[8,12,4096]{2,0,1:T(8,128)S(1)}, f32[8,12,4096]{2,0,1:T(8,128)S(1)}, u32[]{:S(2)}, u32[]{:S(2)}) %collective-permute-start.4) | collective-permute-done | bytes 1572896 | tf_op jit(solution)/shard_map/ppermute | solution.py:83
  122.3 2.4 %fusion.11 = f32[12,8,4096]{2,1,0:T(8,128)} fusion(f32[8,12,4096]{2,0,1:T(8,128)S(1)} %collective-permute-done.4, f32[8,12,1,4096]{3,2,1,0:T(1,128)S(1)} %get-tuple-element.8), kind=kLoop, calls=%fused_computation.17 | loop fusion | flops 393216 | bytes 4718592 | tf_op jit(solution)/shard_map/transpose | solution.py:84
  124.7 0.0 copy-start.1
  124.7 4.9 %all-to-all-start.2 = ((f32[12,8,4096]{2,1,0:T(8,128)}), f32[12,8,4096]{2,1,0:T(8,128)}, u32[]{:S(2)}, u32[]{:S(2)}) async-start(f32[12,8,4096]{2,1,0:T(8,128)} %fusion.11), calls=%async_computation.2 | async-start | bytes 3145728 | tf_op jit(solution)/shard_map/all_to_all | solution.py:32
  129.6 0.0 copy-done.1
  129.7 2.0 convolution_bitcast_fusion
  131.7 5.7 %fusion.14 = bf16[128,64,64]{0,1,2:T(8,128)(2,1)S(1)} fusion(f32[128,56,3,64]{0,3,2,1:T(8,128)S(1)} %convolution_bitcast_fusion, s32[56,3]{0,1:T(4,128)S(1)} %copy-done.4), kind=kOutput, calls=%fused_computation.21 | convolution fusion | flops 1057499648 | bytes 6554272 | tf_op jit(solution)/shard_map/tcki,ckr->tri/dot_general | solution.py:60
  137.4 0.7 copy.35
  138.1 0.1 dynamic-slice_bitcast_fusion.2
  138.1 2.7 %collective-permute-start.3 = (bf16[128,1024]{0,1:T(8,128)(2,1)S(1)}, bf16[128,1024]{0,1:T(8,128)(2,1)S(1)}, u32[]{:S(2)}, u32[]{:S(2)}) collective-permute-start(bf16[128,1024]{0,1:T(8,128)(2,1)S(1)} %get-tuple-element.11), channel_id=1, source_target_pairs={{0,3},{1,0},{2,1},{3,2},{4,7},{5,4},{6,5},{7,6},{8,11},{9,8},{10,9... | collective-permute-start | bytes 786440 | tf_op jit(solution)/shard_map/ppermute | solution.py:70
  140.9 3.0 %collective-permute-start.2 = (bf16[128,1024]{0,1:T(8,128)(2,1)S(1)}, bf16[128,1024]{0,1:T(8,128)(2,1)S(1)}, u32[]{:S(2)}, u32[]{:S(2)}) collective-permute-start(bf16[128,1024]{0,1:T(8,128)(2,1)S(1)} %get-tuple-element.12), channel_id=1, source_target_pairs={{0,2},{1,3},{2,0},{3,1},{4,6},{5,7},{6,4},{7,5},{8,10},{9,11},{10,... | collective-permute-start | bytes 786440 | tf_op jit(solution)/shard_map/ppermute | solution.py:70
  143.9 4.0 %collective-permute-start.1 = (bf16[128,1024]{0,1:T(8,128)(2,1)S(1)}, bf16[128,1024]{0,1:T(8,128)(2,1)S(1)}, u32[]{:S(2)}, u32[]{:S(2)}) collective-permute-start(bf16[128,1024]{0,1:T(8,128)(2,1)S(1)} %get-tuple-element.10), channel_id=1, source_target_pairs={{0,1},{1,2},{2,3},{3,0},{4,5},{5,6},{6,7},{7,4},{8,9},{9,10},{10,1... | collective-permute-start | bytes 786440 | tf_op jit(solution)/shard_map/ppermute | solution.py:70
  147.9 41.2 %all-to-all-done.2 = f32[12,8,4096]{2,1,0:T(8,128)} async-done(((f32[12,8,4096]{2,1,0:T(8,128)}), f32[12,8,4096]{2,1,0:T(8,128)}, u32[]{:S(2)}, u32[]{:S(2)}) %all-to-all-start.2) | async-done | bytes 1572896 | tf_op jit(solution)/shard_map/all_to_all | solution.py:32
  189.1 1.5 reduce_sum.18
  190.6 0.7 reshape.80
  191.4 3.4 %all-to-all-start.3 = ((f32[8,1,4096]{2,1,0:T(1,128)}), f32[8,1,4096]{2,1,0:T(1,128)S(1)}, u32[]{:S(2)}, u32[]{:S(2)}) async-start(f32[8,1,4096]{2,1,0:T(1,128)} %reshape.80), calls=%async_computation.3 | async-start | bytes 262144 | tf_op jit(solution)/shard_map/all_to_all | solution.py:32
  194.7 0.0 collective-permute-done.3
  194.8 0.0 collective-permute-done.2
  194.8 0.0 collective-permute-done.1
  194.8 0.1 fusion.20
  194.9 0.9 copy.39
  195.8 8.0 %all-to-all-done.3 = f32[8,1,4096]{2,1,0:T(1,128)S(1)} async-done(((f32[8,1,4096]{2,1,0:T(1,128)}), f32[8,1,4096]{2,1,0:T(1,128)S(1)}, u32[]{:S(2)}, u32[]{:S(2)}) %all-to-all-start.3) | async-done | bytes 131104 | tf_op jit(solution)/shard_map/all_to_all | solution.py:32
  203.7 0.7 reduce_sum.19
  (5 shorter events, 0.1 us)
Async XLA Ops:
  0.6 3.3 %collective-permute-start = (bf16[1,4096]{1,0:T(2,128)(2,1)}, bf16[1,4096]{1,0:T(2,128)(2,1)S(1)}, u32[]{:S(2)}, u32[]{:S(2)}) collective-permute-start(bf16[1,4096]{1,0:T(2,128)(2,1)} %bitcast.87), channel_id=1, source_target_pairs={{0,4},{4,0},{1,5},{5,1},{2,6},{6,2},{3,7},{7,3},{8,12},{12,8},{9,1... | collective-permute-start | bytes 24584 | tf_op jit(solution)/shard_map/ppermute | solution.py:18
  34.1 8.5 %copy-start.5 = (s32[56,3]{0,1:T(4,128)S(1)}, s32[56,3]{0,1:T(4,128)}, u32[]{:S(2)}) copy-start(s32[56,3]{0,1:T(4,128)} %param.9) | copy-start | bytes 2020
  34.1 8.6 %copy-start.4 = (s32[56,3]{0,1:T(4,128)S(1)}, s32[56,3]{0,1:T(4,128)}, u32[]{:S(2)}) copy-start(s32[56,3]{0,1:T(4,128)} %param.8) | copy-start | bytes 2020
  34.1 8.9 %copy-start.3 = (bf16[128,3584]{1,0:T(8,128)(2,1)S(1)}, bf16[128,3584]{1,0:T(8,128)(2,1)}, u32[]{:S(2)}) copy-start(bf16[128,3584]{1,0:T(8,128)(2,1)} %param.6) | copy-start | bytes 2752516
  35.5 45.5 %all-to-all-start.1 = ((bf16[8,24,4096]{2,1,0:T(8,128)(2,1)}), bf16[8,24,4096]{2,1,0:T(8,128)(2,1)S(1)}, u32[]{:S(2)}, u32[]{:S(2)}) async-start(bf16[8,24,4096]{2,1,0:T(8,128)(2,1)} %broadcast_in_dim.27), calls=%async_computation.1 | async-start | bytes 3145728 | tf_op jit(solution)/shard_map/all_to_all | solution.py:26
  83.6 5.2 %copy-start = (bf16[168,128,64]{1,2,0:T(8,128)(2,1)S(1)}, bf16[168,128,64]{1,2,0:T(8,128)(2,1)}, u32[]{:S(2)}) copy-start(bf16[168,128,64]{1,2,0:T(8,128)(2,1)} %gather_fusion.1) | copy-start | bytes 8257540
  92.6 0.9 copy-start.2
  117.0 5.3 %collective-permute-start.4 = (f32[8,12,4096]{2,0,1:T(8,128)S(1)}, f32[8,12,4096]{2,0,1:T(8,128)S(1)}, u32[]{:S(2)}, u32[]{:S(2)}) collective-permute-start(f32[8,12,4096]{2,0,1:T(8,128)S(1)} %bitcast.85), channel_id=1, source_target_pairs={{0,4},{4,0},{1,5},{5,1},{2,6},{6,2},{3,7},{7,3},{8,12},{12,8},{9,1... | collective-permute-start | bytes 4718600 | tf_op jit(solution)/shard_map/ppermute | solution.py:83
  124.7 5.0 %copy-start.1 = (bf16[56,3,64,64]{3,2,1,0:T(8,128)(2,1)S(1)}, bf16[56,3,64,64]{3,2,1,0:T(8,128)(2,1)}, u32[]{:S(2)}) copy-start(bf16[56,3,64,64]{3,2,1,0:T(8,128)(2,1)} %reshape.75) | copy-start | bytes 4128772
  124.7 64.4 %all-to-all-start.2 = ((f32[12,8,4096]{2,1,0:T(8,128)}), f32[12,8,4096]{2,1,0:T(8,128)}, u32[]{:S(2)}, u32[]{:S(2)}) async-start(f32[12,8,4096]{2,1,0:T(8,128)} %fusion.11), calls=%async_computation.2 | async-start | bytes 3145728 | tf_op jit(solution)/shard_map/all_to_all | solution.py:32
  138.1 56.6 %collective-permute-start.3 = (bf16[128,1024]{0,1:T(8,128)(2,1)S(1)}, bf16[128,1024]{0,1:T(8,128)(2,1)S(1)}, u32[]{:S(2)}, u32[]{:S(2)}) collective-permute-start(bf16[128,1024]{0,1:T(8,128)(2,1)S(1)} %get-tuple-element.11), channel_id=1, source_target_pairs={{0,3},{1,0},{2,1},{3,2},{4,7},{5,4},{6,5},{7,6},{8,11},{9,8},{10,9... | collective-permute-start | bytes 786440 | tf_op jit(solution)/shard_map/ppermute | solution.py:70
  140.9 53.9 %collective-permute-start.2 = (bf16[128,1024]{0,1:T(8,128)(2,1)S(1)}, bf16[128,1024]{0,1:T(8,128)(2,1)S(1)}, u32[]{:S(2)}, u32[]{:S(2)}) collective-permute-start(bf16[128,1024]{0,1:T(8,128)(2,1)S(1)} %get-tuple-element.12), channel_id=1, source_target_pairs={{0,2},{1,3},{2,0},{3,1},{4,6},{5,7},{6,4},{7,5},{8,10},{9,11},{10,... | collective-permute-start | bytes 786440 | tf_op jit(solution)/shard_map/ppermute | solution.py:70
  143.9 50.9 %collective-permute-start.1 = (bf16[128,1024]{0,1:T(8,128)(2,1)S(1)}, bf16[128,1024]{0,1:T(8,128)(2,1)S(1)}, u32[]{:S(2)}, u32[]{:S(2)}) collective-permute-start(bf16[128,1024]{0,1:T(8,128)(2,1)S(1)} %get-tuple-element.10), channel_id=1, source_target_pairs={{0,1},{1,2},{2,3},{3,0},{4,5},{5,6},{6,7},{7,4},{8,9},{9,10},{10,1... | collective-permute-start | bytes 786440 | tf_op jit(solution)/shard_map/ppermute | solution.py:70
  191.4 12.4 %all-to-all-start.3 = ((f32[8,1,4096]{2,1,0:T(1,128)}), f32[8,1,4096]{2,1,0:T(1,128)S(1)}, u32[]{:S(2)}, u32[]{:S(2)}) async-start(f32[8,1,4096]{2,1,0:T(1,128)} %reshape.80), calls=%async_computation.3 | async-start | bytes 262144 | tf_op jit(solution)/shard_map/all_to_all | solution.py:32

commit v2 on v1

--- a/solution.py
+++ b/solution.py
@@ -40,13 +40,22 @@
         row_count = model_width // TILE
         per_slice = tile_row.shape[0]
         keep_count = tile_row.shape[1]
+        cap = tile_store.shape[1]
         flat = tile_store.shape[-1]
-        own = tile_store.reshape(1, flat)
-        chip = pair_over_core(own, 0)
-        row_z = gather_by_a2a(chip, "z", nz)
-        gathered = gather_by_a2a(row_z, "y", ny)
-        slot_count = gathered.shape[0]
-        kept_tiles = gathered[tile_slot].reshape(per_slice, keep_count, TILE, TILE)
+        half = ny * nz * cap
+        core = lax.axis_index("c")
+        owner = tile_slot // cap
+        slot_k = tile_slot % cap
+        rel_core = (owner % nc + nc - core) % nc
+        owner_y = owner // (nz * nc)
+        owner_z = (owner // nc) % nz
+        rel_slot = ((rel_core * ny + owner_y) * nz + owner_z) * cap + slot_k
+        own = tile_store.reshape(cap, flat)
+        row_z = gather_by_a2a(own, "z", nz)
+        mine_tiles = gather_by_a2a(row_z, "y", ny)
+        other_tiles = lax.ppermute(mine_tiles, "c", [(0, 1), (1, 0)])
+        gathered = jnp.concatenate([mine_tiles, other_tiles], axis=0)
+        kept_tiles = gathered[rel_slot].reshape(per_slice, keep_count, TILE, TILE)
         input_blocks = inputs.reshape(tok_rows, row_count, TILE)
         picked = input_blocks[:, tile_row]
         pre_act = jnp.einsum("tcki,ckij->tcj", picked, kept_tiles, preferred_element_type=jnp.float32)
@@ -70,21 +79,16 @@
             got = lax.ppermute(send, "x", [(j, (j + shift) % nx) for j in range(nx)])
             acc = acc + got.astype(jnp.float32)
         grad_inputs = acc.astype(jnp.bfloat16)
-        flat_slot = tile_slot.reshape(-1)
         grad_term = jnp.einsum("tcki,tcj->ckij", picked, pre_grad, preferred_element_type=jnp.float32)
-        slot_store = jnp.zeros((slot_count, TILE * TILE), jnp.float32)
-        slot_store = slot_store.at[flat_slot].set(
-            grad_term.reshape(per_slice * keep_count, TILE * TILE)
+        slot_store = jnp.zeros((nc * half, flat), jnp.float32)
+        slot_store = slot_store.at[rel_slot.reshape(-1)].set(
+            grad_term.reshape(per_slice * keep_count, flat)
         )
-        grid = slot_store.reshape(ny, nz, nc, flat)
-        core = lax.axis_index("c")
-        mine = lax.dynamic_index_in_dim(grid, core, axis=2, keepdims=False)
-        theirs = lax.dynamic_index_in_dim(grid, 1 - core, axis=2, keepdims=False)
-        chip_sum = mine + lax.ppermute(theirs, "c", [(0, 1), (1, 0)])
-        by_z = jnp.swapaxes(chip_sum, 0, 1).reshape(nz * ny, flat)
-        row_sum = reduce_by_a2a(by_z, "z", nz)
-        owned = reduce_by_a2a(row_sum, "y", ny)
-        return (grad_inputs, owned.reshape(1, 1, flat))
+        chip_sum = slot_store[:half] + lax.ppermute(slot_store[half:], "c", [(0, 1), (1, 0)])
+        by_y = chip_sum.reshape(ny, nz * cap * flat)
+        col_sum = reduce_by_a2a(by_y, "y", ny).reshape(nz, cap * flat)
+        owned = reduce_by_a2a(col_sum, "z", nz)
+        return (grad_inputs, owned.reshape(1, cap, flat))
 
     return local
 

time: 205 us -> 186 us (0.907)
  the two profiles are of different devices: /device:TPU:6 before, /device:TPU:9 now
where the time goes in v2:
time: 186 us; the launch traced here: 185 us
  waiting for transfers between devices  66.8 us (36%)
  starting transfers between devices  37.1 us (20%)
  local copies, waits for them, and re-layouts  32.6 us (18%)
  blocking collectives  24.7 us (13%)
  matrix products  14.7 us (8%)
  other arithmetic  8.73 us (5%)
    all_to_all x2, waiting for transfers between devices, reduce_by_a2a(): got = lax.all_to_all(parts, name, 0, 0, tiled=True)  30.5 us
    all_to_all x1, blocking collectives, gather_by_a2a(): got = lax.all_to_all(copies, name, 0, 0, tiled=True)  24.7 us
    all_to_all x1, waiting for transfers between devices, gather_by_a2a(): got = lax.all_to_all(copies, name, 0, 0, tiled=True)  20.7 us
    ppermute x3, waiting for transfers between devices, local(): got = lax.ppermute(send, 'x', [(j, (j + shift) % nx) for j in range(nx)])  12.2 us
    ppermute x1, starting transfers between devices, local(): other_tiles = lax.ppermute(mine_tiles, 'c', [(0, 1), (1, 0)])  9.74 us
    ppermute x3, starting transfers between devices, local(): got = lax.ppermute(send, 'x', [(j, (j + shift) % nx) for j in range(nx)])  9.33 us
    all_to_all x2, starting transfers between devices, reduce_by_a2a(): got = lax.all_to_all(parts, name, 0, 0, tiled=True)  9.1 us
    all_to_all x1, starting transfers between devices, gather_by_a2a(): got = lax.all_to_all(copies, name, 0, 0, tiled=True)  6.99 us
  transfers between devices with their start and end apart: 8, of which 6 were waited for; matrix products, arithmetic and copies ran while one was open for 9% of the time, Pallas kernels for 0%

profile of v2, /device:TPU:9, one launch (start us, length us, event | category | flops | bytes accessed | tf_op | source)
XLA Modules:
  0.0 185.4 jit_solution(2523507262140521792)
XLA Ops:
  0.6 0.8 reduce.2
  1.4 0.1 broadcast_in_dim.27
  1.5 0.5 broadcast.79
  2.1 1.2 reduce.3
  3.3 0.1 reshape.111
  3.3 24.7 %all_to_all.20 = bf16[12,2,2048]{2,1,0:T(2,128)(2,1)S(1)} all-to-all(bf16[12,2,2048]{2,1,0:T(2,128)(2,1)S(1)} %reshape.111), channel_id=1, replica_groups=mesh['y'=8,'z'=12,'c'=2,'x'=4] {'z'}, dimensions={0} | all-to-all | bytes 196608 | tf_op jit(solution)/shard_map/all_to_all | solution.py:26
  28.0 0.1 reshape.112
  28.1 0.0 copy-start.5
  28.1 0.1 copy.57
  28.3 1.1 broadcast_in_dim.29
  29.3 7.0 %all-to-all-start.1 = ((bf16[8,12,4096]{2,1,0:T(8,128)(2,1)}), bf16[8,12,4096]{2,1,0:T(8,128)(2,1)S(1)}, u32[]{:S(2)}, u32[]{:S(2)}) async-start(bf16[8,12,4096]{2,1,0:T(8,128)(2,1)} %broadcast_in_dim.29), calls=%async_computation.1 | async-start | bytes 2097152 | tf_op jit(solution)/shard_map/all_to_all | solution.py:26
  36.3 0.0 copy-start.3
  36.3 20.7 %all-to-all-done.1 = bf16[8,12,4096]{2,1,0:T(8,128)(2,1)S(1)} async-done(((bf16[8,12,4096]{2,1,0:T(8,128)(2,1)}), bf16[8,12,4096]{2,1,0:T(8,128)(2,1)S(1)}, u32[]{:S(2)}, u32[]{:S(2)}) %all-to-all-start.1) | async-done | bytes 786464 | tf_op jit(solution)/shard_map/all_to_all | solution.py:26
  57.0 0.2 reshape.67
  57.2 0.0 copy-start.4
  57.2 9.7 %collective-permute-start = (bf16[96,4096]{1,0:T(8,128)(2,1)S(1)}, bf16[96,4096]{1,0:T(8,128)(2,1)}, u32[]{:S(2)}, u32[]{:S(2)}) collective-permute-start(bf16[96,4096]{1,0:T(8,128)(2,1)S(1)} %reshape.67), channel_id=1, source_target_pairs={{0,4},{4,0},{1,5},{5,1},{2,6},{6,2},{3,7},{7,3},{8,12},{12,8},{9,1... | collective-permute-start | bytes 2359304 | tf_op jit(solution)/shard_map/ppermute | solution.py:56
  66.9 0.0 copy-done.5
  67.0 0.1 copy.36
  67.1 0.1 reshape.77
  67.2 2.5 %copy.37 = f32[128,3584]{0,1:T(8,128)} copy(bf16[128,3584]{1,0:T(8,128)(2,1)} %param.6) | data formatting | bytes 2752512 | tf_op jit(solution)/shard_map/convert_element_type | solution.py:62
  69.7 0.0 copy-done.3
  69.7 0.7 copy.38
  70.3 0.0 copy-done.4
  70.3 0.1 copy.39
  70.4 0.1 reshape.85
  70.6 0.1 copy.43
  70.7 0.1 reshape.70
  70.8 2.6 %gather_fusion.1 = bf16[168,128,64]{1,2,0:T(8,128)(2,1)} fusion(bf16[128,64,64]{0,2,1:T(8,128)(2,1)S(1)} %bitcast.69, s32[1024]{0:T(1024)S(1)} %pad_clamp_fusion), kind=kCustom, calls=%fused_computation.1 | custom fusion | bytes 5505696 | tf_op jit(solution)/shard_map/gather | solution.py:60
  73.4 0.0 collective-permute-done
  73.4 1.2 pad_maximum_fusion
  74.7 2.6 %gather_fusion = bf16[168,4096]{1,0:T(8,128)(2,1)} fusion(bf16[192,4096]{1,0:T(8,128)(2,1)S(1)} %pad_maximum_fusion, s32[1024]{0:T(1024)S(1)} %pad_clamp_fusion.1), kind=kCustom, calls=%fused_computation | custom fusion | bytes 2753184 | tf_op jit(solution)/shard_map/gather | solution.py:58
  77.3 0.0 copy-start
  77.3 5.2 %reshape.68 = bf16[56,3,64,64]{3,2,1,0:T(8,128)(2,1)} reshape(bf16[168,4096]{1,0:T(8,128)(2,1)} %gather_fusion) | data formatting | bytes 2752512 | tf_op jit(solution)/shard_map/reshape | solution.py:58
  82.4 0.0 copy-done
  82.4 3.7 %fusion.16 = bf16[128,56,64,1]{0,2,3,1:T(8,128)(2,1)S(1)} fusion(f32[128,56,64]{0,2,1:T(8,128)} %bitcast.74, bf16[56,3,64,64]{3,2,1,0:T(8,128)(2,1)} %reshape.68, bf16[128,56,3,64]{0,3,2,1:T(8,128)(2,1)S(1)} %bitcast.70), kind=kOutput, calls=%fused_computation.21 | convolution fusion | flops 180289536 | bytes 6881280 | tf_op jit(solution)/shard_map/tcki,ckij->tcj/dot_general | solution.py:61
  86.1 0.0 copy-start.2
  86.2 0.9 copy-done.2
  87.1 3.3 %fusion.33 = f32[56,3,64,64]{3,2,1,0:T(8,128)} fusion(bf16[128,56,3,64]{0,3,2,1:T(8,128)(2,1)S(1)} %bitcast.71, bf16[128,56,64,1]{0,2,3,1:T(8,128)(2,1)S(1)} %fusion.16), kind=kOutput, calls=%fused_computation.59 | convolution fusion | flops 176160768 | bytes 6422528 | tf_op jit(solution)/shard_map/tcki,tcj->ckij/dot_general | solution.py:82
  90.3 5.5 %reshape.95 = f32[168,4096]{1,0:T(8,128)} reshape(f32[56,3,64,64]{3,2,1,0:T(8,128)} %fusion.33) | data formatting | bytes 5505024 | tf_op jit(solution)/shard_map/reshape | solution.py:85
  95.8 4.1 %scatter_custom_fusion = f32[192,4096]{1,0:T(8,128)S(1)} fusion(s32[168]{0:T(256)S(1)} %bitcast.77, f32[168,4096]{1,0:T(8,128)} %reshape.95, f32[]{:T(128)} %constant.117.clone.1), kind=kCustom, calls=%fused_computation.18 | custom fusion | bytes 3146240 | tf_op jit(solution)/shard_map/scatter | solution.py:84
  99.9 0.1 slice.13
  100.0 1.9 %collective-permute-start.4 = (f32[96,4096]{1,0:T(8,128)S(1)}, f32[96,4096]{1,0:T(8,128)S(1)}, u32[]{:S(2)}, u32[]{:S(2)}) collective-permute-start(f32[96,4096]{1,0:T(8,128)S(1)} %slice.13), channel_id=1, source_target_pairs={{0,4},{4,0},{1,5},{5,1},{2,6},{6,2},{3,7},{7,3},{8,12},{12,8},{9,1... | collective-permute-start | bytes 4718600 | tf_op jit(solution)/shard_map/ppermute | solution.py:87
  102.0 3.4 %collective-permute-done.4 = f32[96,4096]{1,0:T(8,128)S(1)} collective-permute-done((f32[96,4096]{1,0:T(8,128)S(1)}, f32[96,4096]{1,0:T(8,128)S(1)}, u32[]{:S(2)}, u32[]{:S(2)}) %collective-permute-start.4) | collective-permute-done | bytes 1572896 | tf_op jit(solution)/shard_map/ppermute | solution.py:87
  105.4 1.4 slice_add_fusion
  106.7 4.0 %reshape_reshape.6 = f32[8,1,49152]{2,1,0:T(1,128)} reshape(f32[96,4096]{1,0:T(8,128)} %slice_add_fusion) | data formatting | bytes 3145728 | tf_op jit(solution)/shard_map/reshape;reshape | solution.py:31
  110.8 5.6 %all-to-all-start.2 = ((f32[8,1,49152]{2,1,0:T(1,128)}), f32[8,1,49152]{2,1,0:T(1,128)}, u32[]{:S(2)}, u32[]{:S(2)}) async-start(f32[8,1,49152]{2,1,0:T(1,128)} %reshape_reshape.6), calls=%async_computation.2 | async-start | bytes 3145728 | tf_op jit(solution)/shard_map/all_to_all | solution.py:32
  116.3 0.0 copy-done.1
  116.3 2.0 %convolution_bitcast_fusion = f32[128,56,3,64]{0,3,2,1:T(8,128)S(1)} fusion(bf16[56,3,64,64]{3,2,1,0:T(8,128)(2,1)S(1)} %copy-done.1, bf16[128,56,64,1]{0,2,3,1:T(8,128)(2,1)} %copy-done.2), kind=kOutput, calls=%fused_computation.5 | convolution fusion | flops 176160768 | bytes 7798784 | tf_op jit(solution)/shard_map/tcj,ckij->tcki/dot_general | solution.py:65
  118.4 5.7 %fusion.13 = bf16[128,64,64]{0,1,2:T(8,128)(2,1)S(1)} fusion(f32[128,56,3,64]{0,3,2,1:T(8,128)S(1)} %convolution_bitcast_fusion, s32[56,3]{0,1:T(4,128)S(1)} %copy-done.4), kind=kOutput, calls=%fused_computation.20 | convolution fusion | flops 1057499648 | bytes 6554272 | tf_op jit(solution)/shard_map/tcki,ckr->tri/dot_general | solution.py:69
  124.0 0.7 copy.42
  124.7 30.5 %all-to-all-done.2 = f32[8,1,49152]{2,1,0:T(1,128)} async-done(((f32[8,1,49152]{2,1,0:T(1,128)}), f32[8,1,49152]{2,1,0:T(1,128)}, u32[]{:S(2)}, u32[]{:S(2)}) %all-to-all-start.2) | async-done | bytes 1572896 | tf_op jit(solution)/shard_map/all_to_all | solution.py:32
  155.2 3.2 %reduce_sum.18 = f32[49152]{0:T(1024)} reduce(f32[8,1,49152]{2,1,0:T(1,128)} %all-to-all-done.2, f32[]{:T(128)} %constant.117.clone.1), dimensions={0,1}, to_apply=%region_1.2 | reduce | flops 344064 | bytes 1769476 | tf_op jit(solution)/shard_map/reduce_sum | solution.py:33
  158.5 3.5 %all-to-all-start.3 = ((f32[12,1,4096]{2,1,0:T(1,128)}), f32[12,1,4096]{2,1,0:T(1,128)S(1)}, u32[]{:S(2)}, u32[]{:S(2)}) async-start(f32[12,1,4096]{2,1,0:T(1,128)} %bitcast.23), calls=%async_computation.3 | async-start | bytes 393216 | tf_op jit(solution)/shard_map/all_to_all | solution.py:32
  162.0 0.1 dynamic-slice_bitcast_fusion.2
  162.1 4.4 %collective-permute-start.3 = (bf16[128,1024]{0,1:T(8,128)(2,1)S(1)}, bf16[128,1024]{0,1:T(8,128)(2,1)S(1)}, u32[]{:S(2)}, u32[]{:S(2)}) collective-permute-start(bf16[128,1024]{0,1:T(8,128)(2,1)S(1)} %get-tuple-element.13), channel_id=1, source_target_pairs={{0,3},{1,0},{2,1},{3,2},{4,7},{5,4},{6,5},{7,6},{8,11},{9,8},{10,9... | collective-permute-start | bytes 786440 | tf_op jit(solution)/shard_map/ppermute | solution.py:79
  166.5 2.4 %collective-permute-start.2 = (bf16[128,1024]{0,1:T(8,128)(2,1)S(1)}, bf16[128,1024]{0,1:T(8,128)(2,1)S(1)}, u32[]{:S(2)}, u32[]{:S(2)}) collective-permute-start(bf16[128,1024]{0,1:T(8,128)(2,1)S(1)} %get-tuple-element.14), channel_id=1, source_target_pairs={{0,2},{1,3},{2,0},{3,1},{4,6},{5,7},{6,4},{7,5},{8,10},{9,11},{10,... | collective-permute-start | bytes 786440 | tf_op jit(solution)/shard_map/ppermute | solution.py:79
  168.9 2.5 %collective-permute-start.1 = (bf16[128,1024]{0,1:T(8,128)(2,1)S(1)}, bf16[128,1024]{0,1:T(8,128)(2,1)S(1)}, u32[]{:S(2)}, u32[]{:S(2)}) collective-permute-start(bf16[128,1024]{0,1:T(8,128)(2,1)S(1)} %get-tuple-element.12), channel_id=1, source_target_pairs={{0,1},{1,2},{2,3},{3,0},{4,5},{5,6},{6,7},{7,4},{8,9},{9,10},{10,1... | collective-permute-start | bytes 786440 | tf_op jit(solution)/shard_map/ppermute | solution.py:79
  171.4 0.5 collective-permute-done.3
  171.9 4.6 %collective-permute-done.2 = bf16[128,1024]{0,1:T(8,128)(2,1)S(1)} collective-permute-done((bf16[128,1024]{0,1:T(8,128)(2,1)S(1)}, bf16[128,1024]{0,1:T(8,128)(2,1)S(1)}, u32[]{:S(2)}, u32[]{:S(2)}) %collective-permute-start.2) | collective-permute-done | bytes 262176 | tf_op jit(solution)/shard_map/ppermute | solution.py:79
  176.5 7.2 %collective-permute-done.1 = bf16[128,1024]{0,1:T(8,128)(2,1)S(1)} collective-permute-done((bf16[128,1024]{0,1:T(8,128)(2,1)S(1)}, bf16[128,1024]{0,1:T(8,128)(2,1)S(1)}, u32[]{:S(2)}, u32[]{:S(2)}) %collective-permute-start.1) | collective-permute-done | bytes 262176 | tf_op jit(solution)/shard_map/ppermute | solution.py:79
  183.6 0.1 fusion.19
  183.8 0.9 copy.44
  184.6 0.0 all-to-all-done.3
  184.6 0.7 reduce_sum.19
  (6 shorter events, 0.0 us)
Async XLA Ops:
  28.1 38.8 %copy-start.5 = (s32[56,3]{0,1:T(4,128)S(1)}, s32[56,3]{0,1:T(4,128)}, u32[]{:S(2)}) copy-start(s32[56,3]{0,1:T(4,128)} %param.9) | copy-start | bytes 2020
  29.3 27.7 %all-to-all-start.1 = ((bf16[8,12,4096]{2,1,0:T(8,128)(2,1)}), bf16[8,12,4096]{2,1,0:T(8,128)(2,1)S(1)}, u32[]{:S(2)}, u32[]{:S(2)}) async-start(bf16[8,12,4096]{2,1,0:T(8,128)(2,1)} %broadcast_in_dim.29), calls=%async_computation.1 | async-start | bytes 2097152 | tf_op jit(solution)/shard_map/all_to_all | solution.py:26
  36.3 33.3 %copy-start.3 = (bf16[128,4096]{1,0:T(8,128)(2,1)S(1)}, bf16[128,4096]{1,0:T(8,128)(2,1)}, u32[]{:S(2)}) copy-start(bf16[128,4096]{1,0:T(8,128)(2,1)} %param.5) | copy-start | bytes 3145732
  57.2 13.1 %copy-start.4 = (s32[56,3]{0,1:T(4,128)S(1)}, s32[56,3]{0,1:T(4,128)}, u32[]{:S(2)}) copy-start(s32[56,3]{0,1:T(4,128)} %param.8) | copy-start | bytes 2020
  57.2 16.2 %collective-permute-start = (bf16[96,4096]{1,0:T(8,128)(2,1)S(1)}, bf16[96,4096]{1,0:T(8,128)(2,1)}, u32[]{:S(2)}, u32[]{:S(2)}) collective-permute-start(bf16[96,4096]{1,0:T(8,128)(2,1)S(1)} %reshape.67), channel_id=1, source_target_pairs={{0,4},{4,0},{1,5},{5,1},{2,6},{6,2},{3,7},{7,3},{8,12},{12,8},{9,1... | collective-permute-start | bytes 2359304 | tf_op jit(solution)/shard_map/ppermute | solution.py:56
  77.3 5.2 %copy-start = (bf16[168,128,64]{1,2,0:T(8,128)(2,1)S(1)}, bf16[168,128,64]{1,2,0:T(8,128)(2,1)}, u32[]{:S(2)}) copy-start(bf16[168,128,64]{1,2,0:T(8,128)(2,1)} %gather_fusion.1) | copy-start | bytes 8257540
  86.1 0.9 copy-start.2
  100.0 5.3 %collective-permute-start.4 = (f32[96,4096]{1,0:T(8,128)S(1)}, f32[96,4096]{1,0:T(8,128)S(1)}, u32[]{:S(2)}, u32[]{:S(2)}) collective-permute-start(f32[96,4096]{1,0:T(8,128)S(1)} %slice.13), channel_id=1, source_target_pairs={{0,4},{4,0},{1,5},{5,1},{2,6},{6,2},{3,7},{7,3},{8,12},{12,8},{9,1... | collective-permute-start | bytes 4718600 | tf_op jit(solution)/shard_map/ppermute | solution.py:87
  106.7 9.6 %copy-start.1 = (bf16[56,3,64,64]{3,2,1,0:T(8,128)(2,1)S(1)}, bf16[56,3,64,64]{3,2,1,0:T(8,128)(2,1)}, u32[]{:S(2)}) copy-start(bf16[56,3,64,64]{3,2,1,0:T(8,128)(2,1)} %reshape.68) | copy-start | bytes 4128772
  110.8 44.5 %all-to-all-start.2 = ((f32[8,1,49152]{2,1,0:T(1,128)}), f32[8,1,49152]{2,1,0:T(1,128)}, u32[]{:S(2)}, u32[]{:S(2)}) async-start(f32[8,1,49152]{2,1,0:T(1,128)} %reshape_reshape.6), calls=%async_computation.2 | async-start | bytes 3145728 | tf_op jit(solution)/shard_map/all_to_all | solution.py:32
  158.5 26.2 %all-to-all-start.3 = ((f32[12,1,4096]{2,1,0:T(1,128)}), f32[12,1,4096]{2,1,0:T(1,128)S(1)}, u32[]{:S(2)}, u32[]{:S(2)}) async-start(f32[12,1,4096]{2,1,0:T(1,128)} %bitcast.23), calls=%async_computation.3 | async-start | bytes 393216 | tf_op jit(solution)/shard_map/all_to_all | solution.py:32
  162.1 9.8 %collective-permute-start.3 = (bf16[128,1024]{0,1:T(8,128)(2,1)S(1)}, bf16[128,1024]{0,1:T(8,128)(2,1)S(1)}, u32[]{:S(2)}, u32[]{:S(2)}) collective-permute-start(bf16[128,1024]{0,1:T(8,128)(2,1)S(1)} %get-tuple-element.13), channel_id=1, source_target_pairs={{0,3},{1,0},{2,1},{3,2},{4,7},{5,4},{6,5},{7,6},{8,11},{9,8},{10,9... | collective-permute-start | bytes 786440 | tf_op jit(solution)/shard_map/ppermute | solution.py:79
  166.5 10.0 %collective-permute-start.2 = (bf16[128,1024]{0,1:T(8,128)(2,1)S(1)}, bf16[128,1024]{0,1:T(8,128)(2,1)S(1)}, u32[]{:S(2)}, u32[]{:S(2)}) collective-permute-start(bf16[128,1024]{0,1:T(8,128)(2,1)S(1)} %get-tuple-element.14), channel_id=1, source_target_pairs={{0,2},{1,3},{2,0},{3,1},{4,6},{5,7},{6,4},{7,5},{8,10},{9,11},{10,... | collective-permute-start | bytes 786440 | tf_op jit(solution)/shard_map/ppermute | solution.py:79
  168.9 14.8 %collective-permute-start.1 = (bf16[128,1024]{0,1:T(8,128)(2,1)S(1)}, bf16[128,1024]{0,1:T(8,128)(2,1)S(1)}, u32[]{:S(2)}, u32[]{:S(2)}) collective-permute-start(bf16[128,1024]{0,1:T(8,128)(2,1)S(1)} %get-tuple-element.12), channel_id=1, source_target_pairs={{0,1},{1,2},{2,3},{3,0},{4,5},{5,6},{6,7},{7,4},{8,9},{9,10},{10,1... | collective-permute-start | bytes 786440 | tf_op jit(solution)/shard_map/ppermute | solution.py:79

commit v3 on v2

--- a/solution.py
+++ b/solution.py
@@ -80,13 +80,15 @@
             acc = acc + got.astype(jnp.float32)
         grad_inputs = acc.astype(jnp.bfloat16)
         grad_term = jnp.einsum("tcki,tcj->ckij", picked, pre_grad, preferred_element_type=jnp.float32)
-        slot_store = jnp.zeros((nc * half, flat), jnp.float32)
+        lanes = 128
+        rows = flat // lanes
+        slot_store = jnp.zeros((nc * half, rows, lanes), jnp.float32)
         slot_store = slot_store.at[rel_slot.reshape(-1)].set(
-            grad_term.reshape(per_slice * keep_count, flat)
+            grad_term.reshape(per_slice * keep_count, rows, lanes)
         )
         chip_sum = slot_store[:half] + lax.ppermute(slot_store[half:], "c", [(0, 1), (1, 0)])
-        by_y = chip_sum.reshape(ny, nz * cap * flat)
-        col_sum = reduce_by_a2a(by_y, "y", ny).reshape(nz, cap * flat)
+        by_y = chip_sum.reshape(ny, nz * cap * rows, lanes)
+        col_sum = reduce_by_a2a(by_y, "y", ny).reshape(nz, cap * rows, lanes)
         owned = reduce_by_a2a(col_sum, "z", nz)
         return (grad_inputs, owned.reshape(1, cap, flat))
 

time: 186 us -> 191 us (1.027)
  the two profiles are of different devices: /device:TPU:9 before, /device:TPU:6 now
where the time goes in v3:
time: 191 us; the launch traced here: 189 us
  waiting for transfers between devices  69.4 us (36%)
  local copies, waits for them, and re-layouts  40.5 us (21%)
  starting transfers between devices  28.8 us (15%)
  blocking collectives  26.9 us (14%)
  matrix products  14.7 us (8%)
  other arithmetic  7.68 us (4%)
    all_to_all x2, waiting for transfers between devices, reduce_by_a2a(): got = lax.all_to_all(parts, name, 0, 0, tiled=True)  29.9 us
    all_to_all x1, blocking collectives, gather_by_a2a(): got = lax.all_to_all(copies, name, 0, 0, tiled=True)  26.9 us
    all_to_all x1, waiting for transfers between devices, gather_by_a2a(): got = lax.all_to_all(copies, name, 0, 0, tiled=True)  26.6 us
    scatter x1, local copies, waits for them, and re-layouts, local(): slot_store.at[rel_slot.reshape(-1)]  16.1 us
    ppermute x3, waiting for transfers between devices, local(): got = lax.ppermute(send, 'x', [(j, (j + shift) % nx) for j in range(nx)])  9.92 us
    ppermute x3, starting transfers between devices, local(): got = lax.ppermute(send, 'x', [(j, (j + shift) % nx) for j in range(nx)])  9.16 us
    all_to_all x2, starting transfers between devices, reduce_by_a2a(): got = lax.all_to_all(parts, name, 0, 0, tiled=True)  8.26 us
    all_to_all x1, starting transfers between devices, gather_by_a2a(): got = lax.all_to_all(copies, name, 0, 0, tiled=True)  7.1 us
  transfers between devices with their start and end apart: 8, of which 5 were waited for; matrix products, arithmetic and copies ran while one was open for 8% of the time, Pallas kernels for 0%

profile of v3, /device:TPU:6, one launch (start us, length us, event | category | flops | bytes accessed | tf_op | source)
XLA Modules:
  0.0 189.0 jit_solution(2539217966495354275)
XLA Ops:
  0.6 0.8 reduce.2
  1.4 0.1 broadcast_in_dim.27
  1.5 0.5 broadcast.79
  2.1 1.2 reduce.3
  3.3 0.1 reshape.109
  3.3 26.9 %all_to_all.20 = bf16[12,2,2048]{2,1,0:T(2,128)(2,1)S(1)} all-to-all(bf16[12,2,2048]{2,1,0:T(2,128)(2,1)S(1)} %reshape.109), channel_id=1, replica_groups=mesh['y'=8,'z'=12,'c'=2,'x'=4] {'z'}, dimensions={0} | all-to-all | bytes 196608 | tf_op jit(solution)/shard_map/all_to_all | solution.py:26
  30.3 0.1 reshape.110
  30.4 0.0 copy-start.5
  30.4 0.0 copy-start.4
  30.4 0.0 copy-start.3
  30.4 0.1 copy.48
  30.5 1.1 broadcast_in_dim.29
  31.6 7.1 %all-to-all-start.1 = ((bf16[8,12,4096]{2,1,0:T(8,128)(2,1)}), bf16[8,12,4096]{2,1,0:T(8,128)(2,1)S(1)}, u32[]{:S(2)}, u32[]{:S(2)}) async-start(bf16[8,12,4096]{2,1,0:T(8,128)(2,1)} %broadcast_in_dim.29), calls=%async_computation.1 | async-start | bytes 2097152 | tf_op jit(solution)/shard_map/all_to_all | solution.py:26
  38.7 26.6 %all-to-all-done.1 = bf16[8,12,4096]{2,1,0:T(8,128)(2,1)S(1)} async-done(((bf16[8,12,4096]{2,1,0:T(8,128)(2,1)}), bf16[8,12,4096]{2,1,0:T(8,128)(2,1)S(1)}, u32[]{:S(2)}, u32[]{:S(2)}) %all-to-all-start.1) | async-done | bytes 786464 | tf_op jit(solution)/shard_map/all_to_all | solution.py:26
  65.2 0.2 reshape.67
  65.4 1.9 %collective-permute-start = (bf16[96,4096]{1,0:T(8,128)(2,1)S(1)}, bf16[96,4096]{1,0:T(8,128)(2,1)}, u32[]{:S(2)}, u32[]{:S(2)}) collective-permute-start(bf16[96,4096]{1,0:T(8,128)(2,1)S(1)} %reshape.67), channel_id=1, source_target_pairs={{0,4},{4,0},{1,5},{5,1},{2,6},{6,2},{3,7},{7,3},{8,12},{12,8},{9,1... | collective-permute-start | bytes 2359304 | tf_op jit(solution)/shard_map/ppermute | solution.py:56
  67.3 0.0 copy-done.5
  67.4 0.1 copy.27
  67.5 0.1 reshape.77
  67.6 0.0 copy-done.4
  67.6 0.1 copy.30
  67.7 0.1 reshape.85
  67.9 0.1 copy.34
  68.0 0.1 reshape.70
  68.1 0.0 copy-done.3
  68.1 0.7 copy.29
  68.8 2.5 %copy.28 = f32[128,3584]{0,1:T(8,128)} copy(bf16[128,3584]{1,0:T(8,128)(2,1)} %param.6) | data formatting | bytes 2752512 | tf_op jit(solution)/shard_map/convert_element_type | solution.py:62
  71.2 2.6 %gather_fusion.1 = bf16[168,128,64]{1,2,0:T(8,128)(2,1)} fusion(bf16[128,64,64]{0,2,1:T(8,128)(2,1)S(1)} %bitcast.71, s32[1024]{0:T(1024)S(1)} %pad_clamp_fusion), kind=kCustom, calls=%fused_computation.1 | custom fusion | bytes 5505696 | tf_op jit(solution)/shard_map/gather | solution.py:60
  73.8 0.0 collective-permute-done
  73.8 1.2 pad_maximum_fusion
  75.1 2.6 %gather_fusion = bf16[168,4096]{1,0:T(8,128)(2,1)} fusion(bf16[192,4096]{1,0:T(8,128)(2,1)S(1)} %pad_maximum_fusion, s32[1024]{0:T(1024)S(1)} %pad_clamp_fusion.1), kind=kCustom, calls=%fused_computation | custom fusion | bytes 2753184 | tf_op jit(solution)/shard_map/gather | solution.py:58
  77.7 0.0 copy-start
  77.7 5.2 %reshape.68 = bf16[56,3,64,64]{3,2,1,0:T(8,128)(2,1)} reshape(bf16[168,4096]{1,0:T(8,128)(2,1)} %gather_fusion) | data formatting | bytes 2752512 | tf_op jit(solution)/shard_map/reshape | solution.py:58
  82.8 0.0 copy-done
  82.8 3.7 %fusion.14 = bf16[128,56,64,1]{0,2,3,1:T(8,128)(2,1)S(1)} fusion(f32[128,56,64]{0,2,1:T(8,128)} %bitcast.77, bf16[56,3,64,64]{3,2,1,0:T(8,128)(2,1)} %reshape.68, bf16[128,56,3,64]{0,3,2,1:T(8,128)(2,1)S(1)} %bitcast.72), kind=kOutput, calls=%fused_computation.19 | convolution fusion | flops 180289536 | bytes 6881280 | tf_op jit(solution)/shard_map/tcki,ckij->tcj/dot_general | solution.py:61
  86.6 0.0 copy-start.2
  86.6 0.9 copy-done.2
  87.5 3.3 %fusion.31 = f32[56,3,64,64]{3,2,1,0:T(8,128)} fusion(bf16[128,56,3,64]{0,3,2,1:T(8,128)(2,1)S(1)} %bitcast.73, bf16[128,56,64,1]{0,2,3,1:T(8,128)(2,1)S(1)} %fusion.14), kind=kOutput, calls=%fused_computation.57 | convolution fusion | flops 176160768 | bytes 6422528 | tf_op jit(solution)/shard_map/tcki,tcj->ckij/dot_general | solution.py:82
  90.7 5.0 %reshape.95 = f32[168,32,128]{2,1,0:T(8,128)} reshape(f32[56,3,64,64]{3,2,1,0:T(8,128)} %fusion.31) | data formatting | bytes 5505024 | tf_op jit(solution)/shard_map/reshape | solution.py:87
  95.8 0.4 broadcast_in_dim.32
  96.2 16.1 %scatter_fusion = f32[192,32,128]{2,1,0:T(8,128)S(1)} fusion(f32[192,32,128]{2,1,0:T(8,128)S(1)} %broadcast_in_dim.32, s32[168]{0:T(256)S(1)} %bitcast.80, f32[168,32,128]{2,1,0:T(8,128)} %reshape.95), kind=kCustom, calls=%fused_computation.2 | custom fusion | bytes 8258208 | tf_op jit(solution)/shard_map/scatter | solution.py:86
  112.3 0.1 slice.13
  112.4 2.4 %collective-permute-start.4 = (f32[96,32,128]{2,1,0:T(8,128)S(1)}, f32[96,32,128]{2,1,0:T(8,128)S(1)}, u32[]{:S(2)}, u32[]{:S(2)}) collective-permute-start(f32[96,32,128]{2,1,0:T(8,128)S(1)} %slice.13), channel_id=1, source_target_pairs={{0,4},{4,0},{1,5},{5,1},{2,6},{6,2},{3,7},{7,3},{8,12},{12,8},{9,1... | collective-permute-start | bytes 4718600 | tf_op jit(solution)/shard_map/ppermute | solution.py:89
  114.8 3.0 %collective-permute-done.4 = f32[96,32,128]{2,1,0:T(8,128)S(1)} collective-permute-done((f32[96,32,128]{2,1,0:T(8,128)S(1)}, f32[96,32,128]{2,1,0:T(8,128)S(1)}, u32[]{:S(2)}, u32[]{:S(2)}) %collective-permute-start.4) | collective-permute-done | bytes 1572896 | tf_op jit(solution)/shard_map/ppermute | solution.py:89
  117.9 1.5 slice_add_fusion
  119.3 4.7 %all-to-all-start.2 = ((f32[8,1,384,128]{3,2,1,0:T(8,128)}), f32[8,1,384,128]{3,2,1,0:T(8,128)}, u32[]{:S(2)}, u32[]{:S(2)}) async-start(f32[8,1,384,128]{3,2,1,0:T(8,128)} %bitcast.74), calls=%async_computation.2 | async-start | bytes 3145728 | tf_op jit(solution)/shard_map/all_to_all | solution.py:32
  124.1 0.0 copy-done.1
  124.1 2.0 %convolution_bitcast_fusion = f32[128,56,3,64]{0,3,2,1:T(8,128)S(1)} fusion(bf16[56,3,64,64]{3,2,1,0:T(8,128)(2,1)S(1)} %copy-done.1, bf16[128,56,64,1]{0,2,3,1:T(8,128)(2,1)} %copy-done.2), kind=kOutput, calls=%fused_computation.5 | convolution fusion | flops 176160768 | bytes 7798784 | tf_op jit(solution)/shard_map/tcj,ckij->tcki/dot_general | solution.py:65
  126.2 5.7 %fusion.11 = bf16[128,64,64]{0,1,2:T(8,128)(2,1)S(1)} fusion(f32[128,56,3,64]{0,3,2,1:T(8,128)S(1)} %convolution_bitcast_fusion, s32[56,3]{0,1:T(4,128)S(1)} %copy-done.4), kind=kOutput, calls=%fused_computation.18 | convolution fusion | flops 1057499648 | bytes 6554272 | tf_op jit(solution)/shard_map/tcki,ckr->tri/dot_general | solution.py:69
  131.8 0.7 copy.33
  132.5 29.9 %all-to-all-done.2 = f32[8,1,384,128]{3,2,1,0:T(8,128)} async-done(((f32[8,1,384,128]{3,2,1,0:T(8,128)}), f32[8,1,384,128]{3,2,1,0:T(8,128)}, u32[]{:S(2)}, u32[]{:S(2)}) %all-to-all-start.2) | async-done | bytes 1572896 | tf_op jit(solution)/shard_map/all_to_all | solution.py:32
  162.5 2.2 %reduce_sum.18 = f32[384,128]{1,0:T(8,128)} reduce(f32[8,1,384,128]{3,2,1,0:T(8,128)} %all-to-all-done.2, f32[]{:T(128)} %constant.117.clone.1), dimensions={0,1}, to_apply=%region_1.2 | reduce | flops 344064 | bytes 1769476 | tf_op jit(solution)/shard_map/reduce_sum | solution.py:33
  164.7 3.5 %all-to-all-start.3 = ((f32[12,1,32,128]{3,2,1,0:T(8,128)}), f32[12,1,32,128]{3,2,1,0:T(8,128)S(1)}, u32[]{:S(2)}, u32[]{:S(2)}) async-start(f32[12,1,32,128]{3,2,1,0:T(8,128)} %bitcast.24), calls=%async_computation.3 | async-start | bytes 393216 | tf_op jit(solution)/shard_map/all_to_all | solution.py:32
  168.2 0.1 dynamic-slice_bitcast_fusion.2
  168.3 2.4 %collective-permute-start.1 = (bf16[128,1024]{0,1:T(8,128)(2,1)S(1)}, bf16[128,1024]{0,1:T(8,128)(2,1)S(1)}, u32[]{:S(2)}, u32[]{:S(2)}) collective-permute-start(bf16[128,1024]{0,1:T(8,128)(2,1)S(1)} %get-tuple-element.10), channel_id=1, source_target_pairs={{0,1},{1,2},{2,3},{3,0},{4,5},{5,6},{6,7},{7,4},{8,9},{9,10},{10,1... | collective-permute-start | bytes 786440 | tf_op jit(solution)/shard_map/ppermute | solution.py:79
  170.7 3.5 %collective-permute-start.3 = (bf16[128,1024]{0,1:T(8,128)(2,1)S(1)}, bf16[128,1024]{0,1:T(8,128)(2,1)S(1)}, u32[]{:S(2)}, u32[]{:S(2)}) collective-permute-start(bf16[128,1024]{0,1:T(8,128)(2,1)S(1)} %get-tuple-element.11), channel_id=1, source_target_pairs={{0,3},{1,0},{2,1},{3,2},{4,7},{5,4},{6,5},{7,6},{8,11},{9,8},{10,9... | collective-permute-start | bytes 786440 | tf_op jit(solution)/shard_map/ppermute | solution.py:79
  174.1 3.3 %collective-permute-start.2 = (bf16[128,1024]{0,1:T(8,128)(2,1)S(1)}, bf16[128,1024]{0,1:T(8,128)(2,1)S(1)}, u32[]{:S(2)}, u32[]{:S(2)}) collective-permute-start(bf16[128,1024]{0,1:T(8,128)(2,1)S(1)} %get-tuple-element.12), channel_id=1, source_target_pairs={{0,2},{1,3},{2,0},{3,1},{4,6},{5,7},{6,4},{7,5},{8,10},{9,11},{10,... | collective-permute-start | bytes 786440 | tf_op jit(solution)/shard_map/ppermute | solution.py:79
  177.4 1.0 collective-permute-done.1
  178.4 8.9 %collective-permute-done.3 = bf16[128,1024]{0,1:T(8,128)(2,1)S(1)} collective-permute-done((bf16[128,1024]{0,1:T(8,128)(2,1)S(1)}, bf16[128,1024]{0,1:T(8,128)(2,1)S(1)}, u32[]{:S(2)}, u32[]{:S(2)}) %collective-permute-start.3) | collective-permute-done | bytes 262176 | tf_op jit(solution)/shard_map/ppermute | solution.py:79
  187.4 0.0 collective-permute-done.2
  187.4 0.1 fusion.17
  187.5 0.9 copy.35
  188.4 0.0 all-to-all-done.3
  188.4 0.6 reduce_sum.19
  (6 shorter events, 0.0 us)
Async XLA Ops:
  30.4 37.0 %copy-start.5 = (s32[56,3]{0,1:T(4,128)S(1)}, s32[56,3]{0,1:T(4,128)}, u32[]{:S(2)}) copy-start(s32[56,3]{0,1:T(4,128)} %param.9) | copy-start | bytes 2020
  30.4 37.2 %copy-start.4 = (s32[56,3]{0,1:T(4,128)S(1)}, s32[56,3]{0,1:T(4,128)}, u32[]{:S(2)}) copy-start(s32[56,3]{0,1:T(4,128)} %param.8) | copy-start | bytes 2020
  30.4 37.7 %copy-start.3 = (bf16[128,4096]{1,0:T(8,128)(2,1)S(1)}, bf16[128,4096]{1,0:T(8,128)(2,1)}, u32[]{:S(2)}) copy-start(bf16[128,4096]{1,0:T(8,128)(2,1)} %param.5) | copy-start | bytes 3145732
  31.6 33.7 %all-to-all-start.1 = ((bf16[8,12,4096]{2,1,0:T(8,128)(2,1)}), bf16[8,12,4096]{2,1,0:T(8,128)(2,1)S(1)}, u32[]{:S(2)}, u32[]{:S(2)}) async-start(bf16[8,12,4096]{2,1,0:T(8,128)(2,1)} %broadcast_in_dim.29), calls=%async_computation.1 | async-start | bytes 2097152 | tf_op jit(solution)/shard_map/all_to_all | solution.py:26
  65.4 8.4 %collective-permute-start = (bf16[96,4096]{1,0:T(8,128)(2,1)S(1)}, bf16[96,4096]{1,0:T(8,128)(2,1)}, u32[]{:S(2)}, u32[]{:S(2)}) collective-permute-start(bf16[96,4096]{1,0:T(8,128)(2,1)S(1)} %reshape.67), channel_id=1, source_target_pairs={{0,4},{4,0},{1,5},{5,1},{2,6},{6,2},{3,7},{7,3},{8,12},{12,8},{9,1... | collective-permute-start | bytes 2359304 | tf_op jit(solution)/shard_map/ppermute | solution.py:56
  77.7 5.2 %copy-start = (bf16[168,128,64]{1,2,0:T(8,128)(2,1)S(1)}, bf16[168,128,64]{1,2,0:T(8,128)(2,1)}, u32[]{:S(2)}) copy-start(bf16[168,128,64]{1,2,0:T(8,128)(2,1)} %gather_fusion.1) | copy-start | bytes 8257540
  86.6 0.9 copy-start.2
  112.4 5.4 %collective-permute-start.4 = (f32[96,32,128]{2,1,0:T(8,128)S(1)}, f32[96,32,128]{2,1,0:T(8,128)S(1)}, u32[]{:S(2)}, u32[]{:S(2)}) collective-permute-start(f32[96,32,128]{2,1,0:T(8,128)S(1)} %slice.13), channel_id=1, source_target_pairs={{0,4},{4,0},{1,5},{5,1},{2,6},{6,2},{3,7},{7,3},{8,12},{12,8},{9,1... | collective-permute-start | bytes 4718600 | tf_op jit(solution)/shard_map/ppermute | solution.py:89
  119.3 4.8 %copy-start.1 = (bf16[56,3,64,64]{3,2,1,0:T(8,128)(2,1)S(1)}, bf16[56,3,64,64]{3,2,1,0:T(8,128)(2,1)}, u32[]{:S(2)}) copy-start(bf16[56,3,64,64]{3,2,1,0:T(8,128)(2,1)} %reshape.68) | copy-start | bytes 4128772
  119.3 43.1 %all-to-all-start.2 = ((f32[8,1,384,128]{3,2,1,0:T(8,128)}), f32[8,1,384,128]{3,2,1,0:T(8,128)}, u32[]{:S(2)}, u32[]{:S(2)}) async-start(f32[8,1,384,128]{3,2,1,0:T(8,128)} %bitcast.74), calls=%async_computation.2 | async-start | bytes 3145728 | tf_op jit(solution)/shard_map/all_to_all | solution.py:32
  164.7 23.7 %all-to-all-start.3 = ((f32[12,1,32,128]{3,2,1,0:T(8,128)}), f32[12,1,32,128]{3,2,1,0:T(8,128)S(1)}, u32[]{:S(2)}, u32[]{:S(2)}) async-start(f32[12,1,32,128]{3,2,1,0:T(8,128)} %bitcast.24), calls=%async_computation.3 | async-start | bytes 393216 | tf_op jit(solution)/shard_map/all_to_all | solution.py:32
  168.3 10.2 %collective-permute-start.1 = (bf16[128,1024]{0,1:T(8,128)(2,1)S(1)}, bf16[128,1024]{0,1:T(8,128)(2,1)S(1)}, u32[]{:S(2)}, u32[]{:S(2)}) collective-permute-start(bf16[128,1024]{0,1:T(8,128)(2,1)S(1)} %get-tuple-element.10), channel_id=1, source_target_pairs={{0,1},{1,2},{2,3},{3,0},{4,5},{5,6},{6,7},{7,4},{8,9},{9,10},{10,1... | collective-permute-start | bytes 786440 | tf_op jit(solution)/shard_map/ppermute | solution.py:79
  170.7 16.7 %collective-permute-start.3 = (bf16[128,1024]{0,1:T(8,128)(2,1)S(1)}, bf16[128,1024]{0,1:T(8,128)(2,1)S(1)}, u32[]{:S(2)}, u32[]{:S(2)}) collective-permute-start(bf16[128,1024]{0,1:T(8,128)(2,1)S(1)} %get-tuple-element.11), channel_id=1, source_target_pairs={{0,3},{1,0},{2,1},{3,2},{4,7},{5,4},{6,5},{7,6},{8,11},{9,8},{10,9... | collective-permute-start | bytes 786440 | tf_op jit(solution)/shard_map/ppermute | solution.py:79
  174.1 13.2 %collective-permute-start.2 = (bf16[128,1024]{0,1:T(8,128)(2,1)S(1)}, bf16[128,1024]{0,1:T(8,128)(2,1)S(1)}, u32[]{:S(2)}, u32[]{:S(2)}) collective-permute-start(bf16[128,1024]{0,1:T(8,128)(2,1)S(1)} %get-tuple-element.12), channel_id=1, source_target_pairs={{0,2},{1,3},{2,0},{3,1},{4,6},{5,7},{6,4},{7,5},{8,10},{9,11},{10,... | collective-permute-start | bytes 786440 | tf_op jit(solution)/shard_map/ppermute | solution.py:79

commit v4 on v2

--- a/solution.py
+++ b/solution.py
@@ -79,14 +79,22 @@
             got = lax.ppermute(send, "x", [(j, (j + shift) % nx) for j in range(nx)])
             acc = acc + got.astype(jnp.float32)
         grad_inputs = acc.astype(jnp.bfloat16)
-        grad_term = jnp.einsum("tcki,tcj->ckij", picked, pre_grad, preferred_element_type=jnp.float32)
-        slot_store = jnp.zeros((nc * half, flat), jnp.float32)
-        slot_store = slot_store.at[rel_slot.reshape(-1)].set(
-            grad_term.reshape(per_slice * keep_count, flat)
-        )
-        chip_sum = slot_store[:half] + lax.ppermute(slot_store[half:], "c", [(0, 1), (1, 0)])
-        by_y = chip_sum.reshape(ny, nz * cap * flat)
-        col_sum = reduce_by_a2a(by_y, "y", ny).reshape(nz, cap * flat)
+        owned_parts = []
+        for part in range(2):
+            lo = part * (TILE // 2)
+            picked_rows = picked[..., lo:lo + TILE // 2]
+            grad_term = jnp.einsum(
+                "tcki,tcj->ckij", picked_rows, pre_grad, preferred_element_type=jnp.float32
+            )
+            part_flat = flat // 2
+            slot_store = jnp.zeros((nc * half, part_flat), jnp.float32)
+            slot_store = slot_store.at[rel_slot.reshape(-1)].set(
+                grad_term.reshape(per_slice * keep_count, part_flat)
+            )
+            chip_sum = slot_store[:half] + lax.ppermute(slot_store[half:], "c", [(0, 1), (1, 0)])
+            by_y = chip_sum.reshape(ny, nz * cap * part_flat)
+            owned_parts.append(reduce_by_a2a(by_y, "y", ny).reshape(nz, cap, part_flat))
+        col_sum = jnp.concatenate(owned_parts, axis=2).reshape(nz, cap * flat)
         owned = reduce_by_a2a(col_sum, "z", nz)
         return (grad_inputs, owned.reshape(1, cap, flat))
 

time: 186 us -> 186 us (level)
  the two profiles are of different devices: /device:TPU:9 before, /device:TPU:6 now
where the time goes in v4:
time: 186 us; the launch traced here: 184 us
  waiting for transfers between devices  59.1 us (32%)
  local copies, waits for them, and re-layouts  37.5 us (20%)
  starting transfers between devices  34.5 us (19%)
  blocking collectives  26.9 us (14%)
  matrix products  17 us (9%)
  other arithmetic  8.34 us (4%)
    all_to_all x1, blocking collectives, gather_by_a2a(): got = lax.all_to_all(copies, name, 0, 0, tiled=True)  26.9 us
    all_to_all x1, waiting for transfers between devices, gather_by_a2a(): got = lax.all_to_all(copies, name, 0, 0, tiled=True)  26.6 us
    all_to_all x3, waiting for transfers between devices, reduce_by_a2a(): got = lax.all_to_all(parts, name, 0, 0, tiled=True)  18.9 us
    all_to_all x3, starting transfers between devices, reduce_by_a2a(): got = lax.all_to_all(parts, name, 0, 0, tiled=True)  11.5 us
    ppermute x3, waiting for transfers between devices, local(): got = lax.ppermute(send, 'x', [(j, (j + shift) % nx) for j in range(nx)])  9.9 us
    ppermute x3, starting transfers between devices, local(): got = lax.ppermute(send, 'x', [(j, (j + shift) % nx) for j in range(nx)])  9.15 us
    all_to_all x1, starting transfers between devices, gather_by_a2a(): got = lax.all_to_all(copies, name, 0, 0, tiled=True)  7.23 us
    reshape x2, local copies, waits for them, and re-layouts, local(): grad_term.reshape(per_slice * keep_count, part_flat)  6.27 us
  transfers between devices with their start and end apart: 10, of which 7 were waited for; matrix products, arithmetic and copies ran while one was open for 16% of the time, Pallas kernels for 0%

profile of v4, /device:TPU:6, one launch (start us, length us, event | category | flops | bytes accessed | tf_op | source)
XLA Modules:
  0.0 184.3 jit_solution(5704237420687002527)
XLA Ops:
  0.6 0.8 reduce.3
  1.4 0.1 broadcast_in_dim.25
  1.5 0.5 broadcast.97
  2.1 1.2 reduce.4
  3.3 0.1 reshape.136
  3.3 26.9 %all_to_all.25 = bf16[12,2,2048]{2,1,0:T(2,128)(2,1)S(1)} all-to-all(bf16[12,2,2048]{2,1,0:T(2,128)(2,1)S(1)} %reshape.136), channel_id=1, replica_groups=mesh['y'=8,'z'=12,'c'=2,'x'=4] {'z'}, dimensions={0} | all-to-all | bytes 196608 | tf_op jit(solution)/shard_map/all_to_all | solution.py:26
  30.3 0.1 reshape.137
  30.4 0.1 copy.56
  30.5 1.1 broadcast_in_dim.27
  31.5 7.2 %all-to-all-start.1 = ((bf16[8,12,4096]{2,1,0:T(8,128)(2,1)}), bf16[8,12,4096]{2,1,0:T(8,128)(2,1)S(1)}, u32[]{:S(2)}, u32[]{:S(2)}) async-start(bf16[8,12,4096]{2,1,0:T(8,128)(2,1)} %broadcast_in_dim.27), calls=%async_computation.1 | async-start | bytes 2097152 | tf_op jit(solution)/shard_map/all_to_all | solution.py:26
  38.8 26.6 %all-to-all-done.1 = bf16[8,12,4096]{2,1,0:T(8,128)(2,1)S(1)} async-done(((bf16[8,12,4096]{2,1,0:T(8,128)(2,1)}), bf16[8,12,4096]{2,1,0:T(8,128)(2,1)S(1)}, u32[]{:S(2)}, u32[]{:S(2)}) %all-to-all-start.1) | async-done | bytes 786464 | tf_op jit(solution)/shard_map/all_to_all | solution.py:26
  65.3 0.2 reshape.79
  65.5 1.9 %collective-permute-start = (bf16[96,4096]{1,0:T(8,128)(2,1)S(1)}, bf16[96,4096]{1,0:T(8,128)(2,1)}, u32[]{:S(2)}, u32[]{:S(2)}) collective-permute-start(bf16[96,4096]{1,0:T(8,128)(2,1)S(1)} %reshape.79), channel_id=1, source_target_pairs={{0,4},{4,0},{1,5},{5,1},{2,6},{6,2},{3,7},{7,3},{8,12},{12,8},{9,1... | collective-permute-start | bytes 2359304 | tf_op jit(solution)/shard_map/ppermute | solution.py:56
  67.5 0.1 copy.35
  67.6 0.1 reshape.92
  67.7 0.1 copy.38
  67.8 0.1 reshape.100
  68.0 0.1 copy.42
  68.0 0.1 reshape.82
  68.2 0.7 copy.37
  68.9 2.5 %copy.36 = f32[128,3584]{0,1:T(8,128)} copy(bf16[128,3584]{1,0:T(8,128)(2,1)} %param.6) | data formatting | bytes 2752512 | tf_op jit(solution)/shard_map/convert_element_type | solution.py:62
  71.4 2.6 %gather_fusion.1 = bf16[168,128,64]{1,2,0:T(8,128)(2,1)} fusion(bf16[128,64,64]{0,2,1:T(8,128)(2,1)S(1)} %bitcast.74, s32[1024]{0:T(1024)S(1)} %pad_clamp_fusion), kind=kCustom, calls=%fused_computation.1 | custom fusion | bytes 5505696 | tf_op jit(solution)/shard_map/gather | solution.py:60
  74.0 0.0 collective-permute-done
  74.0 1.2 pad_maximum_fusion
  75.3 2.6 %gather_fusion = bf16[168,4096]{1,0:T(8,128)(2,1)} fusion(bf16[192,4096]{1,0:T(8,128)(2,1)S(1)} %pad_maximum_fusion, s32[1024]{0:T(1024)S(1)} %pad_clamp_fusion.1), kind=kCustom, calls=%fused_computation | custom fusion | bytes 2753184 | tf_op jit(solution)/shard_map/gather | solution.py:58
  77.8 5.2 %reshape.80 = bf16[56,3,64,64]{3,2,1,0:T(8,128)(2,1)} reshape(bf16[168,4096]{1,0:T(8,128)(2,1)} %gather_fusion) | data formatting | bytes 2752512 | tf_op jit(solution)/shard_map/reshape | solution.py:58
  83.0 3.7 %fusion.18 = bf16[128,56,64,1]{0,2,3,1:T(8,128)(2,1)S(1)} fusion(f32[128,56,64]{0,2,1:T(8,128)} %bitcast.80, bf16[56,3,64,64]{3,2,1,0:T(8,128)(2,1)} %reshape.80, bf16[128,56,3,64]{0,3,2,1:T(8,128)(2,1)S(1)} %bitcast.75), kind=kOutput, calls=%fused_computation.23 | convolution fusion | flops 180289536 | bytes 6881280 | tf_op jit(solution)/shard_map/tcki,ckij->tcj/dot_general | solution.py:61
  86.7 0.9 copy-done.2
  87.6 2.2 %fusion.13 = f32[56,3,32,64]{3,2,1,0:T(8,128)} fusion(bf16[128,56,64,1]{0,2,3,1:T(8,128)(2,1)S(1)} %fusion.18, bf16[128,56,3,64]{0,3,2,1:T(8,128)(2,1)S(1)} %bitcast.76), kind=kOutput, calls=%fused_computation.20 | convolution fusion | flops 88080384 | bytes 3670016 | tf_op jit(solution)/shard_map/tcki,tcj->ckij/dot_general | solution.py:86
  89.8 3.1 %reshape.110 = f32[168,2048]{1,0:T(8,128)} reshape(f32[56,3,32,64]{3,2,1,0:T(8,128)} %fusion.13) | data formatting | bytes 2752512 | tf_op jit(solution)/shard_map/reshape | solution.py:92
  93.0 3.4 %scatter_custom_fusion = f32[192,2048]{1,0:T(8,128)} fusion(s32[168]{0:T(256)S(1)} %bitcast.85, f32[168,2048]{1,0:T(8,128)} %reshape.110, f32[]{:T(128)} %constant.117.clone.1), kind=kCustom, calls=%fused_computation.28 | custom fusion | bytes 1573376 | tf_op jit(solution)/shard_map/scatter | solution.py:91
  96.4 1.3 slice.30
  97.7 2.4 %collective-permute-start.4 = (f32[96,2048]{1,0:T(8,128)S(1)}, f32[96,2048]{1,0:T(8,128)S(1)}, u32[]{:S(2)}, u32[]{:S(2)}) collective-permute-start(f32[96,2048]{1,0:T(8,128)S(1)} %slice.30), channel_id=1, source_target_pairs={{0,4},{4,0},{1,5},{5,1},{2,6},{6,2},{3,7},{7,3},{8,12},{12,8},{9,1... | collective-permute-start | bytes 2359304 | tf_op jit(solution)/shard_map/ppermute | solution.py:94
  100.1 1.9 %collective-permute-done.4 = f32[96,2048]{1,0:T(8,128)S(1)} collective-permute-done((f32[96,2048]{1,0:T(8,128)S(1)}, f32[96,2048]{1,0:T(8,128)S(1)}, u32[]{:S(2)}, u32[]{:S(2)}) %collective-permute-start.4) | collective-permute-done | bytes 786464 | tf_op jit(solution)/shard_map/ppermute | solution.py:94
  102.0 0.1 slice_add_fusion.1
  102.1 1.9 %reshape_reshape.6 = f32[8,1,24576]{2,1,0:T(1,128)} reshape(f32[96,2048]{1,0:T(8,128)S(1)} %slice_add_fusion.1) | data formatting | bytes 1572864 | tf_op jit(solution)/shard_map/reshape;reshape | solution.py:31
  104.0 3.7 %all-to-all-start.2 = ((f32[8,1,24576]{2,1,0:T(1,128)}), f32[8,1,24576]{2,1,0:T(1,128)S(1)}, u32[]{:S(2)}, u32[]{:S(2)}) async-start(f32[8,1,24576]{2,1,0:T(1,128)} %reshape_reshape.6), calls=%async_computation.2 | async-start | bytes 1572864 | tf_op jit(solution)/shard_map/all_to_all | solution.py:32
  107.7 3.4 %fusion.11 = f32[56,3,32,64]{3,2,1,0:T(8,128)} fusion(bf16[128,56,64,1]{0,2,3,1:T(8,128)(2,1)} %copy-done.2, bf16[128,56,3,64]{0,3,2,1:T(8,128)(2,1)S(1)} %bitcast.77), kind=kOutput, calls=%fused_computation.18 | convolution fusion | flops 88080384 | bytes 3670016 | tf_op jit(solution)/shard_map/tcki,tcj->ckij/dot_general | solution.py:86
  111.1 3.1 %reshape.118 = f32[168,2048]{1,0:T(8,128)} reshape(f32[56,3,32,64]{3,2,1,0:T(8,128)} %fusion.11) | data formatting | bytes 2752512 | tf_op jit(solution)/shard_map/reshape | solution.py:92
  114.2 2.6 %scatter_custom_fusion.1 = f32[192,2048]{1,0:T(8,128)S(1)} fusion(s32[168]{0:T(256)S(1)} %bitcast.86, f32[168,2048]{1,0:T(8,128)} %reshape.118, f32[]{:T(128)} %constant.117.clone.1), kind=kCustom, calls=%fused_computation.26 | custom fusion | bytes 1573376 | tf_op jit(solution)/shard_map/scatter | solution.py:91
  116.8 0.1 slice.33
  116.9 2.3 %collective-permute-start.5 = (f32[96,2048]{1,0:T(8,128)S(1)}, f32[96,2048]{1,0:T(8,128)S(1)}, u32[]{:S(2)}, u32[]{:S(2)}) collective-permute-start(f32[96,2048]{1,0:T(8,128)S(1)} %slice.33), channel_id=1, source_target_pairs={{0,4},{4,0},{1,5},{5,1},{2,6},{6,2},{3,7},{7,3},{8,12},{12,8},{9,1... | collective-permute-start | bytes 2359304 | tf_op jit(solution)/shard_map/ppermute | solution.py:94
  119.2 1.9 %collective-permute-done.5 = f32[96,2048]{1,0:T(8,128)S(1)} collective-permute-done((f32[96,2048]{1,0:T(8,128)S(1)}, f32[96,2048]{1,0:T(8,128)S(1)}, u32[]{:S(2)}, u32[]{:S(2)}) %collective-permute-start.5) | collective-permute-done | bytes 786464 | tf_op jit(solution)/shard_map/ppermute | solution.py:94
  121.1 1.0 slice_add_fusion
  122.1 3.1 %reshape_reshape.7 = f32[8,1,24576]{2,1,0:T(1,128)} reshape(f32[96,2048]{1,0:T(8,128)} %slice_add_fusion) | data formatting | bytes 1572864 | tf_op jit(solution)/shard_map/reshape;reshape | solution.py:31
  125.2 4.3 %all-to-all-done.2 = f32[8,1,24576]{2,1,0:T(1,128)S(1)} async-done(((f32[8,1,24576]{2,1,0:T(1,128)}), f32[8,1,24576]{2,1,0:T(1,128)S(1)}, u32[]{:S(2)}, u32[]{:S(2)}) %all-to-all-start.2) | async-done | bytes 786464 | tf_op jit(solution)/shard_map/all_to_all | solution.py:32
  129.5 4.2 %all-to-all-start.3 = ((f32[8,1,24576]{2,1,0:T(1,128)}), f32[8,1,24576]{2,1,0:T(1,128)}, u32[]{:S(2)}, u32[]{:S(2)}) async-start(f32[8,1,24576]{2,1,0:T(1,128)} %reshape_reshape.7), calls=%async_computation.3 | async-start | bytes 1572864 | tf_op jit(solution)/shard_map/all_to_all | solution.py:32
  133.8 2.0 %convolution_bitcast_fusion = f32[128,56,3,64]{0,3,2,1:T(8,128)S(1)} fusion(bf16[56,3,64,64]{3,2,1,0:T(8,128)(2,1)S(1)} %copy-done.1, bf16[128,56,64,1]{0,2,3,1:T(8,128)(2,1)} %copy-done.2), kind=kOutput, calls=%fused_computation.6 | convolution fusion | flops 176160768 | bytes 7798784 | tf_op jit(solution)/shard_map/tcj,ckij->tcki/dot_general | solution.py:65
  135.8 5.7 %fusion.15 = bf16[128,64,64]{0,1,2:T(8,128)(2,1)S(1)} fusion(f32[128,56,3,64]{0,3,2,1:T(8,128)S(1)} %convolution_bitcast_fusion, s32[56,3]{0,1:T(4,128)S(1)} %copy-done.5), kind=kOutput, calls=%fused_computation.22 | convolution fusion | flops 1057499648 | bytes 6554272 | tf_op jit(solution)/shard_map/tcki,ckr->tri/dot_general | solution.py:69
  141.5 0.7 copy.41
  142.1 0.6 reduce_sum.27
  142.7 14.6 %all-to-all-done.3 = f32[8,1,24576]{2,1,0:T(1,128)} async-done(((f32[8,1,24576]{2,1,0:T(1,128)}), f32[8,1,24576]{2,1,0:T(1,128)}, u32[]{:S(2)}, u32[]{:S(2)}) %all-to-all-start.3) | async-done | bytes 786464 | tf_op jit(solution)/shard_map/all_to_all | solution.py:32
  157.3 1.7 reduce_sum.28
  159.0 0.9 pad_maximum_fusion.1
  159.9 3.5 %all-to-all-start.4 = ((f32[12,1,4096]{2,1,0:T(1,128)}), f32[12,1,4096]{2,1,0:T(1,128)S(1)}, u32[]{:S(2)}, u32[]{:S(2)}) async-start(f32[12,1,4096]{2,1,0:T(1,128)} %pad_maximum_fusion.1), calls=%async_computation.4 | async-start | bytes 393216 | tf_op jit(solution)/shard_map/all_to_all | solution.py:32
  163.4 0.1 dynamic-slice_bitcast_fusion.2
  163.5 2.4 %collective-permute-start.1 = (bf16[128,1024]{0,1:T(8,128)(2,1)S(1)}, bf16[128,1024]{0,1:T(8,128)(2,1)S(1)}, u32[]{:S(2)}, u32[]{:S(2)}) collective-permute-start(bf16[128,1024]{0,1:T(8,128)(2,1)S(1)} %get-tuple-element.12), channel_id=1, source_target_pairs={{0,1},{1,2},{2,3},{3,0},{4,5},{5,6},{6,7},{7,4},{8,9},{9,10},{10,1... | collective-permute-start | bytes 786440 | tf_op jit(solution)/shard_map/ppermute | solution.py:79
  165.9 3.5 %collective-permute-start.3 = (bf16[128,1024]{0,1:T(8,128)(2,1)S(1)}, bf16[128,1024]{0,1:T(8,128)(2,1)S(1)}, u32[]{:S(2)}, u32[]{:S(2)}) collective-permute-start(bf16[128,1024]{0,1:T(8,128)(2,1)S(1)} %get-tuple-element.13), channel_id=1, source_target_pairs={{0,3},{1,0},{2,1},{3,2},{4,7},{5,4},{6,5},{7,6},{8,11},{9,8},{10,9... | collective-permute-start | bytes 786440 | tf_op jit(solution)/shard_map/ppermute | solution.py:79
  169.3 3.3 %collective-permute-start.2 = (bf16[128,1024]{0,1:T(8,128)(2,1)S(1)}, bf16[128,1024]{0,1:T(8,128)(2,1)S(1)}, u32[]{:S(2)}, u32[]{:S(2)}) collective-permute-start(bf16[128,1024]{0,1:T(8,128)(2,1)S(1)} %get-tuple-element.14), channel_id=1, source_target_pairs={{0,2},{1,3},{2,0},{3,1},{4,6},{5,7},{6,4},{7,5},{8,10},{9,11},{10,... | collective-permute-start | bytes 786440 | tf_op jit(solution)/shard_map/ppermute | solution.py:79
  172.6 1.0 collective-permute-done.1
  173.6 8.9 %collective-permute-done.3 = bf16[128,1024]{0,1:T(8,128)(2,1)S(1)} collective-permute-done((bf16[128,1024]{0,1:T(8,128)(2,1)S(1)}, bf16[128,1024]{0,1:T(8,128)(2,1)S(1)}, u32[]{:S(2)}, u32[]{:S(2)}) %collective-permute-start.3) | collective-permute-done | bytes 262176 | tf_op jit(solution)/shard_map/ppermute | solution.py:79
  182.5 0.1 fusion.25
  182.7 0.9 copy.43
  183.5 0.7 reduce_sum.29
  (20 shorter events, 0.1 us)
Async XLA Ops:
  31.5 35.9 %copy-start.6 = (s32[56,3]{0,1:T(4,128)S(1)}, s32[56,3]{0,1:T(4,128)}, u32[]{:S(2)}) copy-start(s32[56,3]{0,1:T(4,128)} %param.9) | copy-start | bytes 2020
  31.5 36.2 %copy-start.5 = (s32[56,3]{0,1:T(4,128)S(1)}, s32[56,3]{0,1:T(4,128)}, u32[]{:S(2)}) copy-start(s32[56,3]{0,1:T(4,128)} %param.8) | copy-start | bytes 2020
  31.5 36.6 %copy-start.4 = (bf16[128,4096]{1,0:T(8,128)(2,1)S(1)}, bf16[128,4096]{1,0:T(8,128)(2,1)}, u32[]{:S(2)}) copy-start(bf16[128,4096]{1,0:T(8,128)(2,1)} %param.5) | copy-start | bytes 3145732
  31.5 33.8 %all-to-all-start.1 = ((bf16[8,12,4096]{2,1,0:T(8,128)(2,1)}), bf16[8,12,4096]{2,1,0:T(8,128)(2,1)S(1)}, u32[]{:S(2)}, u32[]{:S(2)}) async-start(bf16[8,12,4096]{2,1,0:T(8,128)(2,1)} %broadcast_in_dim.27), calls=%async_computation.1 | async-start | bytes 2097152 | tf_op jit(solution)/shard_map/all_to_all | solution.py:26
  65.5 8.5 %collective-permute-start = (bf16[96,4096]{1,0:T(8,128)(2,1)S(1)}, bf16[96,4096]{1,0:T(8,128)(2,1)}, u32[]{:S(2)}, u32[]{:S(2)}) collective-permute-start(bf16[96,4096]{1,0:T(8,128)(2,1)S(1)} %reshape.79), channel_id=1, source_target_pairs={{0,4},{4,0},{1,5},{5,1},{2,6},{6,2},{3,7},{7,3},{8,12},{12,8},{9,1... | collective-permute-start | bytes 2359304 | tf_op jit(solution)/shard_map/ppermute | solution.py:56
  77.8 5.2 %copy-start = (bf16[168,128,64]{1,2,0:T(8,128)(2,1)S(1)}, bf16[168,128,64]{1,2,0:T(8,128)(2,1)}, u32[]{:S(2)}) copy-start(bf16[168,128,64]{1,2,0:T(8,128)(2,1)} %gather_fusion.1) | copy-start | bytes 8257540
  86.7 0.9 copy-start.2
  96.4 5.6 %copy-start.3 = (f32[192,2048]{1,0:T(8,128)S(1)}, f32[192,2048]{1,0:T(8,128)}, u32[]{:S(2)}) copy-start(f32[192,2048]{1,0:T(8,128)} %scatter_custom_fusion) | copy-start | bytes 4718596
  97.7 4.3 %collective-permute-start.4 = (f32[96,2048]{1,0:T(8,128)S(1)}, f32[96,2048]{1,0:T(8,128)S(1)}, u32[]{:S(2)}, u32[]{:S(2)}) collective-permute-start(f32[96,2048]{1,0:T(8,128)S(1)} %slice.30), channel_id=1, source_target_pairs={{0,4},{4,0},{1,5},{5,1},{2,6},{6,2},{3,7},{7,3},{8,12},{12,8},{9,1... | collective-permute-start | bytes 2359304 | tf_op jit(solution)/shard_map/ppermute | solution.py:94
  104.0 25.5 %all-to-all-start.2 = ((f32[8,1,24576]{2,1,0:T(1,128)}), f32[8,1,24576]{2,1,0:T(1,128)S(1)}, u32[]{:S(2)}, u32[]{:S(2)}) async-start(f32[8,1,24576]{2,1,0:T(1,128)} %reshape_reshape.6), calls=%async_computation.2 | async-start | bytes 1572864 | tf_op jit(solution)/shard_map/all_to_all | solution.py:32
  116.9 4.2 %collective-permute-start.5 = (f32[96,2048]{1,0:T(8,128)S(1)}, f32[96,2048]{1,0:T(8,128)S(1)}, u32[]{:S(2)}, u32[]{:S(2)}) collective-permute-start(f32[96,2048]{1,0:T(8,128)S(1)} %slice.33), channel_id=1, source_target_pairs={{0,4},{4,0},{1,5},{5,1},{2,6},{6,2},{3,7},{7,3},{8,12},{12,8},{9,1... | collective-permute-start | bytes 2359304 | tf_op jit(solution)/shard_map/ppermute | solution.py:94
  122.1 11.7 %copy-start.1 = (bf16[56,3,64,64]{3,2,1,0:T(8,128)(2,1)S(1)}, bf16[56,3,64,64]{3,2,1,0:T(8,128)(2,1)}, u32[]{:S(2)}) copy-start(bf16[56,3,64,64]{3,2,1,0:T(8,128)(2,1)} %reshape.80) | copy-start | bytes 4128772
  129.5 27.8 %all-to-all-start.3 = ((f32[8,1,24576]{2,1,0:T(1,128)}), f32[8,1,24576]{2,1,0:T(1,128)}, u32[]{:S(2)}, u32[]{:S(2)}) async-start(f32[8,1,24576]{2,1,0:T(1,128)} %reshape_reshape.7), calls=%async_computation.3 | async-start | bytes 1572864 | tf_op jit(solution)/shard_map/all_to_all | solution.py:32
  159.9 23.7 %all-to-all-start.4 = ((f32[12,1,4096]{2,1,0:T(1,128)}), f32[12,1,4096]{2,1,0:T(1,128)S(1)}, u32[]{:S(2)}, u32[]{:S(2)}) async-start(f32[12,1,4096]{2,1,0:T(1,128)} %pad_maximum_fusion.1), calls=%async_computation.4 | async-start | bytes 393216 | tf_op jit(solution)/shard_map/all_to_all | solution.py:32
  163.5 10.1 %collective-permute-start.1 = (bf16[128,1024]{0,1:T(8,128)(2,1)S(1)}, bf16[128,1024]{0,1:T(8,128)(2,1)S(1)}, u32[]{:S(2)}, u32[]{:S(2)}) collective-permute-start(bf16[128,1024]{0,1:T(8,128)(2,1)S(1)} %get-tuple-element.12), channel_id=1, source_target_pairs={{0,1},{1,2},{2,3},{3,0},{4,5},{5,6},{6,7},{7,4},{8,9},{9,10},{10,1... | collective-permute-start | bytes 786440 | tf_op jit(solution)/shard_map/ppermute | solution.py:79
  165.9 16.7 %collective-permute-start.3 = (bf16[128,1024]{0,1:T(8,128)(2,1)S(1)}, bf16[128,1024]{0,1:T(8,128)(2,1)S(1)}, u32[]{:S(2)}, u32[]{:S(2)}) collective-permute-start(bf16[128,1024]{0,1:T(8,128)(2,1)S(1)} %get-tuple-element.13), channel_id=1, source_target_pairs={{0,3},{1,0},{2,1},{3,2},{4,7},{5,4},{6,5},{7,6},{8,11},{9,8},{10,9... | collective-permute-start | bytes 786440 | tf_op jit(solution)/shard_map/ppermute | solution.py:79
  169.3 13.2 %collective-permute-start.2 = (bf16[128,1024]{0,1:T(8,128)(2,1)S(1)}, bf16[128,1024]{0,1:T(8,128)(2,1)S(1)}, u32[]{:S(2)}, u32[]{:S(2)}) collective-permute-start(bf16[128,1024]{0,1:T(8,128)(2,1)S(1)} %get-tuple-element.14), channel_id=1, source_target_pairs={{0,2},{1,3},{2,0},{3,1},{4,6},{5,7},{6,4},{7,5},{8,10},{9,11},{10,... | collective-permute-start | bytes 786440 | tf_op jit(solution)/shard_map/ppermute | solution.py:79

commit v5 on v2

--- a/solution.py
+++ b/solution.py
@@ -87,6 +87,7 @@
         chip_sum = slot_store[:half] + lax.ppermute(slot_store[half:], "c", [(0, 1), (1, 0)])
         by_y = chip_sum.reshape(ny, nz * cap * flat)
         col_sum = reduce_by_a2a(by_y, "y", ny).reshape(nz, cap * flat)
+        col_sum, grad_inputs = lax.optimization_barrier((col_sum, grad_inputs))
         owned = reduce_by_a2a(col_sum, "z", nz)
         return (grad_inputs, owned.reshape(1, cap, flat))
 

time: 186 us -> 179 us (0.962)
  the two profiles are of different devices: /device:TPU:9 before, /device:TPU:6 now
where the time goes in v5:
time: 179 us; the launch traced here: 178 us
  waiting for transfers between devices  64.2 us (36%)
  local copies, waits for them, and re-layouts  33.5 us (19%)
  starting transfers between devices  29.3 us (16%)
  blocking collectives  26.9 us (15%)
  matrix products  14.7 us (8%)
  other arithmetic  8.04 us (4%)
    all_to_all x1, blocking collectives, gather_by_a2a(): got = lax.all_to_all(copies, name, 0, 0, tiled=True)  26.9 us
    all_to_all x1, waiting for transfers between devices, gather_by_a2a(): got = lax.all_to_all(copies, name, 0, 0, tiled=True)  26.6 us
    all_to_all x2, waiting for transfers between devices, reduce_by_a2a(): got = lax.all_to_all(parts, name, 0, 0, tiled=True)  24.6 us
    ppermute x3, waiting for transfers between devices, local(): got = lax.ppermute(send, 'x', [(j, (j + shift) % nx) for j in range(nx)])  10.1 us
    ppermute x3, starting transfers between devices, local(): got = lax.ppermute(send, 'x', [(j, (j + shift) % nx) for j in range(nx)])  9.76 us
    all_to_all x2, starting transfers between devices, reduce_by_a2a(): got = lax.all_to_all(parts, name, 0, 0, tiled=True)  8 us
    all_to_all x1, starting transfers between devices, gather_by_a2a(): got = lax.all_to_all(copies, name, 0, 0, tiled=True)  7.23 us
    dot_general x1, matrix products, local(): jnp.einsum('tcki,ckr->tri', back_all, row_select, precision=lax.Precision...  5.67 us
  transfers between devices with their start and end apart: 8, of which 6 were waited for; matrix products, arithmetic and copies ran while one was open for 9% of the time, Pallas kernels for 0%

profile of v5, /device:TPU:6, one launch (start us, length us, event | category | flops | bytes accessed | tf_op | source)
XLA Modules:
  0.0 177.6 jit_solution(17792242469852125100)
XLA Ops:
  0.6 0.8 reduce.2
  1.4 0.1 broadcast_in_dim.29
  1.5 0.5 broadcast.79
  2.1 1.2 reduce.3
  3.3 0.1 reshape.119
  3.3 26.9 %all_to_all.20 = bf16[12,2,2048]{2,1,0:T(2,128)(2,1)S(1)} all-to-all(bf16[12,2,2048]{2,1,0:T(2,128)(2,1)S(1)} %reshape.119), channel_id=1, replica_groups=mesh['y'=8,'z'=12,'c'=2,'x'=4] {'z'}, dimensions={0} | all-to-all | bytes 196608 | tf_op jit(solution)/shard_map/all_to_all | solution.py:26
  30.3 0.1 reshape.120
  30.4 0.0 copy-start.5
  30.4 0.0 copy-start.3
  30.4 0.1 copy.48
  30.5 1.1 broadcast_in_dim.31
  31.6 0.0 copy-start.4
  31.6 7.2 %all-to-all-start.1 = ((bf16[8,12,4096]{2,1,0:T(8,128)(2,1)}), bf16[8,12,4096]{2,1,0:T(8,128)(2,1)S(1)}, u32[]{:S(2)}, u32[]{:S(2)}) async-start(bf16[8,12,4096]{2,1,0:T(8,128)(2,1)} %broadcast_in_dim.31), calls=%async_computation.1 | async-start | bytes 2097152 | tf_op jit(solution)/shard_map/all_to_all | solution.py:26
  38.8 26.6 %all-to-all-done.1 = bf16[8,12,4096]{2,1,0:T(8,128)(2,1)S(1)} async-done(((bf16[8,12,4096]{2,1,0:T(8,128)(2,1)}), bf16[8,12,4096]{2,1,0:T(8,128)(2,1)S(1)}, u32[]{:S(2)}, u32[]{:S(2)}) %all-to-all-start.1) | async-done | bytes 786464 | tf_op jit(solution)/shard_map/all_to_all | solution.py:26
  65.4 0.2 reshape.75
  65.5 1.9 %collective-permute-start = (bf16[96,4096]{1,0:T(8,128)(2,1)S(1)}, bf16[96,4096]{1,0:T(8,128)(2,1)}, u32[]{:S(2)}, u32[]{:S(2)}) collective-permute-start(bf16[96,4096]{1,0:T(8,128)(2,1)S(1)} %reshape.75), channel_id=1, source_target_pairs={{0,4},{4,0},{1,5},{5,1},{2,6},{6,2},{3,7},{7,3},{8,12},{12,8},{9,1... | collective-permute-start | bytes 2359304 | tf_op jit(solution)/shard_map/ppermute | solution.py:56
  67.5 0.0 copy-done.5
  67.5 0.1 copy.27
  67.6 0.1 reshape.73
  67.7 0.0 copy-done.3
  67.7 0.7 copy.28
  68.4 0.0 copy-done.4
  68.4 0.1 copy.29
  68.5 0.1 reshape.85
  68.7 2.5 %copy.30 = f32[128,3584]{0,1:T(8,128)} copy(bf16[128,3584]{1,0:T(8,128)(2,1)} %param.6) | data formatting | bytes 2752512 | tf_op jit(solution)/shard_map/convert_element_type | solution.py:62
  71.1 0.1 copy.31
  71.2 0.1 reshape.93
  71.4 2.6 %gather_fusion = bf16[168,128,64]{1,2,0:T(8,128)(2,1)} fusion(bf16[128,64,64]{0,2,1:T(8,128)(2,1)S(1)} %bitcast.68, s32[1024]{0:T(1024)S(1)} %pad_clamp_fusion.1), kind=kCustom, calls=%fused_computation | custom fusion | bytes 5505696 | tf_op jit(solution)/shard_map/gather | solution.py:60
  74.0 0.0 collective-permute-done
  74.0 1.2 pad_maximum_fusion
  75.2 2.6 %gather_fusion.1 = bf16[168,4096]{1,0:T(8,128)(2,1)} fusion(bf16[192,4096]{1,0:T(8,128)(2,1)S(1)} %pad_maximum_fusion, s32[1024]{0:T(1024)S(1)} %pad_clamp_fusion), kind=kCustom, calls=%fused_computation.1 | custom fusion | bytes 2753184 | tf_op jit(solution)/shard_map/gather | solution.py:58
  77.8 5.2 %reshape.76 = bf16[56,3,64,64]{3,2,1,0:T(8,128)(2,1)} reshape(bf16[168,4096]{1,0:T(8,128)(2,1)} %gather_fusion.1) | data formatting | bytes 2752512 | tf_op jit(solution)/shard_map/reshape | solution.py:58
  83.0 0.0 copy-done
  83.0 3.7 %fusion.16 = bf16[128,56,64,1]{0,2,3,1:T(8,128)(2,1)S(1)} fusion(f32[128,56,64]{0,2,1:T(8,128)} %bitcast.73, bf16[56,3,64,64]{3,2,1,0:T(8,128)(2,1)} %reshape.76, bf16[128,56,3,64]{0,3,2,1:T(8,128)(2,1)S(1)} %bitcast.69), kind=kOutput, calls=%fused_computation.21 | convolution fusion | flops 180289536 | bytes 6881280 | tf_op jit(solution)/shard_map/tcki,ckij->tcj/dot_general | solution.py:61
  86.7 0.0 copy-start.2
  86.7 0.9 copy-done.2
  87.6 3.3 %fusion.33 = f32[56,3,64,64]{3,2,1,0:T(8,128)} fusion(bf16[128,56,3,64]{0,3,2,1:T(8,128)(2,1)S(1)} %bitcast.70, bf16[128,56,64,1]{0,2,3,1:T(8,128)(2,1)S(1)} %fusion.16), kind=kOutput, calls=%fused_computation.59 | convolution fusion | flops 176160768 | bytes 6422528 | tf_op jit(solution)/shard_map/tcki,tcj->ckij/dot_general | solution.py:82
  90.9 5.5 %reshape.103 = f32[168,4096]{1,0:T(8,128)} reshape(f32[56,3,64,64]{3,2,1,0:T(8,128)} %fusion.33) | data formatting | bytes 5505024 | tf_op jit(solution)/shard_map/reshape | solution.py:85
  96.4 4.1 %scatter_custom_fusion = f32[192,4096]{1,0:T(8,128)S(1)} fusion(s32[168]{0:T(256)S(1)} %bitcast.76, f32[168,4096]{1,0:T(8,128)} %reshape.103, f32[]{:T(128)} %constant.102.clone.1), kind=kCustom, calls=%fused_computation.18 | custom fusion | bytes 3146240 | tf_op jit(solution)/shard_map/scatter | solution.py:84
  100.5 0.1 slice.13
  100.6 2.4 %collective-permute-start.1 = (f32[96,4096]{1,0:T(8,128)S(1)}, f32[96,4096]{1,0:T(8,128)S(1)}, u32[]{:S(2)}, u32[]{:S(2)}) collective-permute-start(f32[96,4096]{1,0:T(8,128)S(1)} %slice.13), channel_id=1, source_target_pairs={{0,4},{4,0},{1,5},{5,1},{2,6},{6,2},{3,7},{7,3},{8,12},{12,8},{9,1... | collective-permute-start | bytes 4718600 | tf_op jit(solution)/shard_map/ppermute | solution.py:87
  103.0 3.0 %collective-permute-done.1 = f32[96,4096]{1,0:T(8,128)S(1)} collective-permute-done((f32[96,4096]{1,0:T(8,128)S(1)}, f32[96,4096]{1,0:T(8,128)S(1)}, u32[]{:S(2)}, u32[]{:S(2)}) %collective-permute-start.1) | collective-permute-done | bytes 1572896 | tf_op jit(solution)/shard_map/ppermute | solution.py:87
  106.0 1.4 slice_add_fusion
  107.4 4.1 %reshape_reshape.3 = f32[8,1,49152]{2,1,0:T(1,128)} reshape(f32[96,4096]{1,0:T(8,128)} %slice_add_fusion) | data formatting | bytes 3145728 | tf_op jit(solution)/shard_map/reshape;reshape | solution.py:31
  111.4 4.5 %all-to-all-start.2 = ((f32[8,1,49152]{2,1,0:T(1,128)}), f32[8,1,49152]{2,1,0:T(1,128)}, u32[]{:S(2)}, u32[]{:S(2)}) async-start(f32[8,1,49152]{2,1,0:T(1,128)} %reshape_reshape.3), calls=%async_computation.2 | async-start | bytes 3145728 | tf_op jit(solution)/shard_map/all_to_all | solution.py:32
  116.0 0.0 copy-done.1
  116.0 2.0 %convolution_bitcast_fusion = f32[128,56,3,64]{0,3,2,1:T(8,128)S(1)} fusion(bf16[56,3,64,64]{3,2,1,0:T(8,128)(2,1)S(1)} %copy-done.1, bf16[128,56,64,1]{0,2,3,1:T(8,128)(2,1)} %copy-done.2), kind=kOutput, calls=%fused_computation.5 | convolution fusion | flops 176160768 | bytes 7798784 | tf_op jit(solution)/shard_map/tcj,ckij->tcki/dot_general | solution.py:65
  118.0 5.7 %fusion.13 = bf16[128,64,64]{0,1,2:T(8,128)(2,1)S(1)} fusion(f32[128,56,3,64]{0,3,2,1:T(8,128)S(1)} %convolution_bitcast_fusion, s32[56,3]{0,1:T(4,128)S(1)} %copy-done.4), kind=kOutput, calls=%fused_computation.20 | convolution fusion | flops 1057499648 | bytes 6554272 | tf_op jit(solution)/shard_map/tcki,ckr->tri/dot_general | solution.py:69
  123.7 0.7 copy.34
  124.4 0.1 dynamic-slice_bitcast_fusion.2
  124.4 2.7 %collective-permute-start.4 = (bf16[128,1024]{0,1:T(8,128)(2,1)S(1)}, bf16[128,1024]{0,1:T(8,128)(2,1)S(1)}, u32[]{:S(2)}, u32[]{:S(2)}) collective-permute-start(bf16[128,1024]{0,1:T(8,128)(2,1)S(1)} %get-tuple-element.15), channel_id=1, source_target_pairs={{0,3},{1,0},{2,1},{3,2},{4,7},{5,4},{6,5},{7,6},{8,11},{9,8},{10,9... | collective-permute-start | bytes 786440 | tf_op jit(solution)/shard_map/ppermute | solution.py:79
  127.2 3.0 %collective-permute-start.3 = (bf16[128,1024]{0,1:T(8,128)(2,1)S(1)}, bf16[128,1024]{0,1:T(8,128)(2,1)S(1)}, u32[]{:S(2)}, u32[]{:S(2)}) collective-permute-start(bf16[128,1024]{0,1:T(8,128)(2,1)S(1)} %get-tuple-element.16), channel_id=1, source_target_pairs={{0,2},{1,3},{2,0},{3,1},{4,6},{5,7},{6,4},{7,5},{8,10},{9,11},{10,... | collective-permute-start | bytes 786440 | tf_op jit(solution)/shard_map/ppermute | solution.py:79
  130.2 4.0 %collective-permute-start.2 = (bf16[128,1024]{0,1:T(8,128)(2,1)S(1)}, bf16[128,1024]{0,1:T(8,128)(2,1)S(1)}, u32[]{:S(2)}, u32[]{:S(2)}) collective-permute-start(bf16[128,1024]{0,1:T(8,128)(2,1)S(1)} %get-tuple-element.14), channel_id=1, source_target_pairs={{0,1},{1,2},{2,3},{3,0},{4,5},{5,6},{6,7},{7,4},{8,9},{9,10},{10,1... | collective-permute-start | bytes 786440 | tf_op jit(solution)/shard_map/ppermute | solution.py:79
  134.2 7.5 %collective-permute-done.4 = bf16[128,1024]{0,1:T(8,128)(2,1)S(1)} collective-permute-done((bf16[128,1024]{0,1:T(8,128)(2,1)S(1)}, bf16[128,1024]{0,1:T(8,128)(2,1)S(1)}, u32[]{:S(2)}, u32[]{:S(2)}) %collective-permute-start.4) | collective-permute-done | bytes 262176 | tf_op jit(solution)/shard_map/ppermute | solution.py:79
  141.7 0.0 collective-permute-done.3
  141.7 2.5 %collective-permute-done.2 = bf16[128,1024]{0,1:T(8,128)(2,1)S(1)} collective-permute-done((bf16[128,1024]{0,1:T(8,128)(2,1)S(1)}, bf16[128,1024]{0,1:T(8,128)(2,1)S(1)}, u32[]{:S(2)}, u32[]{:S(2)}) %collective-permute-start.2) | collective-permute-done | bytes 262176 | tf_op jit(solution)/shard_map/ppermute | solution.py:79
  144.3 0.1 fusion.19
  144.4 12.3 %all-to-all-done.2 = f32[8,1,49152]{2,1,0:T(1,128)} async-done(((f32[8,1,49152]{2,1,0:T(1,128)}), f32[8,1,49152]{2,1,0:T(1,128)}, u32[]{:S(2)}, u32[]{:S(2)}) %all-to-all-start.2) | async-done | bytes 1572896 | tf_op jit(solution)/shard_map/all_to_all | solution.py:32
  156.7 2.6 %reduce_sum.18 = f32[49152]{0:T(1024)S(1)} reduce(f32[8,1,49152]{2,1,0:T(1,128)} %all-to-all-done.2, f32[]{:T(128)} %constant.102.clone.1), dimensions={0,1}, to_apply=%region_1.2 | reduce | flops 344064 | bytes 1769476 | tf_op jit(solution)/shard_map/reduce_sum | solution.py:33
  159.3 0.9 reshape.79
  160.1 3.5 %all-to-all-start.3 = ((f32[12,1,4096]{2,1,0:T(1,128)}), f32[12,1,4096]{2,1,0:T(1,128)S(1)}, u32[]{:S(2)}, u32[]{:S(2)}) async-start(f32[12,1,4096]{2,1,0:T(1,128)} %reshape.79), calls=%async_computation.3 | async-start | bytes 393216 | tf_op jit(solution)/shard_map/all_to_all | solution.py:32
  163.7 0.9 copy.35
  164.5 12.3 %all-to-all-done.3 = f32[12,1,4096]{2,1,0:T(1,128)S(1)} async-done(((f32[12,1,4096]{2,1,0:T(1,128)}), f32[12,1,4096]{2,1,0:T(1,128)S(1)}, u32[]{:S(2)}, u32[]{:S(2)}) %all-to-all-start.3) | async-done | bytes 196640 | tf_op jit(solution)/shard_map/all_to_all | solution.py:32
  176.9 0.7 reduce_sum.19
  (8 shorter events, 0.1 us)
Async XLA Ops:
  30.4 37.1 %copy-start.5 = (s32[56,3]{0,1:T(4,128)S(1)}, s32[56,3]{0,1:T(4,128)}, u32[]{:S(2)}) copy-start(s32[56,3]{0,1:T(4,128)} %param.9) | copy-start | bytes 2020
  30.4 37.4 %copy-start.3 = (bf16[128,4096]{1,0:T(8,128)(2,1)S(1)}, bf16[128,4096]{1,0:T(8,128)(2,1)}, u32[]{:S(2)}) copy-start(bf16[128,4096]{1,0:T(8,128)(2,1)} %param.5) | copy-start | bytes 3145732
  31.6 36.8 %copy-start.4 = (s32[56,3]{0,1:T(4,128)S(1)}, s32[56,3]{0,1:T(4,128)}, u32[]{:S(2)}) copy-start(s32[56,3]{0,1:T(4,128)} %param.8) | copy-start | bytes 2020
  31.6 33.8 %all-to-all-start.1 = ((bf16[8,12,4096]{2,1,0:T(8,128)(2,1)}), bf16[8,12,4096]{2,1,0:T(8,128)(2,1)S(1)}, u32[]{:S(2)}, u32[]{:S(2)}) async-start(bf16[8,12,4096]{2,1,0:T(8,128)(2,1)} %broadcast_in_dim.31), calls=%async_computation.1 | async-start | bytes 2097152 | tf_op jit(solution)/shard_map/all_to_all | solution.py:26
  65.5 8.4 %collective-permute-start = (bf16[96,4096]{1,0:T(8,128)(2,1)S(1)}, bf16[96,4096]{1,0:T(8,128)(2,1)}, u32[]{:S(2)}, u32[]{:S(2)}) collective-permute-start(bf16[96,4096]{1,0:T(8,128)(2,1)S(1)} %reshape.75), channel_id=1, source_target_pairs={{0,4},{4,0},{1,5},{5,1},{2,6},{6,2},{3,7},{7,3},{8,12},{12,8},{9,1... | collective-permute-start | bytes 2359304 | tf_op jit(solution)/shard_map/ppermute | solution.py:56
  77.8 5.2 %copy-start = (bf16[168,128,64]{1,2,0:T(8,128)(2,1)S(1)}, bf16[168,128,64]{1,2,0:T(8,128)(2,1)}, u32[]{:S(2)}) copy-start(bf16[168,128,64]{1,2,0:T(8,128)(2,1)} %gather_fusion) | copy-start | bytes 8257540
  86.7 0.9 copy-start.2
  100.6 5.4 %collective-permute-start.1 = (f32[96,4096]{1,0:T(8,128)S(1)}, f32[96,4096]{1,0:T(8,128)S(1)}, u32[]{:S(2)}, u32[]{:S(2)}) collective-permute-start(f32[96,4096]{1,0:T(8,128)S(1)} %slice.13), channel_id=1, source_target_pairs={{0,4},{4,0},{1,5},{5,1},{2,6},{6,2},{3,7},{7,3},{8,12},{12,8},{9,1... | collective-permute-start | bytes 4718600 | tf_op jit(solution)/shard_map/ppermute | solution.py:87
  107.4 8.6 %copy-start.1 = (bf16[56,3,64,64]{3,2,1,0:T(8,128)(2,1)S(1)}, bf16[56,3,64,64]{3,2,1,0:T(8,128)(2,1)}, u32[]{:S(2)}) copy-start(bf16[56,3,64,64]{3,2,1,0:T(8,128)(2,1)} %reshape.76) | copy-start | bytes 4128772
  111.4 45.3 %all-to-all-start.2 = ((f32[8,1,49152]{2,1,0:T(1,128)}), f32[8,1,49152]{2,1,0:T(1,128)}, u32[]{:S(2)}, u32[]{:S(2)}) async-start(f32[8,1,49152]{2,1,0:T(1,128)} %reshape_reshape.3), calls=%async_computation.2 | async-start | bytes 3145728 | tf_op jit(solution)/shard_map/all_to_all | solution.py:32
  124.4 17.3 %collective-permute-start.4 = (bf16[128,1024]{0,1:T(8,128)(2,1)S(1)}, bf16[128,1024]{0,1:T(8,128)(2,1)S(1)}, u32[]{:S(2)}, u32[]{:S(2)}) collective-permute-start(bf16[128,1024]{0,1:T(8,128)(2,1)S(1)} %get-tuple-element.15), channel_id=1, source_target_pairs={{0,3},{1,0},{2,1},{3,2},{4,7},{5,4},{6,5},{7,6},{8,11},{9,8},{10,9... | collective-permute-start | bytes 786440 | tf_op jit(solution)/shard_map/ppermute | solution.py:79
  127.2 14.6 %collective-permute-start.3 = (bf16[128,1024]{0,1:T(8,128)(2,1)S(1)}, bf16[128,1024]{0,1:T(8,128)(2,1)S(1)}, u32[]{:S(2)}, u32[]{:S(2)}) collective-permute-start(bf16[128,1024]{0,1:T(8,128)(2,1)S(1)} %get-tuple-element.16), channel_id=1, source_target_pairs={{0,2},{1,3},{2,0},{3,1},{4,6},{5,7},{6,4},{7,5},{8,10},{9,11},{10,... | collective-permute-start | bytes 786440 | tf_op jit(solution)/shard_map/ppermute | solution.py:79
  130.2 14.1 %collective-permute-start.2 = (bf16[128,1024]{0,1:T(8,128)(2,1)S(1)}, bf16[128,1024]{0,1:T(8,128)(2,1)S(1)}, u32[]{:S(2)}, u32[]{:S(2)}) collective-permute-start(bf16[128,1024]{0,1:T(8,128)(2,1)S(1)} %get-tuple-element.14), channel_id=1, source_target_pairs={{0,1},{1,2},{2,3},{3,0},{4,5},{5,6},{6,7},{7,4},{8,9},{9,10},{10,1... | collective-permute-start | bytes 786440 | tf_op jit(solution)/shard_map/ppermute | solution.py:79
  160.1 16.7 %all-to-all-start.3 = ((f32[12,1,4096]{2,1,0:T(1,128)}), f32[12,1,4096]{2,1,0:T(1,128)S(1)}, u32[]{:S(2)}, u32[]{:S(2)}) async-start(f32[12,1,4096]{2,1,0:T(1,128)} %reshape.79), calls=%async_computation.3 | async-start | bytes 393216 | tf_op jit(solution)/shard_map/all_to_all | solution.py:32

commit v6 on v5

--- a/solution.py
+++ b/solution.py
@@ -80,11 +80,15 @@
             acc = acc + got.astype(jnp.float32)
         grad_inputs = acc.astype(jnp.bfloat16)
         grad_term = jnp.einsum("tcki,tcj->ckij", picked, pre_grad, preferred_element_type=jnp.float32)
-        slot_store = jnp.zeros((nc * half, flat), jnp.float32)
-        slot_store = slot_store.at[rel_slot.reshape(-1)].set(
-            grad_term.reshape(per_slice * keep_count, flat)
-        )
-        chip_sum = slot_store[:half] + lax.ppermute(slot_store[half:], "c", [(0, 1), (1, 0)])
+        grad_rows = grad_term.reshape(per_slice * keep_count, flat)
+        flat_slot = rel_slot.reshape(-1)
+        to_partner = flat_slot >= half
+        partner_slot = jnp.where(to_partner, flat_slot - half, half)
+        own_slot = jnp.where(to_partner, half, flat_slot)
+        partner_store = jnp.zeros((half, flat), jnp.float32).at[partner_slot].set(grad_rows, mode="drop")
+        arrived = lax.ppermute(partner_store, "c", [(0, 1), (1, 0)])
+        own_store = jnp.zeros((half, flat), jnp.float32).at[own_slot].set(grad_rows, mode="drop")
+        chip_sum = own_store + arrived
         by_y = chip_sum.reshape(ny, nz * cap * flat)
         col_sum = reduce_by_a2a(by_y, "y", ny).reshape(nz, cap * flat)
         col_sum, grad_inputs = lax.optimization_barrier((col_sum, grad_inputs))

time: 179 us -> 176 us (0.983)
  waiting for transfers between devices: 64.2 us -> 60.8 us
    ppermute x1, waiting for transfers between devices: 3.01 us -> 0.01 us  [local(): arrived = lax.ppermute(partner_store, 'c', [(0, 1), (1, 0)])]
    scatter x1 -> x2, local copies, waits for them, and re-layouts: 4.11 us -> 7.04 us  [the longest x1 3.73 us: local(): jnp.zeros((half, flat), jnp.float32).at[own_slot]]
  transfers between devices with their start and end apart: 8 -> 8, of which waited for: 6 -> 5; matrix products, arithmetic and copies ran while one was open for 9% -> 11% of each run, Pallas kernels for 0% -> 0%
where the time goes in v6:
time: 176 us; the launch traced here: 175 us
  waiting for transfers between devices  60.8 us (35%)
  local copies, waits for them, and re-layouts  33.7 us (19%)
  starting transfers between devices  29.6 us (17%)
  blocking collectives  26.9 us (15%)
  matrix products  14.7 us (8%)
  other arithmetic  8.26 us (5%)
    all_to_all x1, blocking collectives, gather_by_a2a(): got = lax.all_to_all(copies, name, 0, 0, tiled=True)  26.9 us
    all_to_all x1, waiting for transfers between devices, gather_by_a2a(): got = lax.all_to_all(copies, name, 0, 0, tiled=True)  26.5 us
    all_to_all x2, waiting for transfers between devices, reduce_by_a2a(): got = lax.all_to_all(parts, name, 0, 0, tiled=True)  24.6 us
    ppermute x3, starting transfers between devices, local(): got = lax.ppermute(send, 'x', [(j, (j + shift) % nx) for j in range(nx)])  9.77 us
    ppermute x3, waiting for transfers between devices, local(): got = lax.ppermute(send, 'x', [(j, (j + shift) % nx) for j in range(nx)])  9.69 us
    all_to_all x2, starting transfers between devices, reduce_by_a2a(): got = lax.all_to_all(parts, name, 0, 0, tiled=True)  8.08 us
    all_to_all x1, starting transfers between devices, gather_by_a2a(): got = lax.all_to_all(copies, name, 0, 0, tiled=True)  7.23 us
    dot_general x1, matrix products, local(): jnp.einsum('tcki,ckr->tri', back_all, row_select, precision=lax.Precision...  5.67 us
  transfers between devices with their start and end apart: 8, of which 5 were waited for; matrix products, arithmetic and copies ran while one was open for 11% of the time, Pallas kernels for 0%

profile of v6, /device:TPU:6, one launch (start us, length us, event | category | flops | bytes accessed | tf_op | source)
XLA Modules:
  0.0 174.9 jit_solution(2254484640820073629)
XLA Ops:
  0.6 0.8 reduce.2
  1.4 0.1 broadcast_in_dim.30
  1.5 0.5 broadcast.150
  2.1 1.2 reduce.3
  3.3 0.1 reshape.154
  3.3 26.9 %all_to_all.20 = bf16[12,2,2048]{2,1,0:T(2,128)(2,1)S(1)} all-to-all(bf16[12,2,2048]{2,1,0:T(2,128)(2,1)S(1)} %reshape.154), channel_id=1, replica_groups=mesh['y'=8,'z'=12,'c'=2,'x'=4] {'z'}, dimensions={0} | all-to-all | bytes 196608 | tf_op jit(solution)/shard_map/all_to_all | solution.py:26
  30.3 0.1 reshape.155
  30.4 0.1 copy.48
  30.5 1.1 broadcast_in_dim.32
  31.6 0.0 copy-start.6
  31.6 7.2 %all-to-all-start.1 = ((bf16[8,12,4096]{2,1,0:T(8,128)(2,1)}), bf16[8,12,4096]{2,1,0:T(8,128)(2,1)S(1)}, u32[]{:S(2)}, u32[]{:S(2)}) async-start(bf16[8,12,4096]{2,1,0:T(8,128)(2,1)} %broadcast_in_dim.32), calls=%async_computation.1 | async-start | bytes 2097152 | tf_op jit(solution)/shard_map/all_to_all | solution.py:26
  38.8 26.5 %all-to-all-done.1 = bf16[8,12,4096]{2,1,0:T(8,128)(2,1)S(1)} async-done(((bf16[8,12,4096]{2,1,0:T(8,128)(2,1)}), bf16[8,12,4096]{2,1,0:T(8,128)(2,1)S(1)}, u32[]{:S(2)}, u32[]{:S(2)}) %all-to-all-start.1) | async-done | bytes 786464 | tf_op jit(solution)/shard_map/all_to_all | solution.py:26
  65.3 0.2 reshape.100
  65.5 1.9 %collective-permute-start = (bf16[96,4096]{1,0:T(8,128)(2,1)S(1)}, bf16[96,4096]{1,0:T(8,128)(2,1)}, u32[]{:S(2)}, u32[]{:S(2)}) collective-permute-start(bf16[96,4096]{1,0:T(8,128)(2,1)S(1)} %reshape.100), channel_id=1, source_target_pairs={{0,4},{4,0},{1,5},{5,1},{2,6},{6,2},{3,7},{7,3},{8,12},{12,8},{9,1... | collective-permute-start | bytes 2359304 | tf_op jit(solution)/shard_map/ppermute | solution.py:56
  67.4 0.0 copy-done.6
  67.5 0.1 copy.27
  67.6 0.1 reshape.98
  67.7 0.0 copy-done.4
  67.7 0.7 copy.28
  68.4 0.0 copy-done.5
  68.4 0.1 copy.29
  68.5 0.1 reshape.110
  68.6 2.5 %copy.30 = f32[128,3584]{0,1:T(8,128)} copy(bf16[128,3584]{1,0:T(8,128)(2,1)} %param.6) | data formatting | bytes 2752512 | tf_op jit(solution)/shard_map/convert_element_type | solution.py:62
  71.1 0.1 copy.31
  71.2 0.1 reshape.118
  71.3 2.6 %gather_fusion = bf16[168,128,64]{1,2,0:T(8,128)(2,1)} fusion(bf16[128,64,64]{0,2,1:T(8,128)(2,1)S(1)} %bitcast.69, s32[1024]{0:T(1024)S(1)} %pad_clamp_fusion.1), kind=kCustom, calls=%fused_computation | custom fusion | bytes 5505696 | tf_op jit(solution)/shard_map/gather | solution.py:60
  74.0 0.0 collective-permute-done
  74.0 1.2 pad_maximum_fusion
  75.2 2.6 %gather_fusion.1 = bf16[168,4096]{1,0:T(8,128)(2,1)} fusion(bf16[192,4096]{1,0:T(8,128)(2,1)S(1)} %pad_maximum_fusion, s32[1024]{0:T(1024)S(1)} %pad_clamp_fusion), kind=kCustom, calls=%fused_computation.1 | custom fusion | bytes 2753184 | tf_op jit(solution)/shard_map/gather | solution.py:58
  77.8 5.1 %reshape.101 = bf16[56,3,64,64]{3,2,1,0:T(8,128)(2,1)} reshape(bf16[168,4096]{1,0:T(8,128)(2,1)} %gather_fusion.1) | data formatting | bytes 2752512 | tf_op jit(solution)/shard_map/reshape | solution.py:58
  82.9 0.0 copy-done
  82.9 3.7 %fusion.14 = bf16[128,56,64,1]{0,2,3,1:T(8,128)(2,1)S(1)} fusion(f32[128,56,64]{0,2,1:T(8,128)} %bitcast.74, bf16[56,3,64,64]{3,2,1,0:T(8,128)(2,1)} %reshape.101, bf16[128,56,3,64]{0,3,2,1:T(8,128)(2,1)S(1)} %bitcast.70), kind=kOutput, calls=%fused_computation.19 | convolution fusion | flops 180289536 | bytes 6881280 | tf_op jit(solution)/shard_map/tcki,ckij->tcj/dot_general | solution.py:61
  86.7 0.0 copy-start.2
  86.7 0.9 copy-done.2
  87.6 3.3 %fusion.35 = f32[56,3,64,64]{3,2,1,0:T(8,128)} fusion(bf16[128,56,3,64]{0,3,2,1:T(8,128)(2,1)S(1)} %bitcast.71, bf16[128,56,64,1]{0,2,3,1:T(8,128)(2,1)S(1)} %fusion.14), kind=kOutput, calls=%fused_computation.64 | convolution fusion | flops 176160768 | bytes 6422528 | tf_op jit(solution)/shard_map/tcki,tcj->ckij/dot_general | solution.py:82
  90.9 4.2 %reshape.136 = f32[168,4096]{1,0:T(8,128)S(1)} reshape(f32[56,3,64,64]{3,2,1,0:T(8,128)} %fusion.35) | data formatting | bytes 5505024 | tf_op jit(solution)/shard_map/reshape | solution.py:83
  95.0 0.0 copy-start.3
  95.0 3.3 %scatter_custom_fusion.1 = f32[96,4096]{1,0:T(8,128)} fusion(s32[168]{0:T(256)S(1)} %bitcast.78, f32[168,4096]{1,0:T(8,128)S(1)} %reshape.136, f32[]{:T(128)} %constant.104.clone.1), kind=kCustom, calls=%fused_computation.20 | custom fusion | bytes 1572868 | tf_op jit(solution)/shard_map/scatter | solution.py:88
  98.3 2.6 %collective-permute-start.1 = (f32[96,4096]{1,0:T(8,128)}, f32[96,4096]{1,0:T(8,128)}, u32[]{:S(2)}, u32[]{:S(2)}) collective-permute-start(f32[96,4096]{1,0:T(8,128)} %scatter_custom_fusion.1), channel_id=1, source_target_pairs={{0,4},{4,0},{1,5},{5,1},{2,6},{6,2},{3,7},{7,3},{8,12},{12,8},{9,1... | collective-permute-start | bytes 4718600 | tf_op jit(solution)/shard_map/ppermute | solution.py:89
  100.9 0.0 copy-done.3
  100.9 3.7 %scatter_custom_fusion = f32[96,4096]{1,0:T(8,128)S(1)} fusion(s32[168]{0:T(256)S(1)} %bitcast.77, f32[168,4096]{1,0:T(8,128)} %copy-done.3, f32[]{:T(128)} %constant.104.clone.1), kind=kCustom, calls=%fused_computation.22 | custom fusion | bytes 1573376 | tf_op jit(solution)/shard_map/scatter | solution.py:90
  104.7 0.0 collective-permute-done.1
  104.7 1.6 add.134
  106.3 2.8 %reshape_reshape.3 = f32[8,1,49152]{2,1,0:T(1,128)} reshape(f32[96,4096]{1,0:T(8,128)S(1)} %add.134) | data formatting | bytes 3145728 | tf_op jit(solution)/shard_map/reshape;reshape | solution.py:31
  109.1 4.6 %all-to-all-start.2 = ((f32[8,1,49152]{2,1,0:T(1,128)}), f32[8,1,49152]{2,1,0:T(1,128)}, u32[]{:S(2)}, u32[]{:S(2)}) async-start(f32[8,1,49152]{2,1,0:T(1,128)} %reshape_reshape.3), calls=%async_computation.2 | async-start | bytes 3145728 | tf_op jit(solution)/shard_map/all_to_all | solution.py:32
  113.7 0.0 copy-done.1
  113.7 2.0 %convolution_bitcast_fusion = f32[128,56,3,64]{0,3,2,1:T(8,128)S(1)} fusion(bf16[56,3,64,64]{3,2,1,0:T(8,128)(2,1)S(1)} %copy-done.1, bf16[128,56,64,1]{0,2,3,1:T(8,128)(2,1)} %copy-done.2), kind=kOutput, calls=%fused_computation.6 | convolution fusion | flops 176160768 | bytes 7798784 | tf_op jit(solution)/shard_map/tcj,ckij->tcki/dot_general | solution.py:65
  115.7 5.7 %fusion.11 = bf16[128,64,64]{0,1,2:T(8,128)(2,1)S(1)} fusion(f32[128,56,3,64]{0,3,2,1:T(8,128)S(1)} %convolution_bitcast_fusion, s32[56,3]{0,1:T(4,128)S(1)} %copy-done.5), kind=kOutput, calls=%fused_computation.18 | convolution fusion | flops 1057499648 | bytes 6554272 | tf_op jit(solution)/shard_map/tcki,ckr->tri/dot_general | solution.py:69
  121.4 0.7 copy.34
  122.1 0.1 dynamic-slice_bitcast_fusion.2
  122.1 2.7 %collective-permute-start.4 = (bf16[128,1024]{0,1:T(8,128)(2,1)S(1)}, bf16[128,1024]{0,1:T(8,128)(2,1)S(1)}, u32[]{:S(2)}, u32[]{:S(2)}) collective-permute-start(bf16[128,1024]{0,1:T(8,128)(2,1)S(1)} %get-tuple-element.15), channel_id=1, source_target_pairs={{0,3},{1,0},{2,1},{3,2},{4,7},{5,4},{6,5},{7,6},{8,11},{9,8},{10,9... | collective-permute-start | bytes 786440 | tf_op jit(solution)/shard_map/ppermute | solution.py:79
  124.9 3.0 %collective-permute-start.3 = (bf16[128,1024]{0,1:T(8,128)(2,1)S(1)}, bf16[128,1024]{0,1:T(8,128)(2,1)S(1)}, u32[]{:S(2)}, u32[]{:S(2)}) collective-permute-start(bf16[128,1024]{0,1:T(8,128)(2,1)S(1)} %get-tuple-element.16), channel_id=1, source_target_pairs={{0,2},{1,3},{2,0},{3,1},{4,6},{5,7},{6,4},{7,5},{8,10},{9,11},{10,... | collective-permute-start | bytes 786440 | tf_op jit(solution)/shard_map/ppermute | solution.py:79
  127.9 4.0 %collective-permute-start.2 = (bf16[128,1024]{0,1:T(8,128)(2,1)S(1)}, bf16[128,1024]{0,1:T(8,128)(2,1)S(1)}, u32[]{:S(2)}, u32[]{:S(2)}) collective-permute-start(bf16[128,1024]{0,1:T(8,128)(2,1)S(1)} %get-tuple-element.14), channel_id=1, source_target_pairs={{0,1},{1,2},{2,3},{3,0},{4,5},{5,6},{6,7},{7,4},{8,9},{9,10},{10,1... | collective-permute-start | bytes 786440 | tf_op jit(solution)/shard_map/ppermute | solution.py:79
  131.9 7.2 %collective-permute-done.4 = bf16[128,1024]{0,1:T(8,128)(2,1)S(1)} collective-permute-done((bf16[128,1024]{0,1:T(8,128)(2,1)S(1)}, bf16[128,1024]{0,1:T(8,128)(2,1)S(1)}, u32[]{:S(2)}, u32[]{:S(2)}) %collective-permute-start.4) | collective-permute-done | bytes 262176 | tf_op jit(solution)/shard_map/ppermute | solution.py:79
  139.1 0.0 collective-permute-done.3
  139.1 2.5 %collective-permute-done.2 = bf16[128,1024]{0,1:T(8,128)(2,1)S(1)} collective-permute-done((bf16[128,1024]{0,1:T(8,128)(2,1)S(1)}, bf16[128,1024]{0,1:T(8,128)(2,1)S(1)}, u32[]{:S(2)}, u32[]{:S(2)}) %collective-permute-start.2) | collective-permute-done | bytes 262176 | tf_op jit(solution)/shard_map/ppermute | solution.py:79
  141.6 0.1 fusion.21
  141.8 12.3 %all-to-all-done.2 = f32[8,1,49152]{2,1,0:T(1,128)} async-done(((f32[8,1,49152]{2,1,0:T(1,128)}), f32[8,1,49152]{2,1,0:T(1,128)}, u32[]{:S(2)}, u32[]{:S(2)}) %all-to-all-start.2) | async-done | bytes 1572896 | tf_op jit(solution)/shard_map/all_to_all | solution.py:32
  154.0 2.6 %reduce_sum.18 = f32[49152]{0:T(1024)S(1)} reduce(f32[8,1,49152]{2,1,0:T(1,128)} %all-to-all-done.2, f32[]{:T(128)} %constant.104.clone.1), dimensions={0,1}, to_apply=%region_2.3 | reduce | flops 344064 | bytes 1769476 | tf_op jit(solution)/shard_map/reduce_sum | solution.py:33
  156.6 0.9 reshape.104
  157.5 3.5 %all-to-all-start.3 = ((f32[12,1,4096]{2,1,0:T(1,128)}), f32[12,1,4096]{2,1,0:T(1,128)S(1)}, u32[]{:S(2)}, u32[]{:S(2)}) async-start(f32[12,1,4096]{2,1,0:T(1,128)} %reshape.104), calls=%async_computation.3 | async-start | bytes 393216 | tf_op jit(solution)/shard_map/all_to_all | solution.py:32
  161.0 0.9 copy.35
  161.9 12.3 %all-to-all-done.3 = f32[12,1,4096]{2,1,0:T(1,128)S(1)} async-done(((f32[12,1,4096]{2,1,0:T(1,128)}), f32[12,1,4096]{2,1,0:T(1,128)S(1)}, u32[]{:S(2)}, u32[]{:S(2)}) %all-to-all-start.3) | async-done | bytes 196640 | tf_op jit(solution)/shard_map/all_to_all | solution.py:32
  174.2 0.7 reduce_sum.19
  (10 shorter events, 0.1 us)
Async XLA Ops:
  31.6 35.9 %copy-start.6 = (s32[56,3]{0,1:T(4,128)S(1)}, s32[56,3]{0,1:T(4,128)}, u32[]{:S(2)}) copy-start(s32[56,3]{0,1:T(4,128)} %param.9) | copy-start | bytes 2020
  31.6 36.2 %copy-start.4 = (bf16[128,4096]{1,0:T(8,128)(2,1)S(1)}, bf16[128,4096]{1,0:T(8,128)(2,1)}, u32[]{:S(2)}) copy-start(bf16[128,4096]{1,0:T(8,128)(2,1)} %param.5) | copy-start | bytes 3145732
  31.6 33.8 %all-to-all-start.1 = ((bf16[8,12,4096]{2,1,0:T(8,128)(2,1)}), bf16[8,12,4096]{2,1,0:T(8,128)(2,1)S(1)}, u32[]{:S(2)}, u32[]{:S(2)}) async-start(bf16[8,12,4096]{2,1,0:T(8,128)(2,1)} %broadcast_in_dim.32), calls=%async_computation.1 | async-start | bytes 2097152 | tf_op jit(solution)/shard_map/all_to_all | solution.py:26
  38.8 29.6 %copy-start.5 = (s32[56,3]{0,1:T(4,128)S(1)}, s32[56,3]{0,1:T(4,128)}, u32[]{:S(2)}) copy-start(s32[56,3]{0,1:T(4,128)} %param.8) | copy-start | bytes 2020
  65.5 8.4 %collective-permute-start = (bf16[96,4096]{1,0:T(8,128)(2,1)S(1)}, bf16[96,4096]{1,0:T(8,128)(2,1)}, u32[]{:S(2)}, u32[]{:S(2)}) collective-permute-start(bf16[96,4096]{1,0:T(8,128)(2,1)S(1)} %reshape.100), channel_id=1, source_target_pairs={{0,4},{4,0},{1,5},{5,1},{2,6},{6,2},{3,7},{7,3},{8,12},{12,8},{9,1... | collective-permute-start | bytes 2359304 | tf_op jit(solution)/shard_map/ppermute | solution.py:56
  77.8 5.1 %copy-start = (bf16[168,128,64]{1,2,0:T(8,128)(2,1)S(1)}, bf16[168,128,64]{1,2,0:T(8,128)(2,1)}, u32[]{:S(2)}) copy-start(bf16[168,128,64]{1,2,0:T(8,128)(2,1)} %gather_fusion) | copy-start | bytes 8257540
  86.7 0.9 copy-start.2
  95.0 5.9 %copy-start.3 = (f32[168,4096]{1,0:T(8,128)}, f32[168,4096]{1,0:T(8,128)S(1)}, u32[]{:S(2)}) copy-start(f32[168,4096]{1,0:T(8,128)S(1)} %reshape.136) | copy-start | bytes 8257540
  98.3 6.3 %collective-permute-start.1 = (f32[96,4096]{1,0:T(8,128)}, f32[96,4096]{1,0:T(8,128)}, u32[]{:S(2)}, u32[]{:S(2)}) collective-permute-start(f32[96,4096]{1,0:T(8,128)} %scatter_custom_fusion.1), channel_id=1, source_target_pairs={{0,4},{4,0},{1,5},{5,1},{2,6},{6,2},{3,7},{7,3},{8,12},{12,8},{9,1... | collective-permute-start | bytes 4718600 | tf_op jit(solution)/shard_map/ppermute | solution.py:89
  109.1 4.6 %copy-start.1 = (bf16[56,3,64,64]{3,2,1,0:T(8,128)(2,1)S(1)}, bf16[56,3,64,64]{3,2,1,0:T(8,128)(2,1)}, u32[]{:S(2)}) copy-start(bf16[56,3,64,64]{3,2,1,0:T(8,128)(2,1)} %reshape.101) | copy-start | bytes 4128772
  109.1 45.0 %all-to-all-start.2 = ((f32[8,1,49152]{2,1,0:T(1,128)}), f32[8,1,49152]{2,1,0:T(1,128)}, u32[]{:S(2)}, u32[]{:S(2)}) async-start(f32[8,1,49152]{2,1,0:T(1,128)} %reshape_reshape.3), calls=%async_computation.2 | async-start | bytes 3145728 | tf_op jit(solution)/shard_map/all_to_all | solution.py:32
  122.1 16.9 %collective-permute-start.4 = (bf16[128,1024]{0,1:T(8,128)(2,1)S(1)}, bf16[128,1024]{0,1:T(8,128)(2,1)S(1)}, u32[]{:S(2)}, u32[]{:S(2)}) collective-permute-start(bf16[128,1024]{0,1:T(8,128)(2,1)S(1)} %get-tuple-element.15), channel_id=1, source_target_pairs={{0,3},{1,0},{2,1},{3,2},{4,7},{5,4},{6,5},{7,6},{8,11},{9,8},{10,9... | collective-permute-start | bytes 786440 | tf_op jit(solution)/shard_map/ppermute | solution.py:79
  124.9 14.2 %collective-permute-start.3 = (bf16[128,1024]{0,1:T(8,128)(2,1)S(1)}, bf16[128,1024]{0,1:T(8,128)(2,1)S(1)}, u32[]{:S(2)}, u32[]{:S(2)}) collective-permute-start(bf16[128,1024]{0,1:T(8,128)(2,1)S(1)} %get-tuple-element.16), channel_id=1, source_target_pairs={{0,2},{1,3},{2,0},{3,1},{4,6},{5,7},{6,4},{7,5},{8,10},{9,11},{10,... | collective-permute-start | bytes 786440 | tf_op jit(solution)/shard_map/ppermute | solution.py:79
  127.9 13.7 %collective-permute-start.2 = (bf16[128,1024]{0,1:T(8,128)(2,1)S(1)}, bf16[128,1024]{0,1:T(8,128)(2,1)S(1)}, u32[]{:S(2)}, u32[]{:S(2)}) collective-permute-start(bf16[128,1024]{0,1:T(8,128)(2,1)S(1)} %get-tuple-element.14), channel_id=1, source_target_pairs={{0,1},{1,2},{2,3},{3,0},{4,5},{5,6},{6,7},{7,4},{8,9},{9,10},{10,1... | collective-permute-start | bytes 786440 | tf_op jit(solution)/shard_map/ppermute | solution.py:79
  157.5 16.7 %all-to-all-start.3 = ((f32[12,1,4096]{2,1,0:T(1,128)}), f32[12,1,4096]{2,1,0:T(1,128)S(1)}, u32[]{:S(2)}, u32[]{:S(2)}) async-start(f32[12,1,4096]{2,1,0:T(1,128)} %reshape.104), calls=%async_computation.3 | async-start | bytes 393216 | tf_op jit(solution)/shard_map/all_to_all | solution.py:32

commit v7 on v6

--- a/solution.py
+++ b/solution.py
@@ -53,13 +53,16 @@
         own = tile_store.reshape(cap, flat)
         row_z = gather_by_a2a(own, "z", nz)
         mine_tiles = gather_by_a2a(row_z, "y", ny)
+        input_blocks = inputs.reshape(tok_rows, row_count, TILE)
+        picked = input_blocks[:, tile_row]
+        upstream = d_hidden.reshape(tok_rows, per_slice, TILE).astype(jnp.float32)
+        mine_tiles, picked, upstream, rel_slot = lax.optimization_barrier(
+            (mine_tiles, picked, upstream, rel_slot)
+        )
         other_tiles = lax.ppermute(mine_tiles, "c", [(0, 1), (1, 0)])
         gathered = jnp.concatenate([mine_tiles, other_tiles], axis=0)
         kept_tiles = gathered[rel_slot].reshape(per_slice, keep_count, TILE, TILE)
-        input_blocks = inputs.reshape(tok_rows, row_count, TILE)
-        picked = input_blocks[:, tile_row]
         pre_act = jnp.einsum("tcki,ckij->tcj", picked, kept_tiles, preferred_element_type=jnp.float32)
-        upstream = d_hidden.reshape(tok_rows, per_slice, TILE).astype(jnp.float32)
         pre_grad = (upstream * silu_slope(pre_act)).astype(jnp.bfloat16)
         row_ids = jnp.arange(row_count, dtype=jnp.int32)
         back_all = jnp.einsum(

time: 176 us -> 172 us (0.977)
  waiting for transfers between devices: 60.8 us -> 57.1 us
    all_to_all x1, waiting for transfers between devices: 26.5 us -> 20.5 us  [gather_by_a2a(): got = lax.all_to_all(copies, name, 0, 0, tiled=True)]
    ppermute x1, waiting for transfers between devices: 0.01 us -> 1.89 us  [local(): other_tiles = lax.ppermute(mine_tiles, 'c', [(0, 1), (1, 0)])]
  transfers between devices with their start and end apart: 8 -> 8, of which waited for: 5 -> 6; matrix products, arithmetic and copies ran while one was open for 11% -> 11% of each run, Pallas kernels for 0% -> 0%
where the time goes in v7:
time: 172 us; the launch traced here: 171 us
  waiting for transfers between devices  57.1 us (33%)
  local copies, waits for them, and re-layouts  33.7 us (20%)
  starting transfers between devices  29.2 us (17%)
  blocking collectives  27.1 us (16%)
  matrix products  14.7 us (9%)
  other arithmetic  8.26 us (5%)
    all_to_all x1, blocking collectives, gather_by_a2a(): got = lax.all_to_all(copies, name, 0, 0, tiled=True)  27.1 us
    all_to_all x2, waiting for transfers between devices, reduce_by_a2a(): got = lax.all_to_all(parts, name, 0, 0, tiled=True)  24.6 us
    all_to_all x1, waiting for transfers between devices, gather_by_a2a(): got = lax.all_to_all(copies, name, 0, 0, tiled=True)  20.5 us
    ppermute x3, waiting for transfers between devices, local(): got = lax.ppermute(send, 'x', [(j, (j + shift) % nx) for j in range(nx)])  10.1 us
    ppermute x3, starting transfers between devices, local(): got = lax.ppermute(send, 'x', [(j, (j + shift) % nx) for j in range(nx)])  9.76 us
    all_to_all x2, starting transfers between devices, reduce_by_a2a(): got = lax.all_to_all(parts, name, 0, 0, tiled=True)  8.08 us
    all_to_all x1, starting transfers between devices, gather_by_a2a(): got = lax.all_to_all(copies, name, 0, 0, tiled=True)  7.23 us
    dot_general x1, matrix products, local(): jnp.einsum('tcki,ckr->tri', back_all, row_select, precision=lax.Precision...  5.67 us
  transfers between devices with their start and end apart: 8, of which 6 were waited for; matrix products, arithmetic and copies ran while one was open for 11% of the time, Pallas kernels for 0%

profile of v7, /device:TPU:6, one launch (start us, length us, event | category | flops | bytes accessed | tf_op | source)
XLA Modules:
  0.0 171.0 jit_solution(5907290177745948849)
XLA Ops:
  0.6 0.8 reduce.2
  1.4 0.1 broadcast_in_dim.29
  1.5 0.5 broadcast.142
  2.1 1.2 reduce.3
  3.3 0.1 reshape.154
  3.3 0.0 copy-start.4
  3.3 27.1 %all_to_all.20 = bf16[12,2,2048]{2,1,0:T(2,128)(2,1)S(1)} all-to-all(bf16[12,2,2048]{2,1,0:T(2,128)(2,1)S(1)} %reshape.154), channel_id=1, replica_groups=mesh['y'=8,'z'=12,'c'=2,'x'=4] {'z'}, dimensions={0} | all-to-all | bytes 196608 | tf_op jit(solution)/shard_map/all_to_all | solution.py:26
  30.4 0.1 reshape.155
  30.5 0.1 copy.48
  30.6 1.1 broadcast_in_dim.31
  31.7 7.2 %all-to-all-start.1 = ((bf16[8,12,4096]{2,1,0:T(8,128)(2,1)}), bf16[8,12,4096]{2,1,0:T(8,128)(2,1)S(1)}, u32[]{:S(2)}, u32[]{:S(2)}) async-start(bf16[8,12,4096]{2,1,0:T(8,128)(2,1)} %broadcast_in_dim.31), calls=%async_computation.1 | async-start | bytes 2097152 | tf_op jit(solution)/shard_map/all_to_all | solution.py:26
  38.9 0.0 copy-done.4
  38.9 0.7 copy.27
  39.6 0.0 copy-done.5
  39.6 0.1 copy.28
  39.7 0.1 reshape.110
  39.8 2.5 %copy.29 = f32[128,3584]{0,1:T(8,128)} copy(bf16[128,3584]{1,0:T(8,128)(2,1)} %param.6) | data formatting | bytes 2752512 | tf_op jit(solution)/shard_map/convert_element_type | solution.py:58
  42.3 2.6 %gather_fusion = bf16[168,128,64]{1,2,0:T(8,128)(2,1)} fusion(bf16[128,64,64]{0,2,1:T(8,128)(2,1)S(1)} %bitcast.69, s32[1024]{0:T(1024)S(1)} %pad_clamp_fusion.1), kind=kCustom, calls=%fused_computation | custom fusion | bytes 5505696 | tf_op jit(solution)/shard_map/gather | solution.py:57
  44.9 0.0 copy-done.6
  45.0 20.5 %all-to-all-done.1 = bf16[8,12,4096]{2,1,0:T(8,128)(2,1)S(1)} async-done(((bf16[8,12,4096]{2,1,0:T(8,128)(2,1)}), bf16[8,12,4096]{2,1,0:T(8,128)(2,1)S(1)}, u32[]{:S(2)}, u32[]{:S(2)}) %all-to-all-start.1) | async-done | bytes 786464 | tf_op jit(solution)/shard_map/all_to_all | solution.py:26
  65.5 0.2 reshape.98
  65.7 1.9 %collective-permute-start = (bf16[96,4096]{1,0:T(8,128)(2,1)S(1)}, bf16[96,4096]{1,0:T(8,128)(2,1)}, u32[]{:S(2)}, u32[]{:S(2)}) collective-permute-start(bf16[96,4096]{1,0:T(8,128)(2,1)S(1)} %reshape.98), channel_id=1, source_target_pairs={{0,4},{4,0},{1,5},{5,1},{2,6},{6,2},{3,7},{7,3},{8,12},{12,8},{9,1... | collective-permute-start | bytes 2359304 | tf_op jit(solution)/shard_map/ppermute | solution.py:62
  67.6 0.1 copy.30
  67.7 0.1 reshape.100
  67.8 0.1 copy.31
  67.9 0.1 reshape.118
  68.1 1.9 %collective-permute-done = bf16[96,4096]{1,0:T(8,128)(2,1)} collective-permute-done((bf16[96,4096]{1,0:T(8,128)(2,1)S(1)}, bf16[96,4096]{1,0:T(8,128)(2,1)}, u32[]{:S(2)}, u32[]{:S(2)}) %collective-permute-start) | collective-permute-done | bytes 786464 | tf_op jit(solution)/shard_map/ppermute | solution.py:62
  70.0 1.2 pad_maximum_fusion
  71.2 2.6 %gather_fusion.1 = bf16[168,4096]{1,0:T(8,128)(2,1)} fusion(bf16[192,4096]{1,0:T(8,128)(2,1)S(1)} %pad_maximum_fusion, s32[1024]{0:T(1024)S(1)} %pad_clamp_fusion), kind=kCustom, calls=%fused_computation.1 | custom fusion | bytes 2753184 | tf_op jit(solution)/shard_map/gather | solution.py:64
  73.8 5.2 %reshape.101 = bf16[56,3,64,64]{3,2,1,0:T(8,128)(2,1)} reshape(bf16[168,4096]{1,0:T(8,128)(2,1)} %gather_fusion.1) | data formatting | bytes 2752512 | tf_op jit(solution)/shard_map/reshape | solution.py:64
  78.9 0.0 copy-done
  78.9 3.7 %fusion.14 = bf16[128,56,64,1]{0,2,3,1:T(8,128)(2,1)S(1)} fusion(f32[128,56,64]{0,2,1:T(8,128)} %bitcast.74, bf16[56,3,64,64]{3,2,1,0:T(8,128)(2,1)} %reshape.101, bf16[128,56,3,64]{0,3,2,1:T(8,128)(2,1)S(1)} %bitcast.70), kind=kOutput, calls=%fused_computation.19 | convolution fusion | flops 180289536 | bytes 6881280 | tf_op jit(solution)/shard_map/tcki,ckij->tcj/dot_general | solution.py:65
  82.7 0.0 copy-start.2
  82.7 0.9 copy-done.2
  83.6 3.3 %fusion.34 = f32[56,3,64,64]{3,2,1,0:T(8,128)} fusion(bf16[128,56,3,64]{0,3,2,1:T(8,128)(2,1)S(1)} %bitcast.71, bf16[128,56,64,1]{0,2,3,1:T(8,128)(2,1)S(1)} %fusion.14), kind=kOutput, calls=%fused_computation.64 | convolution fusion | flops 176160768 | bytes 6422528 | tf_op jit(solution)/shard_map/tcki,tcj->ckij/dot_general | solution.py:85
  86.9 4.2 %reshape.136 = f32[168,4096]{1,0:T(8,128)S(1)} reshape(f32[56,3,64,64]{3,2,1,0:T(8,128)} %fusion.34) | data formatting | bytes 5505024 | tf_op jit(solution)/shard_map/reshape | solution.py:86
  91.0 0.0 copy-start.3
  91.0 3.3 %scatter_custom_fusion.1 = f32[96,4096]{1,0:T(8,128)} fusion(s32[168]{0:T(256)S(1)} %bitcast.78, f32[168,4096]{1,0:T(8,128)S(1)} %reshape.136, f32[]{:T(128)} %constant.104.clone.1), kind=kCustom, calls=%fused_computation.20 | custom fusion | bytes 1572868 | tf_op jit(solution)/shard_map/scatter | solution.py:91
  94.3 2.2 %collective-permute-start.1 = (f32[96,4096]{1,0:T(8,128)}, f32[96,4096]{1,0:T(8,128)}, u32[]{:S(2)}, u32[]{:S(2)}) collective-permute-start(f32[96,4096]{1,0:T(8,128)} %scatter_custom_fusion.1), channel_id=1, source_target_pairs={{0,4},{4,0},{1,5},{5,1},{2,6},{6,2},{3,7},{7,3},{8,12},{12,8},{9,1... | collective-permute-start | bytes 4718600 | tf_op jit(solution)/shard_map/ppermute | solution.py:92
  96.6 0.0 copy-done.3
  96.6 3.7 %scatter_custom_fusion = f32[96,4096]{1,0:T(8,128)S(1)} fusion(s32[168]{0:T(256)S(1)} %bitcast.77, f32[168,4096]{1,0:T(8,128)} %copy-done.3, f32[]{:T(128)} %constant.104.clone.1), kind=kCustom, calls=%fused_computation.22 | custom fusion | bytes 1573376 | tf_op jit(solution)/shard_map/scatter | solution.py:93
  100.3 0.0 collective-permute-done.1
  100.3 1.6 add.134
  101.9 2.8 %reshape_reshape.3 = f32[8,1,49152]{2,1,0:T(1,128)} reshape(f32[96,4096]{1,0:T(8,128)S(1)} %add.134) | data formatting | bytes 3145728 | tf_op jit(solution)/shard_map/reshape;reshape | solution.py:31
  104.7 4.6 %all-to-all-start.2 = ((f32[8,1,49152]{2,1,0:T(1,128)}), f32[8,1,49152]{2,1,0:T(1,128)}, u32[]{:S(2)}, u32[]{:S(2)}) async-start(f32[8,1,49152]{2,1,0:T(1,128)} %reshape_reshape.3), calls=%async_computation.2 | async-start | bytes 3145728 | tf_op jit(solution)/shard_map/all_to_all | solution.py:32
  109.3 0.0 copy-done.1
  109.3 2.0 %convolution_bitcast_fusion = f32[128,56,3,64]{0,3,2,1:T(8,128)S(1)} fusion(bf16[56,3,64,64]{3,2,1,0:T(8,128)(2,1)S(1)} %copy-done.1, bf16[128,56,64,1]{0,2,3,1:T(8,128)(2,1)} %copy-done.2), kind=kOutput, calls=%fused_computation.6 | convolution fusion | flops 176160768 | bytes 7798784 | tf_op jit(solution)/shard_map/tcj,ckij->tcki/dot_general | solution.py:68
  111.4 5.7 %fusion.11 = bf16[128,64,64]{0,1,2:T(8,128)(2,1)S(1)} fusion(f32[128,56,3,64]{0,3,2,1:T(8,128)S(1)} %convolution_bitcast_fusion, s32[56,3]{0,1:T(4,128)S(1)} %copy-done.5), kind=kOutput, calls=%fused_computation.18 | convolution fusion | flops 1057499648 | bytes 6554272 | tf_op jit(solution)/shard_map/tcki,ckr->tri/dot_general | solution.py:72
  117.0 0.7 copy.34
  117.7 0.1 dynamic-slice_bitcast_fusion.2
  117.8 2.7 %collective-permute-start.4 = (bf16[128,1024]{0,1:T(8,128)(2,1)S(1)}, bf16[128,1024]{0,1:T(8,128)(2,1)S(1)}, u32[]{:S(2)}, u32[]{:S(2)}) collective-permute-start(bf16[128,1024]{0,1:T(8,128)(2,1)S(1)} %get-tuple-element.21), channel_id=1, source_target_pairs={{0,3},{1,0},{2,1},{3,2},{4,7},{5,4},{6,5},{7,6},{8,11},{9,8},{10,9... | collective-permute-start | bytes 786440 | tf_op jit(solution)/shard_map/ppermute | solution.py:82
  120.5 3.0 %collective-permute-start.3 = (bf16[128,1024]{0,1:T(8,128)(2,1)S(1)}, bf16[128,1024]{0,1:T(8,128)(2,1)S(1)}, u32[]{:S(2)}, u32[]{:S(2)}) collective-permute-start(bf16[128,1024]{0,1:T(8,128)(2,1)S(1)} %get-tuple-element.22), channel_id=1, source_target_pairs={{0,2},{1,3},{2,0},{3,1},{4,6},{5,7},{6,4},{7,5},{8,10},{9,11},{10,... | collective-permute-start | bytes 786440 | tf_op jit(solution)/shard_map/ppermute | solution.py:82
  123.6 4.0 %collective-permute-start.2 = (bf16[128,1024]{0,1:T(8,128)(2,1)S(1)}, bf16[128,1024]{0,1:T(8,128)(2,1)S(1)}, u32[]{:S(2)}, u32[]{:S(2)}) collective-permute-start(bf16[128,1024]{0,1:T(8,128)(2,1)S(1)} %get-tuple-element.20), channel_id=1, source_target_pairs={{0,1},{1,2},{2,3},{3,0},{4,5},{5,6},{6,7},{7,4},{8,9},{9,10},{10,1... | collective-permute-start | bytes 786440 | tf_op jit(solution)/shard_map/ppermute | solution.py:82
  127.6 7.5 %collective-permute-done.4 = bf16[128,1024]{0,1:T(8,128)(2,1)S(1)} collective-permute-done((bf16[128,1024]{0,1:T(8,128)(2,1)S(1)}, bf16[128,1024]{0,1:T(8,128)(2,1)S(1)}, u32[]{:S(2)}, u32[]{:S(2)}) %collective-permute-start.4) | collective-permute-done | bytes 262176 | tf_op jit(solution)/shard_map/ppermute | solution.py:82
  135.1 0.0 collective-permute-done.3
  135.1 2.5 %collective-permute-done.2 = bf16[128,1024]{0,1:T(8,128)(2,1)S(1)} collective-permute-done((bf16[128,1024]{0,1:T(8,128)(2,1)S(1)}, bf16[128,1024]{0,1:T(8,128)(2,1)S(1)}, u32[]{:S(2)}, u32[]{:S(2)}) %collective-permute-start.2) | collective-permute-done | bytes 262176 | tf_op jit(solution)/shard_map/ppermute | solution.py:82
  137.6 0.1 fusion.21
  137.8 12.3 %all-to-all-done.2 = f32[8,1,49152]{2,1,0:T(1,128)} async-done(((f32[8,1,49152]{2,1,0:T(1,128)}), f32[8,1,49152]{2,1,0:T(1,128)}, u32[]{:S(2)}, u32[]{:S(2)}) %all-to-all-start.2) | async-done | bytes 1572896 | tf_op jit(solution)/shard_map/all_to_all | solution.py:32
  150.1 2.6 %reduce_sum.18 = f32[49152]{0:T(1024)S(1)} reduce(f32[8,1,49152]{2,1,0:T(1,128)} %all-to-all-done.2, f32[]{:T(128)} %constant.104.clone.1), dimensions={0,1}, to_apply=%region_2.3 | reduce | flops 344064 | bytes 1769476 | tf_op jit(solution)/shard_map/reduce_sum | solution.py:33
  152.6 0.9 reshape.104
  153.5 3.5 %all-to-all-start.3 = ((f32[12,1,4096]{2,1,0:T(1,128)}), f32[12,1,4096]{2,1,0:T(1,128)S(1)}, u32[]{:S(2)}, u32[]{:S(2)}) async-start(f32[12,1,4096]{2,1,0:T(1,128)} %reshape.104), calls=%async_computation.3 | async-start | bytes 393216 | tf_op jit(solution)/shard_map/all_to_all | solution.py:32
  157.0 0.9 copy.35
  157.9 12.3 %all-to-all-done.3 = f32[12,1,4096]{2,1,0:T(1,128)S(1)} async-done(((f32[12,1,4096]{2,1,0:T(1,128)}), f32[12,1,4096]{2,1,0:T(1,128)S(1)}, u32[]{:S(2)}, u32[]{:S(2)}) %all-to-all-start.3) | async-done | bytes 196640 | tf_op jit(solution)/shard_map/all_to_all | solution.py:32
  170.2 0.7 reduce_sum.19
  (11 shorter events, 0.1 us)
Async XLA Ops:
  3.3 35.6 %copy-start.4 = (bf16[128,4096]{1,0:T(8,128)(2,1)S(1)}, bf16[128,4096]{1,0:T(8,128)(2,1)}, u32[]{:S(2)}) copy-start(bf16[128,4096]{1,0:T(8,128)(2,1)} %param.5) | copy-start | bytes 3145732
  31.7 7.9 %copy-start.5 = (s32[56,3]{0,1:T(4,128)S(1)}, s32[56,3]{0,1:T(4,128)}, u32[]{:S(2)}) copy-start(s32[56,3]{0,1:T(4,128)} %param.8) | copy-start | bytes 2020
  31.7 33.8 %all-to-all-start.1 = ((bf16[8,12,4096]{2,1,0:T(8,128)(2,1)}), bf16[8,12,4096]{2,1,0:T(8,128)(2,1)S(1)}, u32[]{:S(2)}, u32[]{:S(2)}) async-start(bf16[8,12,4096]{2,1,0:T(8,128)(2,1)} %broadcast_in_dim.31), calls=%async_computation.1 | async-start | bytes 2097152 | tf_op jit(solution)/shard_map/all_to_all | solution.py:26
  42.3 2.6 %copy-start.6 = (s32[56,3]{0,1:T(4,128)S(1)}, s32[56,3]{0,1:T(4,128)}, u32[]{:S(2)}) copy-start(s32[56,3]{0,1:T(4,128)} %param.9) | copy-start | bytes 2020
  65.7 4.3 %collective-permute-start = (bf16[96,4096]{1,0:T(8,128)(2,1)S(1)}, bf16[96,4096]{1,0:T(8,128)(2,1)}, u32[]{:S(2)}, u32[]{:S(2)}) collective-permute-start(bf16[96,4096]{1,0:T(8,128)(2,1)S(1)} %reshape.98), channel_id=1, source_target_pairs={{0,4},{4,0},{1,5},{5,1},{2,6},{6,2},{3,7},{7,3},{8,12},{12,8},{9,1... | collective-permute-start | bytes 2359304 | tf_op jit(solution)/shard_map/ppermute | solution.py:62
  73.8 5.2 %copy-start = (bf16[168,128,64]{1,2,0:T(8,128)(2,1)S(1)}, bf16[168,128,64]{1,2,0:T(8,128)(2,1)}, u32[]{:S(2)}) copy-start(bf16[168,128,64]{1,2,0:T(8,128)(2,1)} %gather_fusion) | copy-start | bytes 8257540
  82.7 0.9 copy-start.2
  91.0 5.5 %copy-start.3 = (f32[168,4096]{1,0:T(8,128)}, f32[168,4096]{1,0:T(8,128)S(1)}, u32[]{:S(2)}) copy-start(f32[168,4096]{1,0:T(8,128)S(1)} %reshape.136) | copy-start | bytes 8257540
  94.3 6.0 %collective-permute-start.1 = (f32[96,4096]{1,0:T(8,128)}, f32[96,4096]{1,0:T(8,128)}, u32[]{:S(2)}, u32[]{:S(2)}) collective-permute-start(f32[96,4096]{1,0:T(8,128)} %scatter_custom_fusion.1), channel_id=1, source_target_pairs={{0,4},{4,0},{1,5},{5,1},{2,6},{6,2},{3,7},{7,3},{8,12},{12,8},{9,1... | collective-permute-start | bytes 4718600 | tf_op jit(solution)/shard_map/ppermute | solution.py:92
  104.7 4.6 %copy-start.1 = (bf16[56,3,64,64]{3,2,1,0:T(8,128)(2,1)S(1)}, bf16[56,3,64,64]{3,2,1,0:T(8,128)(2,1)}, u32[]{:S(2)}) copy-start(bf16[56,3,64,64]{3,2,1,0:T(8,128)(2,1)} %reshape.101) | copy-start | bytes 4128772
  104.7 45.3 %all-to-all-start.2 = ((f32[8,1,49152]{2,1,0:T(1,128)}), f32[8,1,49152]{2,1,0:T(1,128)}, u32[]{:S(2)}, u32[]{:S(2)}) async-start(f32[8,1,49152]{2,1,0:T(1,128)} %reshape_reshape.3), calls=%async_computation.2 | async-start | bytes 3145728 | tf_op jit(solution)/shard_map/all_to_all | solution.py:32
  117.8 17.3 %collective-permute-start.4 = (bf16[128,1024]{0,1:T(8,128)(2,1)S(1)}, bf16[128,1024]{0,1:T(8,128)(2,1)S(1)}, u32[]{:S(2)}, u32[]{:S(2)}) collective-permute-start(bf16[128,1024]{0,1:T(8,128)(2,1)S(1)} %get-tuple-element.21), channel_id=1, source_target_pairs={{0,3},{1,0},{2,1},{3,2},{4,7},{5,4},{6,5},{7,6},{8,11},{9,8},{10,9... | collective-permute-start | bytes 786440 | tf_op jit(solution)/shard_map/ppermute | solution.py:82
  120.5 14.6 %collective-permute-start.3 = (bf16[128,1024]{0,1:T(8,128)(2,1)S(1)}, bf16[128,1024]{0,1:T(8,128)(2,1)S(1)}, u32[]{:S(2)}, u32[]{:S(2)}) collective-permute-start(bf16[128,1024]{0,1:T(8,128)(2,1)S(1)} %get-tuple-element.22), channel_id=1, source_target_pairs={{0,2},{1,3},{2,0},{3,1},{4,6},{5,7},{6,4},{7,5},{8,10},{9,11},{10,... | collective-permute-start | bytes 786440 | tf_op jit(solution)/shard_map/ppermute | solution.py:82
  123.6 14.1 %collective-permute-start.2 = (bf16[128,1024]{0,1:T(8,128)(2,1)S(1)}, bf16[128,1024]{0,1:T(8,128)(2,1)S(1)}, u32[]{:S(2)}, u32[]{:S(2)}) collective-permute-start(bf16[128,1024]{0,1:T(8,128)(2,1)S(1)} %get-tuple-element.20), channel_id=1, source_target_pairs={{0,1},{1,2},{2,3},{3,0},{4,5},{5,6},{6,7},{7,4},{8,9},{9,10},{10,1... | collective-permute-start | bytes 786440 | tf_op jit(solution)/shard_map/ppermute | solution.py:82
  153.5 16.7 %all-to-all-start.3 = ((f32[12,1,4096]{2,1,0:T(1,128)}), f32[12,1,4096]{2,1,0:T(1,128)S(1)}, u32[]{:S(2)}, u32[]{:S(2)}) async-start(f32[12,1,4096]{2,1,0:T(1,128)} %reshape.104), calls=%async_computation.3 | async-start | bytes 393216 | tf_op jit(solution)/shard_map/all_to_all | solution.py:32

commit v8 on v7

--- a/solution.py
+++ b/solution.py
@@ -60,8 +60,11 @@
             (mine_tiles, picked, upstream, rel_slot)
         )
         other_tiles = lax.ppermute(mine_tiles, "c", [(0, 1), (1, 0)])
-        gathered = jnp.concatenate([mine_tiles, other_tiles], axis=0)
-        kept_tiles = gathered[rel_slot].reshape(per_slice, keep_count, TILE, TILE)
+        local_slot = rel_slot % half
+        from_mine = mine_tiles[local_slot]
+        from_other = other_tiles[local_slot]
+        picked_tiles = jnp.where((rel_slot < half)[..., None], from_mine, from_other)
+        kept_tiles = picked_tiles.reshape(per_slice, keep_count, TILE, TILE)
         pre_act = jnp.einsum("tcki,ckij->tcj", picked, kept_tiles, preferred_element_type=jnp.float32)
         pre_grad = (upstream * silu_slope(pre_act)).astype(jnp.bfloat16)
         row_ids = jnp.arange(row_count, dtype=jnp.int32)

time: 172 us -> 178 us (1.035)
  local copies, waits for them, and re-layouts: 33.7 us -> 40.6 us
  waiting for transfers between devices: 57.1 us -> 53.8 us
  matrix products: 14.7 us -> 16.8 us
    gather x1 -> x4, local copies, waits for them, and re-layouts: 2.56 us -> 13 us  [the longest x2 7.65 us: local(): from_other = other_tiles[local_slot]]
    reshape x1 -> x0, local copies, waits for them, and re-layouts: 5.15 us -> none  [local(): kept_tiles = gathered[rel_slot].reshape(per_slice, keep_count, TILE, TILE)]
    ppermute x1, waiting for transfers between devices: 1.89 us -> 0.01 us  [local(): other_tiles = lax.ppermute(mine_tiles, 'c', [(0, 1), (1, 0)])]
  transfers between devices with their start and end apart: 8 -> 8, of which waited for: 6 -> 5; matrix products, arithmetic and copies ran while one was open for 11% -> 15% of each run, Pallas kernels for 0% -> 0%
where the time goes in v8:
time: 178 us; the launch traced here: 177 us
  waiting for transfers between devices  53.8 us (30%)
  local copies, waits for them, and re-layouts  40.6 us (23%)
  starting transfers between devices  29.2 us (16%)
  blocking collectives  26.9 us (15%)
  matrix products  16.8 us (9%)
  other arithmetic  8.37 us (5%)
    all_to_all x1, blocking collectives, gather_by_a2a(): got = lax.all_to_all(copies, name, 0, 0, tiled=True)  26.9 us
    all_to_all x2, waiting for transfers between devices, reduce_by_a2a(): got = lax.all_to_all(parts, name, 0, 0, tiled=True)  23.6 us
    all_to_all x1, waiting for transfers between devices, gather_by_a2a(): got = lax.all_to_all(copies, name, 0, 0, tiled=True)  20.5 us
    ppermute x3, starting transfers between devices, local(): got = lax.ppermute(send, 'x', [(j, (j + shift) % nx) for j in range(nx)])  9.76 us
    ppermute x3, waiting for transfers between devices, local(): got = lax.ppermute(send, 'x', [(j, (j + shift) % nx) for j in range(nx)])  9.7 us
    all_to_all x2, starting transfers between devices, reduce_by_a2a(): got = lax.all_to_all(parts, name, 0, 0, tiled=True)  7.82 us
    gather x2, local copies, waits for them, and re-layouts, local(): from_other = other_tiles[local_slot]  7.65 us
    all_to_all x1, starting transfers between devices, gather_by_a2a(): got = lax.all_to_all(copies, name, 0, 0, tiled=True)  7.1 us
  transfers between devices with their start and end apart: 8, of which 5 were waited for; matrix products, arithmetic and copies ran while one was open for 15% of the time, Pallas kernels for 0%

profile of v8, /device:TPU:6, one launch (start us, length us, event | category | flops | bytes accessed | tf_op | source)
XLA Modules:
  0.0 176.7 jit_solution(9052405838654276851)
XLA Ops:
  0.6 0.0 copy-start.4
  0.6 0.9 reduce.2
  1.5 0.1 broadcast_in_dim.39
  1.6 0.5 broadcast.153
  2.1 1.2 reduce.3
  3.4 0.1 reshape.165
  3.4 26.9 %all_to_all.20 = bf16[12,2,2048]{2,1,0:T(2,128)(2,1)S(1)} all-to-all(bf16[12,2,2048]{2,1,0:T(2,128)(2,1)S(1)} %reshape.165), channel_id=1, replica_groups=mesh['y'=8,'z'=12,'c'=2,'x'=4] {'z'}, dimensions={0} | all-to-all | bytes 196608 | tf_op jit(solution)/shard_map/all_to_all | solution.py:26
  30.4 0.1 reshape.166
  30.4 0.1 copy.54
  30.6 0.0 copy-start.5
  30.6 1.1 broadcast_in_dim.41
  31.7 7.1 %all-to-all-start.1 = ((bf16[8,12,4096]{2,1,0:T(8,128)(2,1)}), bf16[8,12,4096]{2,1,0:T(8,128)(2,1)S(1)}, u32[]{:S(2)}, u32[]{:S(2)}) async-start(bf16[8,12,4096]{2,1,0:T(8,128)(2,1)} %broadcast_in_dim.41), calls=%async_computation.1 | async-start | bytes 2097152 | tf_op jit(solution)/shard_map/all_to_all | solution.py:26
  38.8 0.0 copy-done.4
  38.8 0.7 copy.32
  39.4 0.0 copy-done.5
  39.4 0.1 copy.33
  39.5 0.1 reshape.110
  39.7 2.5 %copy.34 = f32[128,3584]{0,1:T(8,128)} copy(bf16[128,3584]{1,0:T(8,128)(2,1)} %param.6) | data formatting | bytes 2752512 | tf_op jit(solution)/shard_map/convert_element_type | solution.py:58
  42.2 2.6 %gather_fusion = bf16[168,128,64]{1,2,0:T(8,128)(2,1)} fusion(bf16[128,64,64]{0,2,1:T(8,128)(2,1)S(1)} %bitcast.67, s32[1024]{0:T(1024)S(1)} %pad_clamp_fusion.1), kind=kCustom, calls=%fused_computation | custom fusion | bytes 5505696 | tf_op jit(solution)/shard_map/gather | solution.py:57
  44.8 0.0 copy-done.6
  44.8 20.5 %all-to-all-done.1 = bf16[8,12,4096]{2,1,0:T(8,128)(2,1)S(1)} async-done(((bf16[8,12,4096]{2,1,0:T(8,128)(2,1)}), bf16[8,12,4096]{2,1,0:T(8,128)(2,1)S(1)}, u32[]{:S(2)}, u32[]{:S(2)}) %all-to-all-start.1) | async-done | bytes 786464 | tf_op jit(solution)/shard_map/all_to_all | solution.py:26
  65.3 0.2 reshape.99
  65.5 2.1 %collective-permute-start = (bf16[96,4096]{1,0:T(8,128)(2,1)S(1)}, bf16[96,4096]{1,0:T(8,128)(2,1)S(1)}, u32[]{:S(2)}, u32[]{:S(2)}) collective-permute-start(bf16[96,4096]{1,0:T(8,128)(2,1)S(1)} %reshape.99), channel_id=1, source_target_pairs={{0,4},{4,0},{1,5},{5,1},{2,6},{6,2},{3,7},{7,3},{8,12},{12,8},{9,1... | collective-permute-start | bytes 2359304 | tf_op jit(solution)/shard_map/ppermute | solution.py:62
  67.6 0.1 copy.35
  67.7 0.1 reshape.101
  67.8 0.1 copy.37
  67.9 0.1 reshape.118
  68.1 1.4 gather_fusion.1
  69.5 4.0 %gather.15 = bf16[56,3,64,64]{3,2,1,0:T(8,128)(2,1)} reshape(bf16[168,4096]{1,0:T(8,128)(2,1)S(1)} %gather_fusion.1) | data formatting | bytes 2752512 | tf_op jit(solution)/shard_map/gather | solution.py:64
  73.4 0.1 copy.36
  73.6 0.0 collective-permute-done
  73.6 2.5 %gather_fusion.2 = bf16[168,4096]{1,0:T(8,128)(2,1)} fusion(bf16[96,4096]{1,0:T(8,128)(2,1)S(1)} %collective-permute-done, s32[1024]{0:T(1024)S(1)} %pad_clamp_fusion), kind=kCustom, calls=%fused_computation.2 | custom fusion | bytes 2753184 | tf_op jit(solution)/shard_map/gather | solution.py:65
  76.1 5.1 %gather.17 = bf16[56,3,64,64]{3,2,1,0:T(8,128)(2,1)} reshape(bf16[168,4096]{1,0:T(8,128)(2,1)} %gather_fusion.2) | data formatting | bytes 2752512 | tf_op jit(solution)/shard_map/gather | solution.py:65
  81.2 0.0 copy-done
  81.2 4.9 %fusion.14 = bf16[128,56,64,1]{0,2,3,1:T(8,128)(2,1)S(1)} fusion(f32[128,56,64]{0,2,1:T(8,128)} %bitcast.72, bf16[128,56,3,64]{0,3,2,1:T(8,128)(2,1)S(1)} %bitcast.68, bf16[56,3,64,64]{3,2,1,0:T(8,128)(2,1)} %gather.15, bf16[56,3,64,64]{3,2,1,0:T(8,128)(2,1)} %gather.17, pred[56,3]{1,0:T(8,128)(4,1)S(1)} %copy.36), kind=kOutput, calls=%fused_computation.20 | convolution fusion | flops 180977664 | bytes 8257704 | tf_op jit(solution)/shard_map/tcki,ckij->tcj/dot_general | solution.py:68
  86.1 0.9 copy-done.2
  87.0 3.3 %fusion.34 = f32[56,3,64,64]{3,2,1,0:T(8,128)} fusion(bf16[128,56,3,64]{0,3,2,1:T(8,128)(2,1)S(1)} %bitcast.69, bf16[128,56,64,1]{0,2,3,1:T(8,128)(2,1)S(1)} %fusion.14), kind=kOutput, calls=%fused_computation.67 | convolution fusion | flops 176160768 | bytes 6422528 | tf_op jit(solution)/shard_map/tcki,tcj->ckij/dot_general | solution.py:88
  90.4 4.2 %reshape.144 = f32[168,4096]{1,0:T(8,128)S(1)} reshape(f32[56,3,64,64]{3,2,1,0:T(8,128)} %fusion.34) | data formatting | bytes 5505024 | tf_op jit(solution)/shard_map/reshape | solution.py:89
  94.5 3.3 %scatter_custom_fusion.1 = f32[96,4096]{1,0:T(8,128)} fusion(s32[168]{0:T(256)S(1)} %bitcast.76, f32[168,4096]{1,0:T(8,128)S(1)} %reshape.144, f32[]{:T(128)} %constant.110.clone.1), kind=kCustom, calls=%fused_computation.21 | custom fusion | bytes 1572868 | tf_op jit(solution)/shard_map/scatter | solution.py:94
  97.8 2.4 %collective-permute-start.1 = (f32[96,4096]{1,0:T(8,128)}, f32[96,4096]{1,0:T(8,128)}, u32[]{:S(2)}, u32[]{:S(2)}) collective-permute-start(f32[96,4096]{1,0:T(8,128)} %scatter_custom_fusion.1), channel_id=1, source_target_pairs={{0,4},{4,0},{1,5},{5,1},{2,6},{6,2},{3,7},{7,3},{8,12},{12,8},{9,1... | collective-permute-start | bytes 4718600 | tf_op jit(solution)/shard_map/ppermute | solution.py:95
  100.2 4.0 %scatter_custom_fusion = f32[96,4096]{1,0:T(8,128)S(1)} fusion(s32[168]{0:T(256)S(1)} %bitcast.75, f32[168,4096]{1,0:T(8,128)} %copy-done.3, f32[]{:T(128)} %constant.110.clone.1), kind=kCustom, calls=%fused_computation.23 | custom fusion | bytes 1573376 | tf_op jit(solution)/shard_map/scatter | solution.py:96
  104.2 0.0 collective-permute-done.1
  104.2 2.8 %add.136 = f32[96,4096]{1,0:T(8,128)} add(f32[96,4096]{1,0:T(8,128)S(1)} %scatter_custom_fusion, f32[96,4096]{1,0:T(8,128)} %collective-permute-done.1) | non-fusion elementwise | flops 393216 | bytes 4718592 | tf_op jit(solution)/shard_map/add | solution.py:97
  107.0 4.1 %reshape_reshape.3 = f32[8,1,49152]{2,1,0:T(1,128)} reshape(f32[96,4096]{1,0:T(8,128)} %add.136) | data formatting | bytes 3145728 | tf_op jit(solution)/shard_map/reshape;reshape | solution.py:31
  111.1 4.3 %all-to-all-start.2 = ((f32[8,1,49152]{2,1,0:T(1,128)}), f32[8,1,49152]{2,1,0:T(1,128)}, u32[]{:S(2)}, u32[]{:S(2)}) async-start(f32[8,1,49152]{2,1,0:T(1,128)} %reshape_reshape.3), calls=%async_computation.2 | async-start | bytes 3145728 | tf_op jit(solution)/shard_map/all_to_all | solution.py:32
  115.4 0.0 copy-done.1
  115.4 2.9 %convolution_bitcast_fusion = f32[128,56,3,64]{0,3,2,1:T(8,128)S(1)} fusion(bf16[128,56,64,1]{0,2,3,1:T(8,128)(2,1)} %copy-done.2, bf16[56,3,64,64]{3,2,1,0:T(8,128)(2,1)S(1)} %copy-done.1, bf16[56,3,64,64]{3,2,1,0:T(8,128)(2,1)} %gather.17, pred[56,3]{1,0:T(8,128)(4,1)S(1)} %copy.36), kind=kOutput, calls=%fused_computation.8 | convolution fusion | flops 176848896 | bytes 9175208 | tf_op jit(solution)/shard_map/tcj,ckij->tcki/dot_general | solution.py:71
  118.4 5.7 %fusion.11 = bf16[128,64,64]{0,1,2:T(8,128)(2,1)S(1)} fusion(f32[128,56,3,64]{0,3,2,1:T(8,128)S(1)} %convolution_bitcast_fusion, s32[56,3]{0,1:T(4,128)S(1)} %copy-done.5), kind=kOutput, calls=%fused_computation.19 | convolution fusion | flops 1057499648 | bytes 6554272 | tf_op jit(solution)/shard_map/tcki,ckr->tri/dot_general | solution.py:75
  124.0 0.7 copy.40
  124.7 0.1 dynamic-slice_bitcast_fusion.2
  124.8 2.7 %collective-permute-start.4 = (bf16[128,1024]{0,1:T(8,128)(2,1)S(1)}, bf16[128,1024]{0,1:T(8,128)(2,1)S(1)}, u32[]{:S(2)}, u32[]{:S(2)}) collective-permute-start(bf16[128,1024]{0,1:T(8,128)(2,1)S(1)} %get-tuple-element.21), channel_id=1, source_target_pairs={{0,3},{1,0},{2,1},{3,2},{4,7},{5,4},{6,5},{7,6},{8,11},{9,8},{10,9... | collective-permute-start | bytes 786440 | tf_op jit(solution)/shard_map/ppermute | solution.py:85
  127.5 3.0 %collective-permute-start.3 = (bf16[128,1024]{0,1:T(8,128)(2,1)S(1)}, bf16[128,1024]{0,1:T(8,128)(2,1)S(1)}, u32[]{:S(2)}, u32[]{:S(2)}) collective-permute-start(bf16[128,1024]{0,1:T(8,128)(2,1)S(1)} %get-tuple-element.22), channel_id=1, source_target_pairs={{0,2},{1,3},{2,0},{3,1},{4,6},{5,7},{6,4},{7,5},{8,10},{9,11},{10,... | collective-permute-start | bytes 786440 | tf_op jit(solution)/shard_map/ppermute | solution.py:85
  130.6 4.0 %collective-permute-start.2 = (bf16[128,1024]{0,1:T(8,128)(2,1)S(1)}, bf16[128,1024]{0,1:T(8,128)(2,1)S(1)}, u32[]{:S(2)}, u32[]{:S(2)}) collective-permute-start(bf16[128,1024]{0,1:T(8,128)(2,1)S(1)} %get-tuple-element.20), channel_id=1, source_target_pairs={{0,1},{1,2},{2,3},{3,0},{4,5},{5,6},{6,7},{7,4},{8,9},{9,10},{10,1... | collective-permute-start | bytes 786440 | tf_op jit(solution)/shard_map/ppermute | solution.py:85
  134.6 7.2 %collective-permute-done.4 = bf16[128,1024]{0,1:T(8,128)(2,1)S(1)} collective-permute-done((bf16[128,1024]{0,1:T(8,128)(2,1)S(1)}, bf16[128,1024]{0,1:T(8,128)(2,1)S(1)}, u32[]{:S(2)}, u32[]{:S(2)}) %collective-permute-start.4) | collective-permute-done | bytes 262176 | tf_op jit(solution)/shard_map/ppermute | solution.py:85
  141.8 0.0 collective-permute-done.3
  141.8 2.5 %collective-permute-done.2 = bf16[128,1024]{0,1:T(8,128)(2,1)S(1)} collective-permute-done((bf16[128,1024]{0,1:T(8,128)(2,1)S(1)}, bf16[128,1024]{0,1:T(8,128)(2,1)S(1)}, u32[]{:S(2)}, u32[]{:S(2)}) %collective-permute-start.2) | collective-permute-done | bytes 262176 | tf_op jit(solution)/shard_map/ppermute | solution.py:85
  144.3 0.1 fusion.21
  144.4 11.3 %all-to-all-done.2 = f32[8,1,49152]{2,1,0:T(1,128)} async-done(((f32[8,1,49152]{2,1,0:T(1,128)}), f32[8,1,49152]{2,1,0:T(1,128)}, u32[]{:S(2)}, u32[]{:S(2)}) %all-to-all-start.2) | async-done | bytes 1572896 | tf_op jit(solution)/shard_map/all_to_all | solution.py:32
  155.8 2.6 %reduce_sum.18 = f32[49152]{0:T(1024)S(1)} reduce(f32[8,1,49152]{2,1,0:T(1,128)} %all-to-all-done.2, f32[]{:T(128)} %constant.110.clone.1), dimensions={0,1}, to_apply=%region_2.3 | reduce | flops 344064 | bytes 1769476 | tf_op jit(solution)/shard_map/reduce_sum | solution.py:33
  158.4 0.9 reshape.104
  159.2 3.5 %all-to-all-start.3 = ((f32[12,1,4096]{2,1,0:T(1,128)}), f32[12,1,4096]{2,1,0:T(1,128)S(1)}, u32[]{:S(2)}, u32[]{:S(2)}) async-start(f32[12,1,4096]{2,1,0:T(1,128)} %reshape.104), calls=%async_computation.3 | async-start | bytes 393216 | tf_op jit(solution)/shard_map/all_to_all | solution.py:32
  162.8 0.9 copy.41
  163.6 12.3 %all-to-all-done.3 = f32[12,1,4096]{2,1,0:T(1,128)S(1)} async-done(((f32[12,1,4096]{2,1,0:T(1,128)}), f32[12,1,4096]{2,1,0:T(1,128)S(1)}, u32[]{:S(2)}, u32[]{:S(2)}) %all-to-all-start.3) | async-done | bytes 196640 | tf_op jit(solution)/shard_map/all_to_all | solution.py:32
  175.9 0.7 reduce_sum.19
  (14 shorter events, 0.1 us)
Async XLA Ops:
  0.6 38.1 %copy-start.4 = (bf16[128,4096]{1,0:T(8,128)(2,1)S(1)}, bf16[128,4096]{1,0:T(8,128)(2,1)}, u32[]{:S(2)}) copy-start(bf16[128,4096]{1,0:T(8,128)(2,1)} %param.5) | copy-start | bytes 3145732
  30.6 8.9 %copy-start.5 = (s32[56,3]{0,1:T(4,128)S(1)}, s32[56,3]{0,1:T(4,128)}, u32[]{:S(2)}) copy-start(s32[56,3]{0,1:T(4,128)} %param.8) | copy-start | bytes 2020
  31.7 33.7 %all-to-all-start.1 = ((bf16[8,12,4096]{2,1,0:T(8,128)(2,1)}), bf16[8,12,4096]{2,1,0:T(8,128)(2,1)S(1)}, u32[]{:S(2)}, u32[]{:S(2)}) async-start(bf16[8,12,4096]{2,1,0:T(8,128)(2,1)} %broadcast_in_dim.41), calls=%async_computation.1 | async-start | bytes 2097152 | tf_op jit(solution)/shard_map/all_to_all | solution.py:26
  42.2 2.6 %copy-start.6 = (s32[56,3]{0,1:T(4,128)S(1)}, s32[56,3]{0,1:T(4,128)}, u32[]{:S(2)}) copy-start(s32[56,3]{0,1:T(4,128)} %param.9) | copy-start | bytes 2020
  65.5 8.1 %collective-permute-start = (bf16[96,4096]{1,0:T(8,128)(2,1)S(1)}, bf16[96,4096]{1,0:T(8,128)(2,1)S(1)}, u32[]{:S(2)}, u32[]{:S(2)}) collective-permute-start(bf16[96,4096]{1,0:T(8,128)(2,1)S(1)} %reshape.99), channel_id=1, source_target_pairs={{0,4},{4,0},{1,5},{5,1},{2,6},{6,2},{3,7},{7,3},{8,12},{12,8},{9,1... | collective-permute-start | bytes 2359304 | tf_op jit(solution)/shard_map/ppermute | solution.py:62
  76.1 5.2 %copy-start = (bf16[168,128,64]{1,2,0:T(8,128)(2,1)S(1)}, bf16[168,128,64]{1,2,0:T(8,128)(2,1)}, u32[]{:S(2)}) copy-start(bf16[168,128,64]{1,2,0:T(8,128)(2,1)} %gather_fusion) | copy-start | bytes 8257540
  86.1 0.9 copy-start.2
  94.5 5.7 %copy-start.3 = (f32[168,4096]{1,0:T(8,128)}, f32[168,4096]{1,0:T(8,128)S(1)}, u32[]{:S(2)}) copy-start(f32[168,4096]{1,0:T(8,128)S(1)} %reshape.144) | copy-start | bytes 8257540
  97.8 6.4 %collective-permute-start.1 = (f32[96,4096]{1,0:T(8,128)}, f32[96,4096]{1,0:T(8,128)}, u32[]{:S(2)}, u32[]{:S(2)}) collective-permute-start(f32[96,4096]{1,0:T(8,128)} %scatter_custom_fusion.1), channel_id=1, source_target_pairs={{0,4},{4,0},{1,5},{5,1},{2,6},{6,2},{3,7},{7,3},{8,12},{12,8},{9,1... | collective-permute-start | bytes 4718600 | tf_op jit(solution)/shard_map/ppermute | solution.py:95
  107.0 8.4 %copy-start.1 = (bf16[56,3,64,64]{3,2,1,0:T(8,128)(2,1)S(1)}, bf16[56,3,64,64]{3,2,1,0:T(8,128)(2,1)}, u32[]{:S(2)}) copy-start(bf16[56,3,64,64]{3,2,1,0:T(8,128)(2,1)} %gather.15) | copy-start | bytes 4128772
  111.1 44.7 %all-to-all-start.2 = ((f32[8,1,49152]{2,1,0:T(1,128)}), f32[8,1,49152]{2,1,0:T(1,128)}, u32[]{:S(2)}, u32[]{:S(2)}) async-start(f32[8,1,49152]{2,1,0:T(1,128)} %reshape_reshape.3), calls=%async_computation.2 | async-start | bytes 3145728 | tf_op jit(solution)/shard_map/all_to_all | solution.py:32
  124.8 16.9 %collective-permute-start.4 = (bf16[128,1024]{0,1:T(8,128)(2,1)S(1)}, bf16[128,1024]{0,1:T(8,128)(2,1)S(1)}, u32[]{:S(2)}, u32[]{:S(2)}) collective-permute-start(bf16[128,1024]{0,1:T(8,128)(2,1)S(1)} %get-tuple-element.21), channel_id=1, source_target_pairs={{0,3},{1,0},{2,1},{3,2},{4,7},{5,4},{6,5},{7,6},{8,11},{9,8},{10,9... | collective-permute-start | bytes 786440 | tf_op jit(solution)/shard_map/ppermute | solution.py:85
  127.5 14.2 %collective-permute-start.3 = (bf16[128,1024]{0,1:T(8,128)(2,1)S(1)}, bf16[128,1024]{0,1:T(8,128)(2,1)S(1)}, u32[]{:S(2)}, u32[]{:S(2)}) collective-permute-start(bf16[128,1024]{0,1:T(8,128)(2,1)S(1)} %get-tuple-element.22), channel_id=1, source_target_pairs={{0,2},{1,3},{2,0},{3,1},{4,6},{5,7},{6,4},{7,5},{8,10},{9,11},{10,... | collective-permute-start | bytes 786440 | tf_op jit(solution)/shard_map/ppermute | solution.py:85
  130.6 13.7 %collective-permute-start.2 = (bf16[128,1024]{0,1:T(8,128)(2,1)S(1)}, bf16[128,1024]{0,1:T(8,128)(2,1)S(1)}, u32[]{:S(2)}, u32[]{:S(2)}) collective-permute-start(bf16[128,1024]{0,1:T(8,128)(2,1)S(1)} %get-tuple-element.20), channel_id=1, source_target_pairs={{0,1},{1,2},{2,3},{3,0},{4,5},{5,6},{6,7},{7,4},{8,9},{9,10},{10,1... | collective-permute-start | bytes 786440 | tf_op jit(solution)/shard_map/ppermute | solution.py:85
  159.2 16.7 %all-to-all-start.3 = ((f32[12,1,4096]{2,1,0:T(1,128)}), f32[12,1,4096]{2,1,0:T(1,128)S(1)}, u32[]{:S(2)}, u32[]{:S(2)}) async-start(f32[12,1,4096]{2,1,0:T(1,128)} %reshape.104), calls=%async_computation.3 | async-start | bytes 393216 | tf_op jit(solution)/shard_map/all_to_all | solution.py:32
